TPU v7x, 128 devices: a whole 4x4x4 slice. The times are simulated.
128 devices in a mesh: gx: 4 (over z_lo, core), gy: 4 (over x), gz: 8 (over z_hi, y).
Axes of the slice: x: 4, y: 4, z: 4 (z_hi: 2, z_lo: 2; z = z_hi * 2 + z_lo), core: 2. Of those that a mesh axis runs over, the one named last changes fastest.
Arguments:
- coefficients: bfloat16 [8, 16, 16, 512, 128], P('gx', 'gy', 'gz'), may hold values from -6 to 6
- level_weights: bfloat16 [4, 2, 2, 512, 512], replicated, may hold values from -0.125 to 0.125
- coupling: bfloat16 [6, 512, 512], replicated, may hold values from -0.109375 to 0.109375
- positions: float32 [3, 1048576], P(None, ('gx', 'gy', 'gz')), may hold values from -1 to 1
- block_leaf: int32 [8192], P(('gx', 'gy', 'gz')), may hold values from 0 to 15
- block_count: int32 [8192], P(('gx', 'gy', 'gz')), may hold values from 1 to 128
Outputs:
- samples: bfloat16 [1048576, 128], P(('gx', 'gy', 'gz'))
Inputs may be any that keep to these rules, and one draw needn't show every extreme that they name: `block_leaf`: each block names one of the 16 leaves of the device that holds the block.
All inputs are finite; a program needn't handle non-finite values.
Results may differ from a plain program's by a relative error of at most 0.015.
Values may be sent and summed in bfloat16 or wider, within the bound.
No kernel may reach another device: no remote copies, remote signals or barrier semaphores. Data moves between devices by JAX's collectives and lax.ppermute only.
A program may use at most 128 MiB of HBM per device.

v0:
```python
import math

import numpy as np
import jax
import jax.numpy as jnp
from jax import lax
from jax.experimental import pallas as pl
from jax.experimental.pallas import tpu as pltpu
from jax.sharding import PartitionSpec as P

PTS = 8
ROWS = 128
BLOCKS_PER_STEP = 8

NODES = [
    float(v)
    for v in np.cos(
        np.float32(math.pi) * (np.float32(2.0) * np.arange(PTS, dtype=np.float32) + np.float32(1.0)) / np.float32(2.0 * PTS)
    ).astype(np.float32)
]


def from_partner(shard, axis, apart):
    return lax.ppermute(shard, axis, [(i, i ^ 1 << apart) for i in range(lax.axis_size(axis))])


def extended(cells, sides, width):
    for axis, dim in sides:
        count = lax.axis_size(axis)
        ends = count - 1
        head = lax.slice_in_dim(cells, 0, width, axis=dim)
        tail = lax.slice_in_dim(cells, cells.shape[dim] - width, cells.shape[dim], axis=dim)
        cells = jnp.concatenate(
            [
                lax.ppermute(tail, axis, [(i, (i + 1) % count) for i in range(ends)]),
                cells,
                lax.ppermute(head, axis, [((i + 1) % count, i) for i in range(ends)]),
            ],
            axis=dim,
        )
    return cells


def swapped(block):
    half = block.shape[-1] // 2
    return jnp.concatenate([-block[..., half:], block[..., :half]], axis=-1)


def apply_map(weights, block):
    return jnp.einsum("jk,...kc->...jc", weights, block, preferred_element_type=jnp.float32)


def mix(block, other, weights):
    total = apply_map(weights[0, 0], block) + apply_map(weights[0, 1], swapped(block))
    total = total + apply_map(weights[1, 0], other) + apply_map(weights[1, 1], swapped(other))
    return total.astype(jnp.bfloat16)


def basis(u, row):
    ub = jnp.broadcast_to(u, (PTS, ROWS))
    tcol = jnp.zeros((PTS, ROWS), jnp.float32)
    for j in range(PTS):
        tcol = jnp.where(row == j, NODES[j], tcol)
    term = jnp.ones((PTS, ROWS), jnp.float32)
    for m in range(PTS):
        own = row == m
        num = jnp.where(own, 1.0, ub - NODES[m])
        den = jnp.where(own, 1.0, tcol - NODES[m])
        term = term * num / den
    return term


def sample_kernel(leaf_ref, count_ref, pos_ref, grid_ref, out_ref):
    step = pl.program_id(0)
    row = lax.broadcasted_iota(jnp.int32, (PTS, ROWS), 0)
    live_row = lax.broadcasted_iota(jnp.int32, (ROWS, out_ref.shape[1]), 0)
    for i in range(BLOCKS_PER_STEP):
        b = step * BLOCKS_PER_STEP + i
        u = pos_ref[:, i * ROWS:(i + 1) * ROWS]
        lx = basis(u[0:1, :], row)
        ly = basis(u[1:2, :], row)
        lz = basis(u[2:3, :], row)
        pieces = []
        for jx in range(PTS):
            bx = jnp.broadcast_to(lx[jx:jx + 1, :], (PTS, ROWS))
            for jy in range(PTS):
                by = jnp.broadcast_to(ly[jy:jy + 1, :], (PTS, ROWS))
                pieces.append((bx * by) * lz)
        weights_t = jnp.concatenate(pieces, axis=0).astype(jnp.bfloat16)
        leaf = grid_ref[leaf_ref[b]]
        values = lax.dot_general(
            weights_t, leaf, (((0,), (0,)), ((), ())), preferred_element_type=jnp.float32
        )
        values = jnp.where(live_row < count_ref[b], values, 0.0)
        out_ref[i * ROWS:(i + 1) * ROWS, :] = values.astype(out_ref.dtype)


def sample(leaf_grid, positions, block_leaf, block_count):
    leaves, cheb, cols = leaf_grid.shape
    blocks = block_leaf.shape[0]
    width = BLOCKS_PER_STEP * ROWS
    spec = pltpu.PrefetchScalarGridSpec(
        num_scalar_prefetch=2,
        grid=(blocks // BLOCKS_PER_STEP,),
        in_specs=[
            pl.BlockSpec((3, width), lambda s, lf, ct: (0, s)),
            pl.BlockSpec((leaves, cheb, cols), lambda s, lf, ct: (0, 0, 0)),
        ],
        out_specs=pl.BlockSpec((width, cols), lambda s, lf, ct: (s, 0)),
    )
    return pl.pallas_call(
        sample_kernel,
        grid_spec=spec,
        out_shape=jax.ShapeDtypeStruct((blocks * ROWS, cols), jnp.bfloat16),
    )(block_leaf, block_count, positions, leaf_grid)


def butterfly(cells, level_weights):
    for level in range(2):
        cells = mix(cells, from_partner(cells, "gx", level), level_weights[level])
    cells = mix(cells, from_partner(cells, "gy", 0), level_weights[2])
    return mix(cells, from_partner(cells, "gz", 0), level_weights[3])


LEVEL_PLAN = (("gx", 0), ("gx", 1), ("gy", 0), ("gz", 0))


def pipelined(coefficients, level_weights, chunks):
    cells = [coefficients[:, k:k + 1] for k in range(chunks)]
    levels = len(LEVEL_PLAN)
    for tick in range(chunks + levels - 1):
        active = [k for k in range(chunks) if 0 <= tick - k < levels]
        ready = lax.optimization_barrier(tuple(cells[k] for k in active))
        for k, block in zip(active, ready):
            level = tick - k
            axis, bit = LEVEL_PLAN[level]
            cells[k] = mix(block, from_partner(block, axis, bit), level_weights[level])
    return cells


def from_below(slab, axis):
    count = lax.axis_size(axis)
    return lax.ppermute(slab, axis, [(i, i + 1) for i in range(count - 1)])


def from_above(slab, axis):
    count = lax.axis_size(axis)
    return lax.ppermute(slab, axis, [(i + 1, i) for i in range(count - 1)])


def faces(cells, axis, dim):
    size = cells.shape[dim]
    first = lax.slice_in_dim(cells, 0, 1, axis=dim)
    last = lax.slice_in_dim(cells, size - 1, size, axis=dim)
    below = jnp.concatenate([from_below(last, axis), lax.slice_in_dim(cells, 0, size - 1, axis=dim)], axis=dim)
    above = jnp.concatenate([lax.slice_in_dim(cells, 1, size, axis=dim), from_above(first, axis)], axis=dim)
    return below, above


def local(coefficients, level_weights, coupling, positions, block_leaf, block_count):
    chunks = coefficients.shape[1]
    cells = jnp.concatenate(pipelined(coefficients, level_weights, chunks), axis=1)
    minus_x, plus_x = faces(cells, "gx", 0)
    minus_y, plus_y = faces(cells, "gy", 1)
    minus_z, plus_z = faces(cells, "gz", 2)
    neighbours = (minus_x, plus_x, minus_y, plus_y, minus_z, plus_z)
    total = cells.astype(jnp.float32)
    for index in range(6):
        total = total + apply_map(coupling[index], neighbours[index])
    grid = total.astype(jnp.bfloat16)
    leaf_count = grid.shape[0] * grid.shape[1] * grid.shape[2]
    leaf_grid = grid.reshape(leaf_count, grid.shape[3], grid.shape[4])
    return sample(leaf_grid, positions, block_leaf, block_count)


def solution(mesh):
    placed = (
        P("gx", "gy", "gz", None, None),
        P(),
        P(),
        P(None, ("gx", "gy", "gz")),
        P(("gx", "gy", "gz")),
        P(("gx", "gy", "gz")),
    )
    return jax.shard_map(
        local, mesh=mesh, in_specs=placed, out_specs=P(("gx", "gy", "gz"), None), check_vma=False
    )
```

profile of v0, /device:TPU:34, one launch (start us, length us, event | category | flops | bytes accessed | tf_op | source)
XLA Modules:
  0.0 181.5 jit_solution(11415034190742003045)
XLA Ops:
  0.0 1.7 fusion.260
  1.7 1.0 copy.58
  3.2 1.0 copy.59
  4.2 3.9 %slice_bitcast_fusion = (bf16[2,2,512,512]{3,2,1,0:T(8,128)(2,1)S(1)}, bf16[2,2,512,512]{3,2,1,0:T(8,128)(2,1)S(1)}, bf16[2,2,512,512]{3,2,1,0:T(8,128)(2,1)S(1)}, bf16[2,2,512,512]{3,2,1,0:T(8,128)(2,1)S(1)}) fusion(bf16[4,2,2,512,512]{4,3,2,1,0:T(8,128)(2,1)} %param.7), kind=kLoop, calls=%fused_computation.39 | loop fusion | bytes 16777216 | tf_op jit(solution)/shard_map/squeeze | solution.py:137
  8.1 1.5 fusion.212
  9.6 1.1 slice_negate_fusion.17
  11.2 1.1 slice_negate_fusion.16
  12.7 1.6 fusion.79
  14.5 0.5 collective-permute-start.2
  17.0 11.8 %collective-permute-done.1 = bf16[2,1,2,512,128]{3,4,2,0,1:T(8,128)(2,1)S(1)} collective-permute-done((bf16[2,1,2,512,128]{3,4,2,0,1:T(8,128)(2,1)S(1)}, bf16[2,1,2,512,128]{3,4,2,0,1:T(8,128)(2,1)S(1)}, u32[]{:S(2)}, u32[]{:S(2)}) %collective-permute-start.1) | collective-permute-done | bytes 524320 | tf_op jit(solution)/shard_map/ppermute | solution.py:24
  30.8 0.6 collective-permute-start.3
  33.8 0.5 convolution_add_fusion.23
  34.8 9.6 %collective-permute-done.3 = bf16[2,1,2,512,128]{3,4,2,0,1:T(8,128)(2,1)S(1)} collective-permute-done((bf16[2,1,2,512,128]{3,4,2,0,1:T(8,128)(2,1)S(1)}, bf16[2,1,2,512,128]{3,4,2,0,1:T(8,128)(2,1)S(1)}, u32[]{:S(2)}, u32[]{:S(2)}) %collective-permute-start.3) | collective-permute-done | bytes 524320 | tf_op jit(solution)/shard_map/ppermute | solution.py:24
  46.7 0.5 fusion.75
  47.7 1.6 collective-permute-start.6
  49.4 1.6 collective-permute-start.7
  51.0 0.7 collective-permute-start.8
  55.6 5.9 %collective-permute-done.7 = bf16[2,1,2,512,128]{3,4,2,0,1:T(8,128)(2,1)S(1)} collective-permute-done((bf16[2,1,2,512,128]{3,4,2,0,1:T(8,128)(2,1)S(1)}, bf16[2,1,2,512,128]{3,4,2,0,1:T(8,128)(2,1)S(1)}, u32[]{:S(2)}, u32[]{:S(2)}) %collective-permute-start.7) | collective-permute-done | bytes 524320 | tf_op jit(solution)/shard_map/ppermute | solution.py:24
  61.6 1.5 collective-permute-done.8
  65.5 0.5 fusion.70
  66.0 0.5 collective-permute-start.10
  67.0 0.6 collective-permute-start.11
  68.1 0.9 collective-permute-start.12
  70.1 0.5 fusion.73
  70.5 3.2 %collective-permute-start.19 = (bf16[2,1,2,512,128]{3,4,2,0,1:T(8,128)(2,1)S(1)}, bf16[2,1,2,512,128]{3,4,2,0,1:T(8,128)(2,1)S(1)}, u32[]{:S(2)}, u32[]{:S(2)}) collective-permute-start(bf16[2,1,2,512,128]{3,4,2,0,1:T(8,128)(2,1)S(1)} %fusion.73), channel_id=1, source_target_pairs={{8,0},{16,8},{24,16},{9,1},{17,9},{25,17},{10,2},{18,10},{26,18},{... | collective-permute-start | bytes 1572872 | tf_op jit(solution)/shard_map/ppermute | solution.py:148
  74.7 0.5 convolution_add_fusion.7
  75.2 4.8 %collective-permute-done.11 = bf16[2,1,2,512,128]{3,4,2,0,1:T(8,128)(2,1)S(1)} collective-permute-done((bf16[2,1,2,512,128]{3,4,2,0,1:T(8,128)(2,1)S(1)}, bf16[2,1,2,512,128]{3,4,2,0,1:T(8,128)(2,1)S(1)}, u32[]{:S(2)}, u32[]{:S(2)}) %collective-permute-start.11) | collective-permute-done | bytes 524320 | tf_op jit(solution)/shard_map/ppermute | solution.py:24
  81.5 0.5 fusion.67
  82.0 1.6 collective-permute-start.13
  84.1 2.8 %collective-permute-start.14 = (bf16[2,1,2,512,128]{3,4,2,0,1:T(8,128)(2,1)S(1)}, bf16[2,1,2,512,128]{3,4,2,0,1:T(8,128)(2,1)S(1)}, u32[]{:S(2)}, u32[]{:S(2)}) collective-permute-start(bf16[2,1,2,512,128]{3,4,2,0,1:T(8,128)(2,1)S(1)} %fusion.67), channel_id=1, source_target_pairs={{0,8},{8,0},{16,24},{24,16},{1,9},{9,1},{17,25},{25,17},{2,10},{10... | collective-permute-start | bytes 1572872 | tf_op jit(solution)/shard_map/ppermute | solution.py:24
  89.4 8.9 %collective-permute-done.14 = bf16[2,1,2,512,128]{3,4,2,0,1:T(8,128)(2,1)S(1)} collective-permute-done((bf16[2,1,2,512,128]{3,4,2,0,1:T(8,128)(2,1)S(1)}, bf16[2,1,2,512,128]{3,4,2,0,1:T(8,128)(2,1)S(1)}, u32[]{:S(2)}, u32[]{:S(2)}) %collective-permute-start.14) | collective-permute-done | bytes 524320 | tf_op jit(solution)/shard_map/ppermute | solution.py:24
  99.3 1.6 collective-permute-start.15
  102.9 6.3 %collective-permute-done.15 = bf16[2,1,2,512,128]{3,4,2,0,1:T(8,128)(2,1)S(1)} collective-permute-done((bf16[2,1,2,512,128]{3,4,2,0,1:T(8,128)(2,1)S(1)}, bf16[2,1,2,512,128]{3,4,2,0,1:T(8,128)(2,1)S(1)}, u32[]{:S(2)}, u32[]{:S(2)}) %collective-permute-start.15) | collective-permute-done | bytes 524320 | tf_op jit(solution)/shard_map/ppermute | solution.py:24
  110.1 5.3 %collective-permute-start.18 = (bf16[2,1,2,512,128]{3,4,2,0,1:T(8,128)(2,1)S(1)}, bf16[2,1,2,512,128]{3,4,2,0,1:T(8,128)(2,1)S(1)}, u32[]{:S(2)}, u32[]{:S(2)}) collective-permute-start(bf16[2,1,2,512,128]{3,4,2,0,1:T(8,128)(2,1)S(1)} %fusion.64), channel_id=1, source_target_pairs={{0,8},{8,16},{16,24},{1,9},{9,17},{17,25},{2,10},{10,18},{18,26},{... | collective-permute-start | bytes 1572872 | tf_op jit(solution)/shard_map/ppermute | solution.py:143
  115.9 2.2 %collective-permute-start.17 = (bf16[1,4,2,512,128]{3,4,2,0,1:T(8,128)(2,1)S(1)}, bf16[1,4,2,512,128]{3,4,2,0,1:T(8,128)(2,1)S(1)}, u32[]{:S(2)}, u32[]{:S(2)}) collective-permute-start(bf16[1,4,2,512,128]{3,4,2,0,1:T(8,128)(2,1)S(1)} %get-tuple-element.38), channel_id=1, source_target_pairs={{32,0},{64,32},{96,64},{33,1},{65,33},{97,65},{34,2},{66,34},{98,6... | collective-permute-start | bytes 3145736 | tf_op jit(solution)/shard_map/ppermute | solution.py:148
  118.3 3.6 %collective-permute-start.20 = (bf16[2,4,1,512,128]{3,4,2,0,1:T(8,128)(2,1)S(1)}, bf16[2,4,1,512,128]{3,4,2,0,1:T(8,128)(2,1)S(1)}, u32[]{:S(2)}, u32[]{:S(2)}) collective-permute-start(bf16[2,4,1,512,128]{3,4,2,0,1:T(8,128)(2,1)S(1)} %get-tuple-element.39), channel_id=1, source_target_pairs={{0,1},{1,2},{2,3},{3,4},{4,5},{5,6},{6,7},{8,9},{9,10},{10,11},{11... | collective-permute-start | bytes 3145736 | tf_op jit(solution)/shard_map/ppermute | solution.py:143
  121.9 1.3 collective-permute-start.21
  123.2 2.4 %collective-permute-start.16 = (bf16[1,4,2,512,128]{3,4,2,0,1:T(8,128)(2,1)S(1)}, bf16[1,4,2,512,128]{3,4,2,0,1:T(8,128)(2,1)S(1)}, u32[]{:S(2)}, u32[]{:S(2)}) collective-permute-start(bf16[1,4,2,512,128]{3,4,2,0,1:T(8,128)(2,1)S(1)} %get-tuple-element.37), channel_id=1, source_target_pairs={{0,32},{32,64},{64,96},{1,33},{33,65},{65,97},{2,34},{34,66},{66,9... | collective-permute-start | bytes 3145736 | tf_op jit(solution)/shard_map/ppermute | solution.py:143
  125.7 1.3 fusion.17
  127.0 1.3 fusion.9
  128.3 24.6 %collective-permute-done.17 = bf16[1,4,2,512,128]{3,4,2,0,1:T(8,128)(2,1)S(1)} collective-permute-done((bf16[1,4,2,512,128]{3,4,2,0,1:T(8,128)(2,1)S(1)}, bf16[1,4,2,512,128]{3,4,2,0,1:T(8,128)(2,1)S(1)}, u32[]{:S(2)}, u32[]{:S(2)}) %collective-permute-start.17) | collective-permute-done | bytes 1048608 | tf_op jit(solution)/shard_map/ppermute | solution.py:148
  152.9 1.3 fusion.5
  154.2 6.8 %collective-permute-done.16 = bf16[1,4,2,512,128]{3,4,2,0,1:T(8,128)(2,1)S(1)} collective-permute-done((bf16[1,4,2,512,128]{3,4,2,0,1:T(8,128)(2,1)S(1)}, bf16[1,4,2,512,128]{3,4,2,0,1:T(8,128)(2,1)S(1)}, u32[]{:S(2)}, u32[]{:S(2)}) %collective-permute-start.16) | collective-permute-done | bytes 1048608 | tf_op jit(solution)/shard_map/ppermute | solution.py:143
  161.0 1.3 fusion.1
  162.3 3.3 %fusion.25 = f32[2,4,2,128,512]{4,3,2,0,1:T(8,128)} fusion(bf16[2,4,1,512,128]{3,4,2,0,1:T(8,128)(2,1)S(1)} %get-tuple-element.40, bf16[2,4,1,512,128]{3,4,2,0,1:T(8,128)(2,1)S(1)} %collective-permute-done.20, bf16[6,512,512]{2,1,0:T(8,128)(2,1)S(1)} %copy-done.2), kind=kOutput, calls=%fused_computation.32 | convolution fusion | flops 1074790400 | bytes 6815744 | tf_op jit(solution)/shard_map/jk,...kc->...jc/dot_general | solution.py:50
  165.6 5.4 %fusion = bf16[2,4,2,512,128]{3,4,2,0,1:T(8,128)(2,1)S(1)} fusion(f32[2,4,2,128,512]{4,3,2,0,1:T(8,128)} %fusion.25, f32[2,4,2,128,512]{4,3,2,0,1:T(8,128)S(1)} %fusion.17, f32[2,4,2,128,512]{4,3,2,0,1:T(8,128)S(1)} %fusion.9, f32[2,4,2,128,512]{4,3,2,0,1:T(8,128)S(1)} %fusion.5, f32[2,4,2,128,512]{4,3,2,0,1:T(8,128)S(1)} %fusion.1, ...), kind=kOutput, calls=%fused_computation.1 | convolution fusion | flops 1086324736 | bytes 27787264 | tf_op jit(solution)/shard_map/jk,...kc->...jc/dot_general | solution.py:50
  170.9 2.4 %copy.23 = bf16[2,4,2,512,128]{4,3,2,1,0:T(8,128)(2,1)} copy(bf16[2,4,2,512,128]{3,4,2,0,1:T(8,128)(2,1)S(1)} %fusion) | data formatting | bytes 4194304 | tf_op jit(solution)/shard_map/convert_element_type | solution.py:170
  173.3 8.2 %shard_map.64 = bf16[8192,128]{1,0:T(8,128)(2,1)} custom-call(s32[64]{0:T(128)} %leaf_ref.1, s32[64]{0:T(128)} %count_ref.1, f32[3,8192]{1,0:T(4,128)} %pos_ref.1, bf16[16,512,128]{2,1,0:T(8,128)(2,1)} %bitcast.491), custom_call_target="tpu_custom_call" | custom-call | tf_op jit(solution)/shard_map/pallas_call | solution.py:111
  (114 shorter events, 29.5 us)
Async XLA Ops:
  2.7 8.4 %collective-permute-start = (bf16[2,1,2,512,128]{3,4,2,0,1:T(8,128)(2,1)}, bf16[2,1,2,512,128]{3,4,2,0,1:T(8,128)(2,1)}, u32[]{:S(2)}, u32[]{:S(2)}) collective-permute-start(bf16[2,1,2,512,128]{3,4,2,0,1:T(8,128)(2,1)} %copy.58), channel_id=1, source_target_pairs={{0,32},{32,0},{64,96},{96,64},{1,33},{33,1},{65,97},{97,65},{2,34}... | collective-permute-start | bytes 1572872 | tf_op jit(solution)/shard_map/ppermute | solution.py:24
  12.7 1.8 copy-start
  14.3 14.4 %collective-permute-start.1 = (bf16[2,1,2,512,128]{3,4,2,0,1:T(8,128)(2,1)S(1)}, bf16[2,1,2,512,128]{3,4,2,0,1:T(8,128)(2,1)S(1)}, u32[]{:S(2)}, u32[]{:S(2)}) collective-permute-start(bf16[2,1,2,512,128]{3,4,2,0,1:T(8,128)(2,1)S(1)} %fusion.79), channel_id=1, source_target_pairs={{0,64},{32,96},{64,0},{96,32},{1,65},{33,97},{65,1},{97,33},{2,66}... | collective-permute-start | bytes 1572872 | tf_op jit(solution)/shard_map/ppermute | solution.py:24
  14.5 14.7 %collective-permute-start.2 = (bf16[2,1,2,512,128]{3,4,2,0,1:T(8,128)(2,1)S(1)}, bf16[2,1,2,512,128]{3,4,2,0,1:T(8,128)(2,1)S(1)}, u32[]{:S(2)}, u32[]{:S(2)}) collective-permute-start(bf16[2,1,2,512,128]{3,4,2,0,1:T(8,128)(2,1)S(1)} %copy-done), channel_id=1, source_target_pairs={{0,32},{32,0},{64,96},{96,64},{1,33},{33,1},{65,97},{97,65},{2,34}... | collective-permute-start | bytes 1572872 | tf_op jit(solution)/shard_map/ppermute | solution.py:24
  30.8 13.6 %collective-permute-start.3 = (bf16[2,1,2,512,128]{3,4,2,0,1:T(8,128)(2,1)S(1)}, bf16[2,1,2,512,128]{3,4,2,0,1:T(8,128)(2,1)S(1)}, u32[]{:S(2)}, u32[]{:S(2)}) collective-permute-start(bf16[2,1,2,512,128]{3,4,2,0,1:T(8,128)(2,1)S(1)} %fusion.78), channel_id=1, source_target_pairs={{0,8},{8,0},{16,24},{24,16},{1,9},{9,1},{17,25},{25,17},{2,10},{10... | collective-permute-start | bytes 1572872 | tf_op jit(solution)/shard_map/ppermute | solution.py:24
  31.4 13.3 %collective-permute-start.4 = (bf16[2,1,2,512,128]{3,4,2,0,1:T(8,128)(2,1)S(1)}, bf16[2,1,2,512,128]{3,4,2,0,1:T(8,128)(2,1)S(1)}, u32[]{:S(2)}, u32[]{:S(2)}) collective-permute-start(bf16[2,1,2,512,128]{3,4,2,0,1:T(8,128)(2,1)S(1)} %fusion.77), channel_id=1, source_target_pairs={{0,64},{32,96},{64,0},{96,32},{1,65},{33,97},{65,1},{97,33},{2,66}... | collective-permute-start | bytes 1572872 | tf_op jit(solution)/shard_map/ppermute | solution.py:24
  32.2 13.4 %collective-permute-start.5 = (bf16[2,1,2,512,128]{3,4,2,0,1:T(8,128)(2,1)S(1)}, bf16[2,1,2,512,128]{3,4,2,0,1:T(8,128)(2,1)S(1)}, u32[]{:S(2)}, u32[]{:S(2)}) collective-permute-start(bf16[2,1,2,512,128]{3,4,2,0,1:T(8,128)(2,1)S(1)} %copy.60), channel_id=1, source_target_pairs={{0,32},{32,0},{64,96},{96,64},{1,33},{33,1},{65,97},{97,65},{2,34}... | collective-permute-start | bytes 1572872 | tf_op jit(solution)/shard_map/ppermute | solution.py:24
  47.7 21.8 %collective-permute-start.6 = (bf16[2,1,2,512,128]{3,4,2,0,1:T(8,128)(2,1)S(1)}, bf16[2,1,2,512,128]{3,4,2,0,1:T(8,128)(2,1)S(1)}, u32[]{:S(2)}, u32[]{:S(2)}) collective-permute-start(bf16[2,1,2,512,128]{3,4,2,0,1:T(8,128)(2,1)S(1)} %fusion.76), channel_id=1, source_target_pairs={{0,1},{1,0},{2,3},{3,2},{4,5},{5,4},{6,7},{7,6},{8,9},{9,8},{10,11... | collective-permute-start | bytes 1572872 | tf_op jit(solution)/shard_map/ppermute | solution.py:24
  49.4 12.1 %collective-permute-start.7 = (bf16[2,1,2,512,128]{3,4,2,0,1:T(8,128)(2,1)S(1)}, bf16[2,1,2,512,128]{3,4,2,0,1:T(8,128)(2,1)S(1)}, u32[]{:S(2)}, u32[]{:S(2)}) collective-permute-start(bf16[2,1,2,512,128]{3,4,2,0,1:T(8,128)(2,1)S(1)} %fusion.75), channel_id=1, source_target_pairs={{0,8},{8,0},{16,24},{24,16},{1,9},{9,1},{17,25},{25,17},{2,10},{10... | collective-permute-start | bytes 1572872 | tf_op jit(solution)/shard_map/ppermute | solution.py:24
  51.0 12.1 %collective-permute-start.8 = (bf16[2,1,2,512,128]{3,4,2,0,1:T(8,128)(2,1)S(1)}, bf16[2,1,2,512,128]{3,4,2,0,1:T(8,128)(2,1)S(1)}, u32[]{:S(2)}, u32[]{:S(2)}) collective-permute-start(bf16[2,1,2,512,128]{3,4,2,0,1:T(8,128)(2,1)S(1)} %fusion.74), channel_id=1, source_target_pairs={{0,64},{32,96},{64,0},{96,32},{1,65},{33,97},{65,1},{97,33},{2,66}... | collective-permute-start | bytes 1572872 | tf_op jit(solution)/shard_map/ppermute | solution.py:24
  52.6 11.4 %collective-permute-start.9 = (bf16[2,1,2,512,128]{3,4,2,0,1:T(8,128)(2,1)S(1)}, bf16[2,1,2,512,128]{3,4,2,0,1:T(8,128)(2,1)S(1)}, u32[]{:S(2)}, u32[]{:S(2)}) collective-permute-start(bf16[2,1,2,512,128]{3,4,2,0,1:T(8,128)(2,1)S(1)} %copy.61), channel_id=1, source_target_pairs={{0,32},{32,0},{64,96},{96,64},{1,33},{33,1},{65,97},{97,65},{2,34}... | collective-permute-start | bytes 1572872 | tf_op jit(solution)/shard_map/ppermute | solution.py:24
  66.0 21.3 %collective-permute-start.10 = (bf16[2,1,2,512,128]{3,4,2,0,1:T(8,128)(2,1)S(1)}, bf16[2,1,2,512,128]{3,4,2,0,1:T(8,128)(2,1)S(1)}, u32[]{:S(2)}, u32[]{:S(2)}) collective-permute-start(bf16[2,1,2,512,128]{3,4,2,0,1:T(8,128)(2,1)S(1)} %fusion.72), channel_id=1, source_target_pairs={{0,1},{1,0},{2,3},{3,2},{4,5},{5,4},{6,7},{7,6},{8,9},{9,8},{10,11... | collective-permute-start | bytes 1572872 | tf_op jit(solution)/shard_map/ppermute | solution.py:24
  67.0 12.9 %collective-permute-start.11 = (bf16[2,1,2,512,128]{3,4,2,0,1:T(8,128)(2,1)S(1)}, bf16[2,1,2,512,128]{3,4,2,0,1:T(8,128)(2,1)S(1)}, u32[]{:S(2)}, u32[]{:S(2)}) collective-permute-start(bf16[2,1,2,512,128]{3,4,2,0,1:T(8,128)(2,1)S(1)} %fusion.71), channel_id=1, source_target_pairs={{0,8},{8,0},{16,24},{24,16},{1,9},{9,1},{17,25},{25,17},{2,10},{10... | collective-permute-start | bytes 1572872 | tf_op jit(solution)/shard_map/ppermute | solution.py:24
  68.1 12.4 %collective-permute-start.12 = (bf16[2,1,2,512,128]{3,4,2,0,1:T(8,128)(2,1)S(1)}, bf16[2,1,2,512,128]{3,4,2,0,1:T(8,128)(2,1)S(1)}, u32[]{:S(2)}, u32[]{:S(2)}) collective-permute-start(bf16[2,1,2,512,128]{3,4,2,0,1:T(8,128)(2,1)S(1)} %fusion.70), channel_id=1, source_target_pairs={{0,64},{32,96},{64,0},{96,32},{1,65},{33,97},{65,1},{97,33},{2,66}... | collective-permute-start | bytes 1572872 | tf_op jit(solution)/shard_map/ppermute | solution.py:24
  70.5 52.7 %collective-permute-start.19 = (bf16[2,1,2,512,128]{3,4,2,0,1:T(8,128)(2,1)S(1)}, bf16[2,1,2,512,128]{3,4,2,0,1:T(8,128)(2,1)S(1)}, u32[]{:S(2)}, u32[]{:S(2)}) collective-permute-start(bf16[2,1,2,512,128]{3,4,2,0,1:T(8,128)(2,1)S(1)} %fusion.73), channel_id=1, source_target_pairs={{8,0},{16,8},{24,16},{9,1},{17,9},{25,17},{10,2},{18,10},{26,18},{... | collective-permute-start | bytes 1572872 | tf_op jit(solution)/shard_map/ppermute | solution.py:148
  82.0 19.4 %collective-permute-start.13 = (bf16[2,1,2,512,128]{3,4,2,0,1:T(8,128)(2,1)S(1)}, bf16[2,1,2,512,128]{3,4,2,0,1:T(8,128)(2,1)S(1)}, u32[]{:S(2)}, u32[]{:S(2)}) collective-permute-start(bf16[2,1,2,512,128]{3,4,2,0,1:T(8,128)(2,1)S(1)} %fusion.68), channel_id=1, source_target_pairs={{0,1},{1,0},{2,3},{3,2},{4,5},{5,4},{6,7},{7,6},{8,9},{9,8},{10,11... | collective-permute-start | bytes 1572872 | tf_op jit(solution)/shard_map/ppermute | solution.py:24
  84.1 14.2 %collective-permute-start.14 = (bf16[2,1,2,512,128]{3,4,2,0,1:T(8,128)(2,1)S(1)}, bf16[2,1,2,512,128]{3,4,2,0,1:T(8,128)(2,1)S(1)}, u32[]{:S(2)}, u32[]{:S(2)}) collective-permute-start(bf16[2,1,2,512,128]{3,4,2,0,1:T(8,128)(2,1)S(1)} %fusion.67), channel_id=1, source_target_pairs={{0,8},{8,0},{16,24},{24,16},{1,9},{9,1},{17,25},{25,17},{2,10},{10... | collective-permute-start | bytes 1572872 | tf_op jit(solution)/shard_map/ppermute | solution.py:24
  99.3 9.9 %collective-permute-start.15 = (bf16[2,1,2,512,128]{3,4,2,0,1:T(8,128)(2,1)S(1)}, bf16[2,1,2,512,128]{3,4,2,0,1:T(8,128)(2,1)S(1)}, u32[]{:S(2)}, u32[]{:S(2)}) collective-permute-start(bf16[2,1,2,512,128]{3,4,2,0,1:T(8,128)(2,1)S(1)} %fusion.65), channel_id=1, source_target_pairs={{0,1},{1,0},{2,3},{3,2},{4,5},{5,4},{6,7},{7,6},{8,9},{9,8},{10,11... | collective-permute-start | bytes 1572872 | tf_op jit(solution)/shard_map/ppermute | solution.py:24
  110.1 16.9 %collective-permute-start.18 = (bf16[2,1,2,512,128]{3,4,2,0,1:T(8,128)(2,1)S(1)}, bf16[2,1,2,512,128]{3,4,2,0,1:T(8,128)(2,1)S(1)}, u32[]{:S(2)}, u32[]{:S(2)}) collective-permute-start(bf16[2,1,2,512,128]{3,4,2,0,1:T(8,128)(2,1)S(1)} %fusion.64), channel_id=1, source_target_pairs={{0,8},{8,16},{16,24},{1,9},{9,17},{17,25},{2,10},{10,18},{18,26},{... | collective-permute-start | bytes 1572872 | tf_op jit(solution)/shard_map/ppermute | solution.py:143
  115.9 9.8 %copy-start.2 = (bf16[6,512,512]{2,1,0:T(8,128)(2,1)S(1)}, bf16[6,512,512]{2,1,0:T(8,128)(2,1)}, u32[]{:S(2)}) copy-start(bf16[6,512,512]{2,1,0:T(8,128)(2,1)} %param.8) | copy-start | bytes 9437188
  115.9 37.0 %collective-permute-start.17 = (bf16[1,4,2,512,128]{3,4,2,0,1:T(8,128)(2,1)S(1)}, bf16[1,4,2,512,128]{3,4,2,0,1:T(8,128)(2,1)S(1)}, u32[]{:S(2)}, u32[]{:S(2)}) collective-permute-start(bf16[1,4,2,512,128]{3,4,2,0,1:T(8,128)(2,1)S(1)} %get-tuple-element.38), channel_id=1, source_target_pairs={{32,0},{64,32},{96,64},{33,1},{65,33},{97,65},{34,2},{66,34},{98,6... | collective-permute-start | bytes 3145736 | tf_op jit(solution)/shard_map/ppermute | solution.py:148
  118.3 8.7 %copy-start.1 = (bf16[2,4,1,512,128]{3,4,2,0,1:T(8,128)(2,1)}, bf16[2,4,1,512,128]{3,4,2,0,1:T(8,128)(2,1)S(1)}, u32[]{:S(2)}) copy-start(bf16[2,4,1,512,128]{3,4,2,0,1:T(8,128)(2,1)S(1)} %get-tuple-element.39) | copy-start | bytes 3145732
  118.3 43.9 %collective-permute-start.20 = (bf16[2,4,1,512,128]{3,4,2,0,1:T(8,128)(2,1)S(1)}, bf16[2,4,1,512,128]{3,4,2,0,1:T(8,128)(2,1)S(1)}, u32[]{:S(2)}, u32[]{:S(2)}) collective-permute-start(bf16[2,4,1,512,128]{3,4,2,0,1:T(8,128)(2,1)S(1)} %get-tuple-element.39), channel_id=1, source_target_pairs={{0,1},{1,2},{2,3},{3,4},{4,5},{5,6},{6,7},{8,9},{9,10},{10,11},{11... | collective-permute-start | bytes 3145736 | tf_op jit(solution)/shard_map/ppermute | solution.py:143
  121.9 43.6 %collective-permute-start.21 = (bf16[2,4,1,512,128]{3,4,2,0,1:T(8,128)(2,1)S(1)}, bf16[2,4,1,512,128]{3,4,2,0,1:T(8,128)(2,1)}, u32[]{:S(2)}, u32[]{:S(2)}) collective-permute-start(bf16[2,4,1,512,128]{3,4,2,0,1:T(8,128)(2,1)S(1)} %get-tuple-element.40), channel_id=1, source_target_pairs={{1,0},{2,1},{3,2},{4,3},{5,4},{6,5},{7,6},{9,8},{10,9},{11,10},{12... | collective-permute-start | bytes 3145736 | tf_op jit(solution)/shard_map/ppermute | solution.py:148
  123.2 37.7 %collective-permute-start.16 = (bf16[1,4,2,512,128]{3,4,2,0,1:T(8,128)(2,1)S(1)}, bf16[1,4,2,512,128]{3,4,2,0,1:T(8,128)(2,1)S(1)}, u32[]{:S(2)}, u32[]{:S(2)}) collective-permute-start(bf16[1,4,2,512,128]{3,4,2,0,1:T(8,128)(2,1)S(1)} %get-tuple-element.37), channel_id=1, source_target_pairs={{0,32},{32,64},{64,96},{1,33},{33,65},{65,97},{2,34},{34,66},{66,9... | collective-permute-start | bytes 3145736 | tf_op jit(solution)/shard_map/ppermute | solution.py:143
where the time goes:
time: 184 us; the launch traced here: 181 us
  waiting for transfers between devices  80.4 us (44%)
  matrix products  45.9 us (25%)
  starting transfers between devices  31.8 us (17%)
  local copies, waits for them, and re-layouts  10.8 us (6%)
  Pallas kernels  8.15 us (4%)
  other arithmetic  3.49 us (2%)
    ppermute x16, waiting for transfers between devices, from_partner(): lax.ppermute(shard, axis, [(i, i ^ 1 << apart) for i in range(lax.axis_si...  49 us
    dot_general x70, matrix products, apply_map(): jnp.einsum('jk,...kc->...jc', weights, block, preferred_element_type=jnp....  45.9 us
    ppermute x3, waiting for transfers between devices, from_above(): return lax.ppermute(slab, axis, [(i + 1, i) for i in range(count - 1)])  24.6 us
    ppermute x16, starting transfers between devices, from_partner(): lax.ppermute(shard, axis, [(i, i ^ 1 << apart) for i in range(lax.axis_si...  13.9 us
    ppermute x3, starting transfers between devices, from_below(): return lax.ppermute(slab, axis, [(i, i + 1) for i in range(count - 1)])  11.3 us
    pallas_call x1, Pallas kernels, sample(): pl.pallas_call(sample_kernel, grid_spec=spec, out_shape=jax.ShapeDtypeStr...  8.15 us
    ppermute x3, waiting for transfers between devices, from_below(): return lax.ppermute(slab, axis, [(i, i + 1) for i in range(count - 1)])  6.8 us
    ppermute x3, starting transfers between devices, from_above(): return lax.ppermute(slab, axis, [(i + 1, i) for i in range(count - 1)])  6.66 us
  transfers between devices with their start and end apart: 22, of which 10 were waited for; matrix products, arithmetic and copies ran while one was open for 24% of the time, Pallas kernels for 0%

commit v1 on v0

--- a/solution.py
+++ b/solution.py
@@ -24,23 +24,6 @@
     return lax.ppermute(shard, axis, [(i, i ^ 1 << apart) for i in range(lax.axis_size(axis))])
 
 
-def extended(cells, sides, width):
-    for axis, dim in sides:
-        count = lax.axis_size(axis)
-        ends = count - 1
-        head = lax.slice_in_dim(cells, 0, width, axis=dim)
-        tail = lax.slice_in_dim(cells, cells.shape[dim] - width, cells.shape[dim], axis=dim)
-        cells = jnp.concatenate(
-            [
-                lax.ppermute(tail, axis, [(i, (i + 1) % count) for i in range(ends)]),
-                cells,
-                lax.ppermute(head, axis, [((i + 1) % count, i) for i in range(ends)]),
-            ],
-            axis=dim,
-        )
-    return cells
-
-
 def swapped(block):
     half = block.shape[-1] // 2
     return jnp.concatenate([-block[..., half:], block[..., :half]], axis=-1)
@@ -51,9 +34,9 @@
 
 
 def mix(block, other, weights):
-    total = apply_map(weights[0, 0], block) + apply_map(weights[0, 1], swapped(block))
-    total = total + apply_map(weights[1, 0], other) + apply_map(weights[1, 1], swapped(other))
-    return total.astype(jnp.bfloat16)
+    plain = apply_map(weights[0, 0], block) + apply_map(weights[1, 0], other)
+    turned = apply_map(weights[0, 1], block) + apply_map(weights[1, 1], other)
+    return (plain + swapped(turned)).astype(jnp.bfloat16)
 
 
 def basis(u, row):
@@ -74,9 +57,11 @@
     step = pl.program_id(0)
     row = lax.broadcasted_iota(jnp.int32, (PTS, ROWS), 0)
     live_row = lax.broadcasted_iota(jnp.int32, (ROWS, out_ref.shape[1]), 0)
-    for i in range(BLOCKS_PER_STEP):
+
+    def one_block(i, carry):
         b = step * BLOCKS_PER_STEP + i
-        u = pos_ref[:, i * ROWS:(i + 1) * ROWS]
+        start = pl.multiple_of(i * ROWS, ROWS)
+        u = pos_ref[:, pl.ds(start, ROWS)]
         lx = basis(u[0:1, :], row)
         ly = basis(u[1:2, :], row)
         lz = basis(u[2:3, :], row)
@@ -87,16 +72,19 @@
                 by = jnp.broadcast_to(ly[jy:jy + 1, :], (PTS, ROWS))
                 pieces.append((bx * by) * lz)
         weights_t = jnp.concatenate(pieces, axis=0).astype(jnp.bfloat16)
-        leaf = grid_ref[leaf_ref[b]]
-        values = lax.dot_general(
-            weights_t, leaf, (((0,), (0,)), ((), ())), preferred_element_type=jnp.float32
-        )
+        leaf = leaf_ref[b]
+        place = ((leaf // 2) % 4) * 4 + (leaf // 8) * 2 + leaf % 2
+        values = jnp.dot(grid_ref[place], weights_t, preferred_element_type=jnp.float32).T
         values = jnp.where(live_row < count_ref[b], values, 0.0)
-        out_ref[i * ROWS:(i + 1) * ROWS, :] = values.astype(out_ref.dtype)
+        out_ref[pl.ds(start, ROWS), :] = values.astype(out_ref.dtype)
+        return carry
+
+    lax.fori_loop(0, BLOCKS_PER_STEP, one_block, 0)
 
 
-def sample(leaf_grid, positions, block_leaf, block_count):
-    leaves, cheb, cols = leaf_grid.shape
+def sample(grid, positions, block_leaf, block_count):
+    lx, ly, lz, cheb, cols = grid.shape
+    leaf_grid = jnp.transpose(grid, (1, 0, 2, 4, 3)).reshape(ly * lx * lz, cols, cheb)
     blocks = block_leaf.shape[0]
     width = BLOCKS_PER_STEP * ROWS
     spec = pltpu.PrefetchScalarGridSpec(
@@ -104,7 +92,7 @@
         grid=(blocks // BLOCKS_PER_STEP,),
         in_specs=[
             pl.BlockSpec((3, width), lambda s, lf, ct: (0, s)),
-            pl.BlockSpec((leaves, cheb, cols), lambda s, lf, ct: (0, 0, 0)),
+            pl.BlockSpec((lx * ly * lz, cols, cheb), lambda s, lf, ct: (0, 0, 0)),
         ],
         out_specs=pl.BlockSpec((width, cols), lambda s, lf, ct: (s, 0)),
     )
@@ -115,13 +103,6 @@
     )(block_leaf, block_count, positions, leaf_grid)
 
 
-def butterfly(cells, level_weights):
-    for level in range(2):
-        cells = mix(cells, from_partner(cells, "gx", level), level_weights[level])
-    cells = mix(cells, from_partner(cells, "gy", 0), level_weights[2])
-    return mix(cells, from_partner(cells, "gz", 0), level_weights[3])
-
-
 LEVEL_PLAN = (("gx", 0), ("gx", 1), ("gy", 0), ("gz", 0))
 
 
@@ -130,11 +111,18 @@
     levels = len(LEVEL_PLAN)
     for tick in range(chunks + levels - 1):
         active = [k for k in range(chunks) if 0 <= tick - k < levels]
-        ready = lax.optimization_barrier(tuple(cells[k] for k in active))
-        for k, block in zip(active, ready):
+        ready = {}
+        for k in active:
+            if k > 0 and tick - k + 1 < levels:
+                ready[k], _ = lax.optimization_barrier((cells[k], cells[k - 1]))
+            else:
+                ready[k] = cells[k]
+        for k in active:
             level = tick - k
             axis, bit = LEVEL_PLAN[level]
-            cells[k] = mix(block, from_partner(block, axis, bit), level_weights[level])
+            block = ready[k]
+            other = from_partner(block, axis, bit)
+            cells[k] = mix(block, other, level_weights[level])
     return cells
 
 
@@ -168,9 +156,7 @@
     for index in range(6):
         total = total + apply_map(coupling[index], neighbours[index])
     grid = total.astype(jnp.bfloat16)
-    leaf_count = grid.shape[0] * grid.shape[1] * grid.shape[2]
-    leaf_grid = grid.reshape(leaf_count, grid.shape[3], grid.shape[4])
-    return sample(leaf_grid, positions, block_leaf, block_count)
+    return sample(grid, positions, block_leaf, block_count)
 
 
 def solution(mesh):

time: 184 us -> 188 us (1.022); the launches traced: 181 us -> 187 us
  Pallas kernels: 8.15 us -> 21.2 us
  starting transfers between devices: 31.8 us -> 29.6 us
  local copies, waits for them, and re-layouts: 10.8 us -> 8.62 us
    pallas_call x1, Pallas kernels: 8.15 us -> 21.2 us  [sample(): pl.pallas_call(sample_kernel, grid_spec=spec, out_shape=jax.ShapeDtypeStr...]
    convert_element_type x1 -> x0, local copies, waits for them, and re-layouts: 2.37 us -> none  [local(): grid = total.astype(jnp.bfloat16)]
where the time goes in v1:
time: 188 us; the launch traced here: 187 us
  waiting for transfers between devices  79.7 us (42%)
  matrix products  45.6 us (24%)
  starting transfers between devices  29.6 us (16%)
  Pallas kernels  21.2 us (11%)
  local copies, waits for them, and re-layouts  8.62 us (5%)
  other arithmetic  1.96 us (1%)
    ppermute x16, waiting for transfers between devices, from_partner(): lax.ppermute(shard, axis, [(i, i ^ 1 << apart) for i in range(lax.axis_si...  47.5 us
    dot_general x70, matrix products, apply_map(): jnp.einsum('jk,...kc->...jc', weights, block, preferred_element_type=jnp....  45.6 us
    ppermute x3, waiting for transfers between devices, from_above(): return lax.ppermute(slab, axis, [(i + 1, i) for i in range(count - 1)])  25.7 us
    pallas_call x1, Pallas kernels, sample(): pl.pallas_call(sample_kernel, grid_spec=spec, out_shape=jax.ShapeDtypeStr...  21.2 us
    ppermute x16, starting transfers between devices, from_partner(): lax.ppermute(shard, axis, [(i, i ^ 1 << apart) for i in range(lax.axis_si...  13.8 us
    ppermute x3, starting transfers between devices, from_below(): return lax.ppermute(slab, axis, [(i, i + 1) for i in range(count - 1)])  9.89 us
    ppermute x3, waiting for transfers between devices, from_below(): return lax.ppermute(slab, axis, [(i, i + 1) for i in range(count - 1)])  6.49 us
    ppermute x3, starting transfers between devices, from_above(): return lax.ppermute(slab, axis, [(i + 1, i) for i in range(count - 1)])  5.92 us
  transfers between devices with their start and end apart: 22, of which 10 were waited for; matrix products, arithmetic and copies ran while one was open for 24% of the time, Pallas kernels for 0%

profile of v1, /device:TPU:34, one launch (start us, length us, event | category | flops | bytes accessed | tf_op | source)
XLA Modules:
  0.0 187.5 jit_solution(11575513379518401049)
XLA Ops:
  0.0 1.7 fusion.214
  1.7 1.0 copy.57
  2.9 1.0 copy.58
  4.2 4.0 %slice_bitcast_fusion = (bf16[2,2,512,512]{3,2,1,0:T(8,128)(2,1)S(1)}, bf16[2,2,512,512]{3,2,1,0:T(8,128)(2,1)S(1)}, bf16[2,2,512,512]{3,2,1,0:T(8,128)(2,1)S(1)}, bf16[2,2,512,512]{3,2,1,0:T(8,128)(2,1)S(1)}) fusion(bf16[4,2,2,512,512]{4,3,2,1,0:T(8,128)(2,1)} %param.7), kind=kLoop, calls=%fused_computation.39 | loop fusion | bytes 16777216 | tf_op jit(solution)/shard_map/squeeze | solution.py:125
  8.2 0.5 fusion.96
  8.7 0.5 fusion.98
  9.2 1.5 fusion.62
  10.9 1.6 fusion.95
  12.6 0.5 collective-permute-start.4
  15.6 0.5 fusion.91
  17.1 9.7 %collective-permute-done.1 = bf16[2,1,2,512,128]{3,4,2,0,1:T(8,128)(2,1)S(1)} collective-permute-done((bf16[2,1,2,512,128]{3,4,2,0,1:T(8,128)(2,1)S(1)}, bf16[2,1,2,512,128]{3,4,2,0,1:T(8,128)(2,1)S(1)}, u32[]{:S(2)}, u32[]{:S(2)}) %collective-permute-start.1) | collective-permute-done | bytes 524320 | tf_op jit(solution)/shard_map/ppermute | solution.py:24
  27.9 0.6 collective-permute-start.2
  32.8 8.9 %collective-permute-done.5 = bf16[2,1,2,512,128]{3,4,2,0,1:T(8,128)(2,1)S(1)} collective-permute-done((bf16[2,1,2,512,128]{3,4,2,0,1:T(8,128)(2,1)S(1)}, bf16[2,1,2,512,128]{3,4,2,0,1:T(8,128)(2,1)S(1)}, u32[]{:S(2)}, u32[]{:S(2)}) %collective-permute-start.5) | collective-permute-done | bytes 524320 | tf_op jit(solution)/shard_map/ppermute | solution.py:24
  42.3 0.5 fusion.90
  42.8 0.8 collective-permute-start.9
  45.7 1.5 collective-permute-start.3
  47.2 1.5 collective-permute-start.6
  51.2 4.2 %collective-permute-done.9 = bf16[2,1,2,512,128]{3,4,2,0,1:T(8,128)(2,1)S(1)} collective-permute-done((bf16[2,1,2,512,128]{3,4,2,0,1:T(8,128)(2,1)S(1)}, bf16[2,1,2,512,128]{3,4,2,0,1:T(8,128)(2,1)S(1)}, u32[]{:S(2)}, u32[]{:S(2)}) %collective-permute-start.9) | collective-permute-done | bytes 524320 | tf_op jit(solution)/shard_map/ppermute | solution.py:24
  56.0 0.5 fusion.83
  56.5 0.5 fusion.86
  57.0 0.9 collective-permute-start.13
  59.7 0.5 fusion.89
  60.2 1.1 collective-permute-start.7
  61.4 1.5 collective-permute-start.10
  65.8 2.4 %collective-permute-start.19 = (bf16[2,1,2,512,128]{3,4,2,0,1:T(8,128)(2,1)S(1)}, bf16[2,1,2,512,128]{3,4,2,0,1:T(8,128)(2,1)S(1)}, u32[]{:S(2)}, u32[]{:S(2)}) collective-permute-start(bf16[2,1,2,512,128]{3,4,2,0,1:T(8,128)(2,1)S(1)} %fusion.92), channel_id=1, source_target_pairs={{8,0},{16,8},{24,16},{9,1},{17,9},{25,17},{10,2},{18,10},{26,18},{... | collective-permute-start | bytes 1572872 | tf_op jit(solution)/shard_map/ppermute | solution.py:136
  69.1 6.0 %collective-permute-done.10 = bf16[2,1,2,512,128]{3,4,2,0,1:T(8,128)(2,1)S(1)} collective-permute-done((bf16[2,1,2,512,128]{3,4,2,0,1:T(8,128)(2,1)S(1)}, bf16[2,1,2,512,128]{3,4,2,0,1:T(8,128)(2,1)S(1)}, u32[]{:S(2)}, u32[]{:S(2)}) %collective-permute-start.10) | collective-permute-done | bytes 524320 | tf_op jit(solution)/shard_map/ppermute | solution.py:24
  75.8 0.5 fusion.85
  76.2 1.1 collective-permute-start.11
  77.3 0.5 fusion.82
  77.8 2.8 %collective-permute-start.14 = (bf16[2,1,2,512,128]{3,4,2,0,1:T(8,128)(2,1)S(1)}, bf16[2,1,2,512,128]{3,4,2,0,1:T(8,128)(2,1)S(1)}, u32[]{:S(2)}, u32[]{:S(2)}) collective-permute-start(bf16[2,1,2,512,128]{3,4,2,0,1:T(8,128)(2,1)S(1)} %fusion.82), channel_id=1, source_target_pairs={{0,8},{8,0},{16,24},{24,16},{1,9},{9,1},{17,25},{25,17},{2,10},{10... | collective-permute-start | bytes 1572872 | tf_op jit(solution)/shard_map/ppermute | solution.py:24
  83.0 0.5 fusion.88
  83.5 10.4 %collective-permute-done.14 = bf16[2,1,2,512,128]{3,4,2,0,1:T(8,128)(2,1)S(1)} collective-permute-done((bf16[2,1,2,512,128]{3,4,2,0,1:T(8,128)(2,1)S(1)}, bf16[2,1,2,512,128]{3,4,2,0,1:T(8,128)(2,1)S(1)}, u32[]{:S(2)}, u32[]{:S(2)}) %collective-permute-start.14) | collective-permute-done | bytes 524320 | tf_op jit(solution)/shard_map/ppermute | solution.py:24
  95.0 0.8 collective-permute-start.15
  97.8 7.5 %collective-permute-done.15 = bf16[2,1,2,512,128]{3,4,2,0,1:T(8,128)(2,1)S(1)} collective-permute-done((bf16[2,1,2,512,128]{3,4,2,0,1:T(8,128)(2,1)S(1)}, bf16[2,1,2,512,128]{3,4,2,0,1:T(8,128)(2,1)S(1)}, u32[]{:S(2)}, u32[]{:S(2)}) %collective-permute-start.15) | collective-permute-done | bytes 524320 | tf_op jit(solution)/shard_map/ppermute | solution.py:24
  106.4 5.0 %collective-permute-start.18 = (bf16[2,1,2,512,128]{3,4,2,0,1:T(8,128)(2,1)S(1)}, bf16[2,1,2,512,128]{3,4,2,0,1:T(8,128)(2,1)S(1)}, u32[]{:S(2)}, u32[]{:S(2)}) collective-permute-start(bf16[2,1,2,512,128]{3,4,2,0,1:T(8,128)(2,1)S(1)} %fusion.80), channel_id=1, source_target_pairs={{0,8},{8,16},{16,24},{1,9},{9,17},{17,25},{2,10},{10,18},{18,26},{... | collective-permute-start | bytes 1572872 | tf_op jit(solution)/shard_map/ppermute | solution.py:131
  111.9 2.2 %collective-permute-start.17 = (bf16[1,4,2,512,128]{3,4,2,0,1:T(8,128)(2,1)S(1)}, bf16[1,4,2,512,128]{3,4,2,0,1:T(8,128)(2,1)S(1)}, u32[]{:S(2)}, u32[]{:S(2)}) collective-permute-start(bf16[1,4,2,512,128]{3,4,2,0,1:T(8,128)(2,1)S(1)} %get-tuple-element.28), channel_id=1, source_target_pairs={{32,0},{64,32},{96,64},{33,1},{65,33},{97,65},{34,2},{66,34},{98,6... | collective-permute-start | bytes 3145736 | tf_op jit(solution)/shard_map/ppermute | solution.py:136
  114.4 2.4 %collective-permute-start.20 = (bf16[2,4,1,512,128]{3,4,2,0,1:T(8,128)(2,1)S(1)}, bf16[2,4,1,512,128]{3,4,2,0,1:T(8,128)(2,1)S(1)}, u32[]{:S(2)}, u32[]{:S(2)}) collective-permute-start(bf16[2,4,1,512,128]{3,4,2,0,1:T(8,128)(2,1)S(1)} %get-tuple-element.29), channel_id=1, source_target_pairs={{0,1},{1,2},{2,3},{3,4},{4,5},{5,6},{6,7},{8,9},{9,10},{10,11},{11... | collective-permute-start | bytes 3145736 | tf_op jit(solution)/shard_map/ppermute | solution.py:131
  116.8 1.3 collective-permute-start.21
  118.1 2.4 %collective-permute-start.16 = (bf16[1,4,2,512,128]{3,4,2,0,1:T(8,128)(2,1)S(1)}, bf16[1,4,2,512,128]{3,4,2,0,1:T(8,128)(2,1)S(1)}, u32[]{:S(2)}, u32[]{:S(2)}) collective-permute-start(bf16[1,4,2,512,128]{3,4,2,0,1:T(8,128)(2,1)S(1)} %get-tuple-element.27), channel_id=1, source_target_pairs={{0,32},{32,64},{64,96},{1,33},{33,65},{65,97},{2,34},{34,66},{66,9... | collective-permute-start | bytes 3145736 | tf_op jit(solution)/shard_map/ppermute | solution.py:131
  120.5 1.3 fusion.17
  121.9 1.3 fusion.9
  123.2 25.7 %collective-permute-done.17 = bf16[1,4,2,512,128]{3,4,2,0,1:T(8,128)(2,1)S(1)} collective-permute-done((bf16[1,4,2,512,128]{3,4,2,0,1:T(8,128)(2,1)S(1)}, bf16[1,4,2,512,128]{3,4,2,0,1:T(8,128)(2,1)S(1)}, u32[]{:S(2)}, u32[]{:S(2)}) %collective-permute-start.17) | collective-permute-done | bytes 1048608 | tf_op jit(solution)/shard_map/ppermute | solution.py:136
  148.9 1.3 fusion.5
  150.2 6.5 %collective-permute-done.16 = bf16[1,4,2,512,128]{3,4,2,0,1:T(8,128)(2,1)S(1)} collective-permute-done((bf16[1,4,2,512,128]{3,4,2,0,1:T(8,128)(2,1)S(1)}, bf16[1,4,2,512,128]{3,4,2,0,1:T(8,128)(2,1)S(1)}, u32[]{:S(2)}, u32[]{:S(2)}) %collective-permute-start.16) | collective-permute-done | bytes 1048608 | tf_op jit(solution)/shard_map/ppermute | solution.py:131
  156.7 1.3 fusion.1
  158.0 3.3 %fusion.25 = f32[2,4,2,128,512]{4,3,2,0,1:T(8,128)} fusion(bf16[2,4,1,512,128]{3,4,2,0,1:T(8,128)(2,1)S(1)} %get-tuple-element.30, bf16[2,4,1,512,128]{3,4,2,0,1:T(8,128)(2,1)S(1)} %collective-permute-done.20, bf16[6,512,512]{2,1,0:T(8,128)(2,1)S(1)} %copy-done.4), kind=kOutput, calls=%fused_computation.32 | convolution fusion | flops 1074790400 | bytes 6815744 | tf_op jit(solution)/shard_map/jk,...kc->...jc/dot_general | solution.py:33
  161.3 5.1 %fusion = bf16[2,4,2,512,128]{3,4,2,0,1:T(8,128)(2,1)} fusion(f32[2,4,2,128,512]{4,3,2,0,1:T(8,128)} %fusion.25, f32[2,4,2,128,512]{4,3,2,0,1:T(8,128)S(1)} %fusion.17, f32[2,4,2,128,512]{4,3,2,0,1:T(8,128)S(1)} %fusion.9, f32[2,4,2,128,512]{4,3,2,0,1:T(8,128)S(1)} %fusion.5, f32[2,4,2,128,512]{4,3,2,0,1:T(8,128)S(1)} %fusion.1, ...), kind=kOutput, calls=%fused_computation.1 | convolution fusion | flops 1086324736 | bytes 27787264 | tf_op jit(solution)/shard_map/jk,...kc->...jc/dot_general | solution.py:33
  166.3 21.2 %shard_map.64 = bf16[8192,128]{1,0:T(8,128)(2,1)} custom-call(s32[64]{0:T(128)} %leaf_ref.1, s32[64]{0:T(128)} %count_ref.1, f32[3,8192]{1,0:T(4,128)} %pos_ref.1, bf16[16,128,512]{2,1,0:T(8,128)(2,1)} %bitcast.591), custom_call_target="tpu_custom_call" | custom-call | tf_op jit(solution)/shard_map/pallas_call | solution.py:99
  (102 shorter events, 28.4 us)
Async XLA Ops:
  2.7 6.5 %collective-permute-start = (bf16[2,1,2,512,128]{3,4,2,0,1:T(8,128)(2,1)}, bf16[2,1,2,512,128]{3,4,2,0,1:T(8,128)(2,1)}, u32[]{:S(2)}, u32[]{:S(2)}) collective-permute-start(bf16[2,1,2,512,128]{3,4,2,0,1:T(8,128)(2,1)} %copy.57), channel_id=1, source_target_pairs={{0,32},{32,0},{64,96},{96,64},{1,33},{33,1},{65,97},{97,65},{2,34}... | collective-permute-start | bytes 1572872 | tf_op jit(solution)/shard_map/ppermute | solution.py:24
  4.2 4.1 %copy-start = (bf16[2,4,2,512,128]{4,3,2,1,0:T(8,128)(2,1)S(1)}, bf16[2,4,2,512,128]{4,3,2,1,0:T(8,128)(2,1)}, u32[]{:S(2)}) copy-start(bf16[2,4,2,512,128]{4,3,2,1,0:T(8,128)(2,1)} %param.6) | copy-start | bytes 6291460
  10.9 1.8 copy-start.1
  12.4 14.4 %collective-permute-start.1 = (bf16[2,1,2,512,128]{3,4,2,0,1:T(8,128)(2,1)S(1)}, bf16[2,1,2,512,128]{3,4,2,0,1:T(8,128)(2,1)S(1)}, u32[]{:S(2)}, u32[]{:S(2)}) collective-permute-start(bf16[2,1,2,512,128]{3,4,2,0,1:T(8,128)(2,1)S(1)} %fusion.95), channel_id=1, source_target_pairs={{0,64},{32,96},{64,0},{96,32},{1,65},{33,97},{65,1},{97,33},{2,66}... | collective-permute-start | bytes 1572872 | tf_op jit(solution)/shard_map/ppermute | solution.py:24
  12.6 2.4 %collective-permute-start.4 = (bf16[2,1,2,512,128]{3,4,2,0,1:T(8,128)(2,1)S(1)}, bf16[2,1,2,512,128]{3,4,2,0,1:T(8,128)(2,1)S(1)}, u32[]{:S(2)}, u32[]{:S(2)}) collective-permute-start(bf16[2,1,2,512,128]{3,4,2,0,1:T(8,128)(2,1)S(1)} %copy-done.1), channel_id=1, source_target_pairs={{0,32},{32,0},{64,96},{96,64},{1,33},{33,1},{65,97},{97,65},{2,34}... | collective-permute-start | bytes 1572872 | tf_op jit(solution)/shard_map/ppermute | solution.py:24
  16.1 14.6 %collective-permute-start.8 = (bf16[2,1,2,512,128]{3,4,2,0,1:T(8,128)(2,1)S(1)}, bf16[2,1,2,512,128]{3,4,2,0,1:T(8,128)(2,1)S(1)}, u32[]{:S(2)}, u32[]{:S(2)}) collective-permute-start(bf16[2,1,2,512,128]{3,4,2,0,1:T(8,128)(2,1)S(1)} %copy.59), channel_id=1, source_target_pairs={{0,32},{32,0},{64,96},{96,64},{1,33},{33,1},{65,97},{97,65},{2,34}... | collective-permute-start | bytes 1572872 | tf_op jit(solution)/shard_map/ppermute | solution.py:24
  27.9 16.7 %collective-permute-start.2 = (bf16[2,1,2,512,128]{3,4,2,0,1:T(8,128)(2,1)S(1)}, bf16[2,1,2,512,128]{3,4,2,0,1:T(8,128)(2,1)S(1)}, u32[]{:S(2)}, u32[]{:S(2)}) collective-permute-start(bf16[2,1,2,512,128]{3,4,2,0,1:T(8,128)(2,1)S(1)} %fusion.94), channel_id=1, source_target_pairs={{0,8},{8,0},{16,24},{24,16},{1,9},{9,1},{17,25},{25,17},{2,10},{10... | collective-permute-start | bytes 1572872 | tf_op jit(solution)/shard_map/ppermute | solution.py:24
  28.5 13.2 %collective-permute-start.5 = (bf16[2,1,2,512,128]{3,4,2,0,1:T(8,128)(2,1)S(1)}, bf16[2,1,2,512,128]{3,4,2,0,1:T(8,128)(2,1)S(1)}, u32[]{:S(2)}, u32[]{:S(2)}) collective-permute-start(bf16[2,1,2,512,128]{3,4,2,0,1:T(8,128)(2,1)S(1)} %fusion.91), channel_id=1, source_target_pairs={{0,64},{32,96},{64,0},{96,32},{1,65},{33,97},{65,1},{97,33},{2,66}... | collective-permute-start | bytes 1572872 | tf_op jit(solution)/shard_map/ppermute | solution.py:24
  31.8 18.8 %collective-permute-start.12 = (bf16[2,1,2,512,128]{3,4,2,0,1:T(8,128)(2,1)S(1)}, bf16[2,1,2,512,128]{3,4,2,0,1:T(8,128)(2,1)S(1)}, u32[]{:S(2)}, u32[]{:S(2)}) collective-permute-start(bf16[2,1,2,512,128]{3,4,2,0,1:T(8,128)(2,1)S(1)} %copy.60), channel_id=1, source_target_pairs={{0,32},{32,0},{64,96},{96,64},{1,33},{33,1},{65,97},{97,65},{2,34}... | collective-permute-start | bytes 1572872 | tf_op jit(solution)/shard_map/ppermute | solution.py:24
  42.8 12.6 %collective-permute-start.9 = (bf16[2,1,2,512,128]{3,4,2,0,1:T(8,128)(2,1)S(1)}, bf16[2,1,2,512,128]{3,4,2,0,1:T(8,128)(2,1)S(1)}, u32[]{:S(2)}, u32[]{:S(2)}) collective-permute-start(bf16[2,1,2,512,128]{3,4,2,0,1:T(8,128)(2,1)S(1)} %fusion.87), channel_id=1, source_target_pairs={{0,64},{32,96},{64,0},{96,32},{1,65},{33,97},{65,1},{97,33},{2,66}... | collective-permute-start | bytes 1572872 | tf_op jit(solution)/shard_map/ppermute | solution.py:24
  45.7 18.1 %collective-permute-start.3 = (bf16[2,1,2,512,128]{3,4,2,0,1:T(8,128)(2,1)S(1)}, bf16[2,1,2,512,128]{3,4,2,0,1:T(8,128)(2,1)S(1)}, u32[]{:S(2)}, u32[]{:S(2)}) collective-permute-start(bf16[2,1,2,512,128]{3,4,2,0,1:T(8,128)(2,1)S(1)} %fusion.93), channel_id=1, source_target_pairs={{0,1},{1,0},{2,3},{3,2},{4,5},{5,4},{6,7},{7,6},{8,9},{9,8},{10,11... | collective-permute-start | bytes 1572872 | tf_op jit(solution)/shard_map/ppermute | solution.py:24
  47.2 12.0 %collective-permute-start.6 = (bf16[2,1,2,512,128]{3,4,2,0,1:T(8,128)(2,1)S(1)}, bf16[2,1,2,512,128]{3,4,2,0,1:T(8,128)(2,1)S(1)}, u32[]{:S(2)}, u32[]{:S(2)}) collective-permute-start(bf16[2,1,2,512,128]{3,4,2,0,1:T(8,128)(2,1)S(1)} %fusion.90), channel_id=1, source_target_pairs={{0,8},{8,0},{16,24},{24,16},{1,9},{9,1},{17,25},{25,17},{2,10},{10... | collective-permute-start | bytes 1572872 | tf_op jit(solution)/shard_map/ppermute | solution.py:24
  57.0 11.6 %collective-permute-start.13 = (bf16[2,1,2,512,128]{3,4,2,0,1:T(8,128)(2,1)S(1)}, bf16[2,1,2,512,128]{3,4,2,0,1:T(8,128)(2,1)S(1)}, u32[]{:S(2)}, u32[]{:S(2)}) collective-permute-start(bf16[2,1,2,512,128]{3,4,2,0,1:T(8,128)(2,1)S(1)} %fusion.83), channel_id=1, source_target_pairs={{0,64},{32,96},{64,0},{96,32},{1,65},{33,97},{65,1},{97,33},{2,66}... | collective-permute-start | bytes 1572872 | tf_op jit(solution)/shard_map/ppermute | solution.py:24
  60.2 22.2 %collective-permute-start.7 = (bf16[2,1,2,512,128]{3,4,2,0,1:T(8,128)(2,1)S(1)}, bf16[2,1,2,512,128]{3,4,2,0,1:T(8,128)(2,1)S(1)}, u32[]{:S(2)}, u32[]{:S(2)}) collective-permute-start(bf16[2,1,2,512,128]{3,4,2,0,1:T(8,128)(2,1)S(1)} %fusion.89), channel_id=1, source_target_pairs={{0,1},{1,0},{2,3},{3,2},{4,5},{5,4},{6,7},{7,6},{8,9},{9,8},{10,11... | collective-permute-start | bytes 1572872 | tf_op jit(solution)/shard_map/ppermute | solution.py:24
  61.4 13.8 %collective-permute-start.10 = (bf16[2,1,2,512,128]{3,4,2,0,1:T(8,128)(2,1)S(1)}, bf16[2,1,2,512,128]{3,4,2,0,1:T(8,128)(2,1)S(1)}, u32[]{:S(2)}, u32[]{:S(2)}) collective-permute-start(bf16[2,1,2,512,128]{3,4,2,0,1:T(8,128)(2,1)S(1)} %fusion.86), channel_id=1, source_target_pairs={{0,8},{8,0},{16,24},{24,16},{1,9},{9,1},{17,25},{25,17},{2,10},{10... | collective-permute-start | bytes 1572872 | tf_op jit(solution)/shard_map/ppermute | solution.py:24
  65.8 52.2 %collective-permute-start.19 = (bf16[2,1,2,512,128]{3,4,2,0,1:T(8,128)(2,1)S(1)}, bf16[2,1,2,512,128]{3,4,2,0,1:T(8,128)(2,1)S(1)}, u32[]{:S(2)}, u32[]{:S(2)}) collective-permute-start(bf16[2,1,2,512,128]{3,4,2,0,1:T(8,128)(2,1)S(1)} %fusion.92), channel_id=1, source_target_pairs={{8,0},{16,8},{24,16},{9,1},{17,9},{25,17},{10,2},{18,10},{26,18},{... | collective-permute-start | bytes 1572872 | tf_op jit(solution)/shard_map/ppermute | solution.py:136
  76.2 20.5 %collective-permute-start.11 = (bf16[2,1,2,512,128]{3,4,2,0,1:T(8,128)(2,1)S(1)}, bf16[2,1,2,512,128]{3,4,2,0,1:T(8,128)(2,1)S(1)}, u32[]{:S(2)}, u32[]{:S(2)}) collective-permute-start(bf16[2,1,2,512,128]{3,4,2,0,1:T(8,128)(2,1)S(1)} %fusion.85), channel_id=1, source_target_pairs={{0,1},{1,0},{2,3},{3,2},{4,5},{5,4},{6,7},{7,6},{8,9},{9,8},{10,11... | collective-permute-start | bytes 1572872 | tf_op jit(solution)/shard_map/ppermute | solution.py:24
  77.8 16.2 %collective-permute-start.14 = (bf16[2,1,2,512,128]{3,4,2,0,1:T(8,128)(2,1)S(1)}, bf16[2,1,2,512,128]{3,4,2,0,1:T(8,128)(2,1)S(1)}, u32[]{:S(2)}, u32[]{:S(2)}) collective-permute-start(bf16[2,1,2,512,128]{3,4,2,0,1:T(8,128)(2,1)S(1)} %fusion.82), channel_id=1, source_target_pairs={{0,8},{8,0},{16,24},{24,16},{1,9},{9,1},{17,25},{25,17},{2,10},{10... | collective-permute-start | bytes 1572872 | tf_op jit(solution)/shard_map/ppermute | solution.py:24
  95.0 10.3 %collective-permute-start.15 = (bf16[2,1,2,512,128]{3,4,2,0,1:T(8,128)(2,1)S(1)}, bf16[2,1,2,512,128]{3,4,2,0,1:T(8,128)(2,1)S(1)}, u32[]{:S(2)}, u32[]{:S(2)}) collective-permute-start(bf16[2,1,2,512,128]{3,4,2,0,1:T(8,128)(2,1)S(1)} %fusion.81), channel_id=1, source_target_pairs={{0,1},{1,0},{2,3},{3,2},{4,5},{5,4},{6,7},{7,6},{8,9},{9,8},{10,11... | collective-permute-start | bytes 1572872 | tf_op jit(solution)/shard_map/ppermute | solution.py:24
  106.4 15.5 %collective-permute-start.18 = (bf16[2,1,2,512,128]{3,4,2,0,1:T(8,128)(2,1)S(1)}, bf16[2,1,2,512,128]{3,4,2,0,1:T(8,128)(2,1)S(1)}, u32[]{:S(2)}, u32[]{:S(2)}) collective-permute-start(bf16[2,1,2,512,128]{3,4,2,0,1:T(8,128)(2,1)S(1)} %fusion.80), channel_id=1, source_target_pairs={{0,8},{8,16},{16,24},{1,9},{9,17},{17,25},{2,10},{10,18},{18,26},{... | collective-permute-start | bytes 1572872 | tf_op jit(solution)/shard_map/ppermute | solution.py:131
  111.9 8.6 %copy-start.4 = (bf16[6,512,512]{2,1,0:T(8,128)(2,1)S(1)}, bf16[6,512,512]{2,1,0:T(8,128)(2,1)}, u32[]{:S(2)}) copy-start(bf16[6,512,512]{2,1,0:T(8,128)(2,1)} %param.8) | copy-start | bytes 9437188
  111.9 37.0 %collective-permute-start.17 = (bf16[1,4,2,512,128]{3,4,2,0,1:T(8,128)(2,1)S(1)}, bf16[1,4,2,512,128]{3,4,2,0,1:T(8,128)(2,1)S(1)}, u32[]{:S(2)}, u32[]{:S(2)}) collective-permute-start(bf16[1,4,2,512,128]{3,4,2,0,1:T(8,128)(2,1)S(1)} %get-tuple-element.28), channel_id=1, source_target_pairs={{32,0},{64,32},{96,64},{33,1},{65,33},{97,65},{34,2},{66,34},{98,6... | collective-permute-start | bytes 3145736 | tf_op jit(solution)/shard_map/ppermute | solution.py:136
  114.3 7.5 %copy-start.2 = (bf16[2,4,1,512,128]{3,4,2,0,1:T(8,128)(2,1)}, bf16[2,4,1,512,128]{3,4,2,0,1:T(8,128)(2,1)S(1)}, u32[]{:S(2)}) copy-start(bf16[2,4,1,512,128]{3,4,2,0,1:T(8,128)(2,1)S(1)} %get-tuple-element.29) | copy-start | bytes 3145732
  114.4 43.6 %collective-permute-start.20 = (bf16[2,4,1,512,128]{3,4,2,0,1:T(8,128)(2,1)S(1)}, bf16[2,4,1,512,128]{3,4,2,0,1:T(8,128)(2,1)S(1)}, u32[]{:S(2)}, u32[]{:S(2)}) collective-permute-start(bf16[2,4,1,512,128]{3,4,2,0,1:T(8,128)(2,1)S(1)} %get-tuple-element.29), channel_id=1, source_target_pairs={{0,1},{1,2},{2,3},{3,4},{4,5},{5,6},{6,7},{8,9},{9,10},{10,11},{11... | collective-permute-start | bytes 3145736 | tf_op jit(solution)/shard_map/ppermute | solution.py:131
  116.8 44.5 %collective-permute-start.21 = (bf16[2,4,1,512,128]{3,4,2,0,1:T(8,128)(2,1)S(1)}, bf16[2,4,1,512,128]{3,4,2,0,1:T(8,128)(2,1)S(1)}, u32[]{:S(2)}, u32[]{:S(2)}) collective-permute-start(bf16[2,4,1,512,128]{3,4,2,0,1:T(8,128)(2,1)S(1)} %get-tuple-element.30), channel_id=1, source_target_pairs={{1,0},{2,1},{3,2},{4,3},{5,4},{6,5},{7,6},{9,8},{10,9},{11,10},{12... | collective-permute-start | bytes 3145736 | tf_op jit(solution)/shard_map/ppermute | solution.py:136
  118.1 38.6 %collective-permute-start.16 = (bf16[1,4,2,512,128]{3,4,2,0,1:T(8,128)(2,1)S(1)}, bf16[1,4,2,512,128]{3,4,2,0,1:T(8,128)(2,1)S(1)}, u32[]{:S(2)}, u32[]{:S(2)}) collective-permute-start(bf16[1,4,2,512,128]{3,4,2,0,1:T(8,128)(2,1)S(1)} %get-tuple-element.27), channel_id=1, source_target_pairs={{0,32},{32,64},{64,96},{1,33},{33,65},{65,97},{2,34},{34,66},{66,9... | collective-permute-start | bytes 3145736 | tf_op jit(solution)/shard_map/ppermute | solution.py:131
  158.0 3.3 %copy-start.3 = (bf16[2,4,1,512,128]{3,4,2,0,1:T(8,128)(2,1)S(1)}, bf16[2,4,1,512,128]{3,4,2,0,1:T(8,128)(2,1)}, u32[]{:S(2)}) copy-start(bf16[2,4,1,512,128]{3,4,2,0,1:T(8,128)(2,1)} %copy-done.2) | copy-start | bytes 3145732

commit v2 on v1

--- a/solution.py
+++ b/solution.py
@@ -57,11 +57,9 @@
     step = pl.program_id(0)
     row = lax.broadcasted_iota(jnp.int32, (PTS, ROWS), 0)
     live_row = lax.broadcasted_iota(jnp.int32, (ROWS, out_ref.shape[1]), 0)
-
-    def one_block(i, carry):
+    for i in range(BLOCKS_PER_STEP):
         b = step * BLOCKS_PER_STEP + i
-        start = pl.multiple_of(i * ROWS, ROWS)
-        u = pos_ref[:, pl.ds(start, ROWS)]
+        u = pos_ref[:, i * ROWS:(i + 1) * ROWS]
         lx = basis(u[0:1, :], row)
         ly = basis(u[1:2, :], row)
         lz = basis(u[2:3, :], row)
@@ -76,10 +74,7 @@
         place = ((leaf // 2) % 4) * 4 + (leaf // 8) * 2 + leaf % 2
         values = jnp.dot(grid_ref[place], weights_t, preferred_element_type=jnp.float32).T
         values = jnp.where(live_row < count_ref[b], values, 0.0)
-        out_ref[pl.ds(start, ROWS), :] = values.astype(out_ref.dtype)
-        return carry
-
-    lax.fori_loop(0, BLOCKS_PER_STEP, one_block, 0)
+        out_ref[i * ROWS:(i + 1) * ROWS, :] = values.astype(out_ref.dtype)
 
 
 def sample(grid, positions, block_leaf, block_count):

time: 188 us -> 176 us (0.936)
  Pallas kernels: 21.2 us -> 8.26 us
    pallas_call x1, Pallas kernels: 21.2 us -> 8.26 us  [sample(): pl.pallas_call(sample_kernel, grid_spec=spec, out_shape=jax.ShapeDtypeStr...]
  transfers between devices with their start and end apart: 22 -> 22, of which waited for: 10 -> 10; matrix products, arithmetic and copies ran while one was open for 24% -> 26% of each run, Pallas kernels for 0% -> 0%
where the time goes in v2:
time: 176 us; the launch traced here: 175 us
  waiting for transfers between devices  79.7 us (45%)
  matrix products  45.6 us (26%)
  starting transfers between devices  29.6 us (17%)
  local copies, waits for them, and re-layouts  8.62 us (5%)
  Pallas kernels  8.26 us (5%)
  other arithmetic  1.96 us (1%)
    ppermute x16, waiting for transfers between devices, from_partner(): lax.ppermute(shard, axis, [(i, i ^ 1 << apart) for i in range(lax.axis_si...  47.5 us
    dot_general x70, matrix products, apply_map(): jnp.einsum('jk,...kc->...jc', weights, block, preferred_element_type=jnp....  45.6 us
    ppermute x3, waiting for transfers between devices, from_above(): return lax.ppermute(slab, axis, [(i + 1, i) for i in range(count - 1)])  25.7 us
    ppermute x16, starting transfers between devices, from_partner(): lax.ppermute(shard, axis, [(i, i ^ 1 << apart) for i in range(lax.axis_si...  13.8 us
    ppermute x3, starting transfers between devices, from_below(): return lax.ppermute(slab, axis, [(i, i + 1) for i in range(count - 1)])  9.89 us
    pallas_call x1, Pallas kernels, sample(): pl.pallas_call(sample_kernel, grid_spec=spec, out_shape=jax.ShapeDtypeStr...  8.26 us
    ppermute x3, waiting for transfers between devices, from_below(): return lax.ppermute(slab, axis, [(i, i + 1) for i in range(count - 1)])  6.49 us
    ppermute x3, starting transfers between devices, from_above(): return lax.ppermute(slab, axis, [(i + 1, i) for i in range(count - 1)])  5.92 us
  transfers between devices with their start and end apart: 22, of which 10 were waited for; matrix products, arithmetic and copies ran while one was open for 26% of the time, Pallas kernels for 0%

profile of v2, /device:TPU:34, one launch (start us, length us, event | category | flops | bytes accessed | tf_op | source)
XLA Modules:
  0.0 174.6 jit_solution(10686473763726255930)
XLA Ops:
  0.0 1.7 fusion.214
  1.7 1.0 copy.57
  2.9 1.0 copy.58
  4.2 4.0 %slice_bitcast_fusion = (bf16[2,2,512,512]{3,2,1,0:T(8,128)(2,1)S(1)}, bf16[2,2,512,512]{3,2,1,0:T(8,128)(2,1)S(1)}, bf16[2,2,512,512]{3,2,1,0:T(8,128)(2,1)S(1)}, bf16[2,2,512,512]{3,2,1,0:T(8,128)(2,1)S(1)}) fusion(bf16[4,2,2,512,512]{4,3,2,1,0:T(8,128)(2,1)} %param.7), kind=kLoop, calls=%fused_computation.39 | loop fusion | bytes 16777216 | tf_op jit(solution)/shard_map/squeeze | solution.py:120
  8.2 0.5 fusion.96
  8.7 0.5 fusion.98
  9.2 1.5 fusion.62
  10.9 1.6 fusion.95
  12.6 0.5 collective-permute-start.4
  15.6 0.5 fusion.91
  17.1 9.7 %collective-permute-done.1 = bf16[2,1,2,512,128]{3,4,2,0,1:T(8,128)(2,1)S(1)} collective-permute-done((bf16[2,1,2,512,128]{3,4,2,0,1:T(8,128)(2,1)S(1)}, bf16[2,1,2,512,128]{3,4,2,0,1:T(8,128)(2,1)S(1)}, u32[]{:S(2)}, u32[]{:S(2)}) %collective-permute-start.1) | collective-permute-done | bytes 524320 | tf_op jit(solution)/shard_map/ppermute | solution.py:24
  27.9 0.6 collective-permute-start.2
  32.8 8.9 %collective-permute-done.5 = bf16[2,1,2,512,128]{3,4,2,0,1:T(8,128)(2,1)S(1)} collective-permute-done((bf16[2,1,2,512,128]{3,4,2,0,1:T(8,128)(2,1)S(1)}, bf16[2,1,2,512,128]{3,4,2,0,1:T(8,128)(2,1)S(1)}, u32[]{:S(2)}, u32[]{:S(2)}) %collective-permute-start.5) | collective-permute-done | bytes 524320 | tf_op jit(solution)/shard_map/ppermute | solution.py:24
  42.3 0.5 fusion.90
  42.8 0.8 collective-permute-start.9
  45.7 1.5 collective-permute-start.3
  47.2 1.5 collective-permute-start.6
  51.2 4.2 %collective-permute-done.9 = bf16[2,1,2,512,128]{3,4,2,0,1:T(8,128)(2,1)S(1)} collective-permute-done((bf16[2,1,2,512,128]{3,4,2,0,1:T(8,128)(2,1)S(1)}, bf16[2,1,2,512,128]{3,4,2,0,1:T(8,128)(2,1)S(1)}, u32[]{:S(2)}, u32[]{:S(2)}) %collective-permute-start.9) | collective-permute-done | bytes 524320 | tf_op jit(solution)/shard_map/ppermute | solution.py:24
  56.0 0.5 fusion.83
  56.5 0.5 fusion.86
  57.0 0.9 collective-permute-start.13
  59.7 0.5 fusion.89
  60.2 1.1 collective-permute-start.7
  61.4 1.5 collective-permute-start.10
  65.8 2.4 %collective-permute-start.19 = (bf16[2,1,2,512,128]{3,4,2,0,1:T(8,128)(2,1)S(1)}, bf16[2,1,2,512,128]{3,4,2,0,1:T(8,128)(2,1)S(1)}, u32[]{:S(2)}, u32[]{:S(2)}) collective-permute-start(bf16[2,1,2,512,128]{3,4,2,0,1:T(8,128)(2,1)S(1)} %fusion.92), channel_id=1, source_target_pairs={{8,0},{16,8},{24,16},{9,1},{17,9},{25,17},{10,2},{18,10},{26,18},{... | collective-permute-start | bytes 1572872 | tf_op jit(solution)/shard_map/ppermute | solution.py:131
  69.1 6.0 %collective-permute-done.10 = bf16[2,1,2,512,128]{3,4,2,0,1:T(8,128)(2,1)S(1)} collective-permute-done((bf16[2,1,2,512,128]{3,4,2,0,1:T(8,128)(2,1)S(1)}, bf16[2,1,2,512,128]{3,4,2,0,1:T(8,128)(2,1)S(1)}, u32[]{:S(2)}, u32[]{:S(2)}) %collective-permute-start.10) | collective-permute-done | bytes 524320 | tf_op jit(solution)/shard_map/ppermute | solution.py:24
  76.2 1.1 collective-permute-start.11
  77.3 0.5 fusion.82
  77.8 2.8 %collective-permute-start.14 = (bf16[2,1,2,512,128]{3,4,2,0,1:T(8,128)(2,1)S(1)}, bf16[2,1,2,512,128]{3,4,2,0,1:T(8,128)(2,1)S(1)}, u32[]{:S(2)}, u32[]{:S(2)}) collective-permute-start(bf16[2,1,2,512,128]{3,4,2,0,1:T(8,128)(2,1)S(1)} %fusion.82), channel_id=1, source_target_pairs={{0,8},{8,0},{16,24},{24,16},{1,9},{9,1},{17,25},{25,17},{2,10},{10... | collective-permute-start | bytes 1572872 | tf_op jit(solution)/shard_map/ppermute | solution.py:24
  83.0 0.5 fusion.88
  83.5 10.4 %collective-permute-done.14 = bf16[2,1,2,512,128]{3,4,2,0,1:T(8,128)(2,1)S(1)} collective-permute-done((bf16[2,1,2,512,128]{3,4,2,0,1:T(8,128)(2,1)S(1)}, bf16[2,1,2,512,128]{3,4,2,0,1:T(8,128)(2,1)S(1)}, u32[]{:S(2)}, u32[]{:S(2)}) %collective-permute-start.14) | collective-permute-done | bytes 524320 | tf_op jit(solution)/shard_map/ppermute | solution.py:24
  94.5 0.5 fusion.81
  95.0 0.8 collective-permute-start.15
  97.8 7.5 %collective-permute-done.15 = bf16[2,1,2,512,128]{3,4,2,0,1:T(8,128)(2,1)S(1)} collective-permute-done((bf16[2,1,2,512,128]{3,4,2,0,1:T(8,128)(2,1)S(1)}, bf16[2,1,2,512,128]{3,4,2,0,1:T(8,128)(2,1)S(1)}, u32[]{:S(2)}, u32[]{:S(2)}) %collective-permute-start.15) | collective-permute-done | bytes 524320 | tf_op jit(solution)/shard_map/ppermute | solution.py:24
  106.4 5.0 %collective-permute-start.18 = (bf16[2,1,2,512,128]{3,4,2,0,1:T(8,128)(2,1)S(1)}, bf16[2,1,2,512,128]{3,4,2,0,1:T(8,128)(2,1)S(1)}, u32[]{:S(2)}, u32[]{:S(2)}) collective-permute-start(bf16[2,1,2,512,128]{3,4,2,0,1:T(8,128)(2,1)S(1)} %fusion.80), channel_id=1, source_target_pairs={{0,8},{8,16},{16,24},{1,9},{9,17},{17,25},{2,10},{10,18},{18,26},{... | collective-permute-start | bytes 1572872 | tf_op jit(solution)/shard_map/ppermute | solution.py:126
  111.9 2.2 %collective-permute-start.17 = (bf16[1,4,2,512,128]{3,4,2,0,1:T(8,128)(2,1)S(1)}, bf16[1,4,2,512,128]{3,4,2,0,1:T(8,128)(2,1)S(1)}, u32[]{:S(2)}, u32[]{:S(2)}) collective-permute-start(bf16[1,4,2,512,128]{3,4,2,0,1:T(8,128)(2,1)S(1)} %get-tuple-element.28), channel_id=1, source_target_pairs={{32,0},{64,32},{96,64},{33,1},{65,33},{97,65},{34,2},{66,34},{98,6... | collective-permute-start | bytes 3145736 | tf_op jit(solution)/shard_map/ppermute | solution.py:131
  114.4 2.4 %collective-permute-start.20 = (bf16[2,4,1,512,128]{3,4,2,0,1:T(8,128)(2,1)S(1)}, bf16[2,4,1,512,128]{3,4,2,0,1:T(8,128)(2,1)S(1)}, u32[]{:S(2)}, u32[]{:S(2)}) collective-permute-start(bf16[2,4,1,512,128]{3,4,2,0,1:T(8,128)(2,1)S(1)} %get-tuple-element.29), channel_id=1, source_target_pairs={{0,1},{1,2},{2,3},{3,4},{4,5},{5,6},{6,7},{8,9},{9,10},{10,11},{11... | collective-permute-start | bytes 3145736 | tf_op jit(solution)/shard_map/ppermute | solution.py:126
  116.8 1.3 collective-permute-start.21
  118.1 2.4 %collective-permute-start.16 = (bf16[1,4,2,512,128]{3,4,2,0,1:T(8,128)(2,1)S(1)}, bf16[1,4,2,512,128]{3,4,2,0,1:T(8,128)(2,1)S(1)}, u32[]{:S(2)}, u32[]{:S(2)}) collective-permute-start(bf16[1,4,2,512,128]{3,4,2,0,1:T(8,128)(2,1)S(1)} %get-tuple-element.27), channel_id=1, source_target_pairs={{0,32},{32,64},{64,96},{1,33},{33,65},{65,97},{2,34},{34,66},{66,9... | collective-permute-start | bytes 3145736 | tf_op jit(solution)/shard_map/ppermute | solution.py:126
  120.5 1.3 fusion.17
  121.9 1.3 fusion.9
  123.2 25.7 %collective-permute-done.17 = bf16[1,4,2,512,128]{3,4,2,0,1:T(8,128)(2,1)S(1)} collective-permute-done((bf16[1,4,2,512,128]{3,4,2,0,1:T(8,128)(2,1)S(1)}, bf16[1,4,2,512,128]{3,4,2,0,1:T(8,128)(2,1)S(1)}, u32[]{:S(2)}, u32[]{:S(2)}) %collective-permute-start.17) | collective-permute-done | bytes 1048608 | tf_op jit(solution)/shard_map/ppermute | solution.py:131
  148.9 1.3 fusion.5
  150.2 6.5 %collective-permute-done.16 = bf16[1,4,2,512,128]{3,4,2,0,1:T(8,128)(2,1)S(1)} collective-permute-done((bf16[1,4,2,512,128]{3,4,2,0,1:T(8,128)(2,1)S(1)}, bf16[1,4,2,512,128]{3,4,2,0,1:T(8,128)(2,1)S(1)}, u32[]{:S(2)}, u32[]{:S(2)}) %collective-permute-start.16) | collective-permute-done | bytes 1048608 | tf_op jit(solution)/shard_map/ppermute | solution.py:126
  156.7 1.3 fusion.1
  158.0 3.3 %fusion.25 = f32[2,4,2,128,512]{4,3,2,0,1:T(8,128)} fusion(bf16[2,4,1,512,128]{3,4,2,0,1:T(8,128)(2,1)S(1)} %get-tuple-element.30, bf16[2,4,1,512,128]{3,4,2,0,1:T(8,128)(2,1)S(1)} %collective-permute-done.20, bf16[6,512,512]{2,1,0:T(8,128)(2,1)S(1)} %copy-done.4), kind=kOutput, calls=%fused_computation.32 | convolution fusion | flops 1074790400 | bytes 6815744 | tf_op jit(solution)/shard_map/jk,...kc->...jc/dot_general | solution.py:33
  161.3 5.1 %fusion = bf16[2,4,2,512,128]{3,4,2,0,1:T(8,128)(2,1)} fusion(f32[2,4,2,128,512]{4,3,2,0,1:T(8,128)} %fusion.25, f32[2,4,2,128,512]{4,3,2,0,1:T(8,128)S(1)} %fusion.17, f32[2,4,2,128,512]{4,3,2,0,1:T(8,128)S(1)} %fusion.9, f32[2,4,2,128,512]{4,3,2,0,1:T(8,128)S(1)} %fusion.5, f32[2,4,2,128,512]{4,3,2,0,1:T(8,128)S(1)} %fusion.1, ...), kind=kOutput, calls=%fused_computation.1 | convolution fusion | flops 1086324736 | bytes 27787264 | tf_op jit(solution)/shard_map/jk,...kc->...jc/dot_general | solution.py:33
  166.3 8.3 %shard_map.64 = bf16[8192,128]{1,0:T(8,128)(2,1)} custom-call(s32[64]{0:T(128)} %leaf_ref.1, s32[64]{0:T(128)} %count_ref.1, f32[3,8192]{1,0:T(4,128)} %pos_ref.1, bf16[16,128,512]{2,1,0:T(8,128)(2,1)} %bitcast.591), custom_call_target="tpu_custom_call" | custom-call | tf_op jit(solution)/shard_map/pallas_call | solution.py:94
  (102 shorter events, 28.4 us)
Async XLA Ops:
  2.7 6.5 %collective-permute-start = (bf16[2,1,2,512,128]{3,4,2,0,1:T(8,128)(2,1)}, bf16[2,1,2,512,128]{3,4,2,0,1:T(8,128)(2,1)}, u32[]{:S(2)}, u32[]{:S(2)}) collective-permute-start(bf16[2,1,2,512,128]{3,4,2,0,1:T(8,128)(2,1)} %copy.57), channel_id=1, source_target_pairs={{0,32},{32,0},{64,96},{96,64},{1,33},{33,1},{65,97},{97,65},{2,34}... | collective-permute-start | bytes 1572872 | tf_op jit(solution)/shard_map/ppermute | solution.py:24
  4.2 4.1 %copy-start = (bf16[2,4,2,512,128]{4,3,2,1,0:T(8,128)(2,1)S(1)}, bf16[2,4,2,512,128]{4,3,2,1,0:T(8,128)(2,1)}, u32[]{:S(2)}) copy-start(bf16[2,4,2,512,128]{4,3,2,1,0:T(8,128)(2,1)} %param.6) | copy-start | bytes 6291460
  10.9 1.8 %copy-start.1 = (bf16[2,1,2,512,128]{3,4,2,0,1:T(8,128)(2,1)S(1)}, bf16[2,1,2,512,128]{3,4,2,0,1:T(8,128)(2,1)}, u32[]{:S(2)}) copy-start(bf16[2,1,2,512,128]{3,4,2,0,1:T(8,128)(2,1)} %copy.58) | copy-start | bytes 1572868
  12.4 14.4 %collective-permute-start.1 = (bf16[2,1,2,512,128]{3,4,2,0,1:T(8,128)(2,1)S(1)}, bf16[2,1,2,512,128]{3,4,2,0,1:T(8,128)(2,1)S(1)}, u32[]{:S(2)}, u32[]{:S(2)}) collective-permute-start(bf16[2,1,2,512,128]{3,4,2,0,1:T(8,128)(2,1)S(1)} %fusion.95), channel_id=1, source_target_pairs={{0,64},{32,96},{64,0},{96,32},{1,65},{33,97},{65,1},{97,33},{2,66}... | collective-permute-start | bytes 1572872 | tf_op jit(solution)/shard_map/ppermute | solution.py:24
  12.6 2.4 %collective-permute-start.4 = (bf16[2,1,2,512,128]{3,4,2,0,1:T(8,128)(2,1)S(1)}, bf16[2,1,2,512,128]{3,4,2,0,1:T(8,128)(2,1)S(1)}, u32[]{:S(2)}, u32[]{:S(2)}) collective-permute-start(bf16[2,1,2,512,128]{3,4,2,0,1:T(8,128)(2,1)S(1)} %copy-done.1), channel_id=1, source_target_pairs={{0,32},{32,0},{64,96},{96,64},{1,33},{33,1},{65,97},{97,65},{2,34}... | collective-permute-start | bytes 1572872 | tf_op jit(solution)/shard_map/ppermute | solution.py:24
  16.1 14.6 %collective-permute-start.8 = (bf16[2,1,2,512,128]{3,4,2,0,1:T(8,128)(2,1)S(1)}, bf16[2,1,2,512,128]{3,4,2,0,1:T(8,128)(2,1)S(1)}, u32[]{:S(2)}, u32[]{:S(2)}) collective-permute-start(bf16[2,1,2,512,128]{3,4,2,0,1:T(8,128)(2,1)S(1)} %copy.59), channel_id=1, source_target_pairs={{0,32},{32,0},{64,96},{96,64},{1,33},{33,1},{65,97},{97,65},{2,34}... | collective-permute-start | bytes 1572872 | tf_op jit(solution)/shard_map/ppermute | solution.py:24
  27.9 16.7 %collective-permute-start.2 = (bf16[2,1,2,512,128]{3,4,2,0,1:T(8,128)(2,1)S(1)}, bf16[2,1,2,512,128]{3,4,2,0,1:T(8,128)(2,1)S(1)}, u32[]{:S(2)}, u32[]{:S(2)}) collective-permute-start(bf16[2,1,2,512,128]{3,4,2,0,1:T(8,128)(2,1)S(1)} %fusion.94), channel_id=1, source_target_pairs={{0,8},{8,0},{16,24},{24,16},{1,9},{9,1},{17,25},{25,17},{2,10},{10... | collective-permute-start | bytes 1572872 | tf_op jit(solution)/shard_map/ppermute | solution.py:24
  28.5 13.2 %collective-permute-start.5 = (bf16[2,1,2,512,128]{3,4,2,0,1:T(8,128)(2,1)S(1)}, bf16[2,1,2,512,128]{3,4,2,0,1:T(8,128)(2,1)S(1)}, u32[]{:S(2)}, u32[]{:S(2)}) collective-permute-start(bf16[2,1,2,512,128]{3,4,2,0,1:T(8,128)(2,1)S(1)} %fusion.91), channel_id=1, source_target_pairs={{0,64},{32,96},{64,0},{96,32},{1,65},{33,97},{65,1},{97,33},{2,66}... | collective-permute-start | bytes 1572872 | tf_op jit(solution)/shard_map/ppermute | solution.py:24
  31.8 18.8 %collective-permute-start.12 = (bf16[2,1,2,512,128]{3,4,2,0,1:T(8,128)(2,1)S(1)}, bf16[2,1,2,512,128]{3,4,2,0,1:T(8,128)(2,1)S(1)}, u32[]{:S(2)}, u32[]{:S(2)}) collective-permute-start(bf16[2,1,2,512,128]{3,4,2,0,1:T(8,128)(2,1)S(1)} %copy.60), channel_id=1, source_target_pairs={{0,32},{32,0},{64,96},{96,64},{1,33},{33,1},{65,97},{97,65},{2,34}... | collective-permute-start | bytes 1572872 | tf_op jit(solution)/shard_map/ppermute | solution.py:24
  42.8 12.6 %collective-permute-start.9 = (bf16[2,1,2,512,128]{3,4,2,0,1:T(8,128)(2,1)S(1)}, bf16[2,1,2,512,128]{3,4,2,0,1:T(8,128)(2,1)S(1)}, u32[]{:S(2)}, u32[]{:S(2)}) collective-permute-start(bf16[2,1,2,512,128]{3,4,2,0,1:T(8,128)(2,1)S(1)} %fusion.87), channel_id=1, source_target_pairs={{0,64},{32,96},{64,0},{96,32},{1,65},{33,97},{65,1},{97,33},{2,66}... | collective-permute-start | bytes 1572872 | tf_op jit(solution)/shard_map/ppermute | solution.py:24
  45.7 18.1 %collective-permute-start.3 = (bf16[2,1,2,512,128]{3,4,2,0,1:T(8,128)(2,1)S(1)}, bf16[2,1,2,512,128]{3,4,2,0,1:T(8,128)(2,1)S(1)}, u32[]{:S(2)}, u32[]{:S(2)}) collective-permute-start(bf16[2,1,2,512,128]{3,4,2,0,1:T(8,128)(2,1)S(1)} %fusion.93), channel_id=1, source_target_pairs={{0,1},{1,0},{2,3},{3,2},{4,5},{5,4},{6,7},{7,6},{8,9},{9,8},{10,11... | collective-permute-start | bytes 1572872 | tf_op jit(solution)/shard_map/ppermute | solution.py:24
  47.2 12.0 %collective-permute-start.6 = (bf16[2,1,2,512,128]{3,4,2,0,1:T(8,128)(2,1)S(1)}, bf16[2,1,2,512,128]{3,4,2,0,1:T(8,128)(2,1)S(1)}, u32[]{:S(2)}, u32[]{:S(2)}) collective-permute-start(bf16[2,1,2,512,128]{3,4,2,0,1:T(8,128)(2,1)S(1)} %fusion.90), channel_id=1, source_target_pairs={{0,8},{8,0},{16,24},{24,16},{1,9},{9,1},{17,25},{25,17},{2,10},{10... | collective-permute-start | bytes 1572872 | tf_op jit(solution)/shard_map/ppermute | solution.py:24
  57.0 11.6 %collective-permute-start.13 = (bf16[2,1,2,512,128]{3,4,2,0,1:T(8,128)(2,1)S(1)}, bf16[2,1,2,512,128]{3,4,2,0,1:T(8,128)(2,1)S(1)}, u32[]{:S(2)}, u32[]{:S(2)}) collective-permute-start(bf16[2,1,2,512,128]{3,4,2,0,1:T(8,128)(2,1)S(1)} %fusion.83), channel_id=1, source_target_pairs={{0,64},{32,96},{64,0},{96,32},{1,65},{33,97},{65,1},{97,33},{2,66}... | collective-permute-start | bytes 1572872 | tf_op jit(solution)/shard_map/ppermute | solution.py:24
  60.2 22.2 %collective-permute-start.7 = (bf16[2,1,2,512,128]{3,4,2,0,1:T(8,128)(2,1)S(1)}, bf16[2,1,2,512,128]{3,4,2,0,1:T(8,128)(2,1)S(1)}, u32[]{:S(2)}, u32[]{:S(2)}) collective-permute-start(bf16[2,1,2,512,128]{3,4,2,0,1:T(8,128)(2,1)S(1)} %fusion.89), channel_id=1, source_target_pairs={{0,1},{1,0},{2,3},{3,2},{4,5},{5,4},{6,7},{7,6},{8,9},{9,8},{10,11... | collective-permute-start | bytes 1572872 | tf_op jit(solution)/shard_map/ppermute | solution.py:24
  61.4 13.8 %collective-permute-start.10 = (bf16[2,1,2,512,128]{3,4,2,0,1:T(8,128)(2,1)S(1)}, bf16[2,1,2,512,128]{3,4,2,0,1:T(8,128)(2,1)S(1)}, u32[]{:S(2)}, u32[]{:S(2)}) collective-permute-start(bf16[2,1,2,512,128]{3,4,2,0,1:T(8,128)(2,1)S(1)} %fusion.86), channel_id=1, source_target_pairs={{0,8},{8,0},{16,24},{24,16},{1,9},{9,1},{17,25},{25,17},{2,10},{10... | collective-permute-start | bytes 1572872 | tf_op jit(solution)/shard_map/ppermute | solution.py:24
  65.8 52.2 %collective-permute-start.19 = (bf16[2,1,2,512,128]{3,4,2,0,1:T(8,128)(2,1)S(1)}, bf16[2,1,2,512,128]{3,4,2,0,1:T(8,128)(2,1)S(1)}, u32[]{:S(2)}, u32[]{:S(2)}) collective-permute-start(bf16[2,1,2,512,128]{3,4,2,0,1:T(8,128)(2,1)S(1)} %fusion.92), channel_id=1, source_target_pairs={{8,0},{16,8},{24,16},{9,1},{17,9},{25,17},{10,2},{18,10},{26,18},{... | collective-permute-start | bytes 1572872 | tf_op jit(solution)/shard_map/ppermute | solution.py:131
  76.2 20.5 %collective-permute-start.11 = (bf16[2,1,2,512,128]{3,4,2,0,1:T(8,128)(2,1)S(1)}, bf16[2,1,2,512,128]{3,4,2,0,1:T(8,128)(2,1)S(1)}, u32[]{:S(2)}, u32[]{:S(2)}) collective-permute-start(bf16[2,1,2,512,128]{3,4,2,0,1:T(8,128)(2,1)S(1)} %fusion.85), channel_id=1, source_target_pairs={{0,1},{1,0},{2,3},{3,2},{4,5},{5,4},{6,7},{7,6},{8,9},{9,8},{10,11... | collective-permute-start | bytes 1572872 | tf_op jit(solution)/shard_map/ppermute | solution.py:24
  77.8 16.2 %collective-permute-start.14 = (bf16[2,1,2,512,128]{3,4,2,0,1:T(8,128)(2,1)S(1)}, bf16[2,1,2,512,128]{3,4,2,0,1:T(8,128)(2,1)S(1)}, u32[]{:S(2)}, u32[]{:S(2)}) collective-permute-start(bf16[2,1,2,512,128]{3,4,2,0,1:T(8,128)(2,1)S(1)} %fusion.82), channel_id=1, source_target_pairs={{0,8},{8,0},{16,24},{24,16},{1,9},{9,1},{17,25},{25,17},{2,10},{10... | collective-permute-start | bytes 1572872 | tf_op jit(solution)/shard_map/ppermute | solution.py:24
  95.0 10.3 %collective-permute-start.15 = (bf16[2,1,2,512,128]{3,4,2,0,1:T(8,128)(2,1)S(1)}, bf16[2,1,2,512,128]{3,4,2,0,1:T(8,128)(2,1)S(1)}, u32[]{:S(2)}, u32[]{:S(2)}) collective-permute-start(bf16[2,1,2,512,128]{3,4,2,0,1:T(8,128)(2,1)S(1)} %fusion.81), channel_id=1, source_target_pairs={{0,1},{1,0},{2,3},{3,2},{4,5},{5,4},{6,7},{7,6},{8,9},{9,8},{10,11... | collective-permute-start | bytes 1572872 | tf_op jit(solution)/shard_map/ppermute | solution.py:24
  106.4 15.5 %collective-permute-start.18 = (bf16[2,1,2,512,128]{3,4,2,0,1:T(8,128)(2,1)S(1)}, bf16[2,1,2,512,128]{3,4,2,0,1:T(8,128)(2,1)S(1)}, u32[]{:S(2)}, u32[]{:S(2)}) collective-permute-start(bf16[2,1,2,512,128]{3,4,2,0,1:T(8,128)(2,1)S(1)} %fusion.80), channel_id=1, source_target_pairs={{0,8},{8,16},{16,24},{1,9},{9,17},{17,25},{2,10},{10,18},{18,26},{... | collective-permute-start | bytes 1572872 | tf_op jit(solution)/shard_map/ppermute | solution.py:126
  111.9 8.6 %copy-start.4 = (bf16[6,512,512]{2,1,0:T(8,128)(2,1)S(1)}, bf16[6,512,512]{2,1,0:T(8,128)(2,1)}, u32[]{:S(2)}) copy-start(bf16[6,512,512]{2,1,0:T(8,128)(2,1)} %param.8) | copy-start | bytes 9437188
  111.9 37.0 %collective-permute-start.17 = (bf16[1,4,2,512,128]{3,4,2,0,1:T(8,128)(2,1)S(1)}, bf16[1,4,2,512,128]{3,4,2,0,1:T(8,128)(2,1)S(1)}, u32[]{:S(2)}, u32[]{:S(2)}) collective-permute-start(bf16[1,4,2,512,128]{3,4,2,0,1:T(8,128)(2,1)S(1)} %get-tuple-element.28), channel_id=1, source_target_pairs={{32,0},{64,32},{96,64},{33,1},{65,33},{97,65},{34,2},{66,34},{98,6... | collective-permute-start | bytes 3145736 | tf_op jit(solution)/shard_map/ppermute | solution.py:131
  114.3 7.5 %copy-start.2 = (bf16[2,4,1,512,128]{3,4,2,0,1:T(8,128)(2,1)}, bf16[2,4,1,512,128]{3,4,2,0,1:T(8,128)(2,1)S(1)}, u32[]{:S(2)}) copy-start(bf16[2,4,1,512,128]{3,4,2,0,1:T(8,128)(2,1)S(1)} %get-tuple-element.29) | copy-start | bytes 3145732
  114.4 43.6 %collective-permute-start.20 = (bf16[2,4,1,512,128]{3,4,2,0,1:T(8,128)(2,1)S(1)}, bf16[2,4,1,512,128]{3,4,2,0,1:T(8,128)(2,1)S(1)}, u32[]{:S(2)}, u32[]{:S(2)}) collective-permute-start(bf16[2,4,1,512,128]{3,4,2,0,1:T(8,128)(2,1)S(1)} %get-tuple-element.29), channel_id=1, source_target_pairs={{0,1},{1,2},{2,3},{3,4},{4,5},{5,6},{6,7},{8,9},{9,10},{10,11},{11... | collective-permute-start | bytes 3145736 | tf_op jit(solution)/shard_map/ppermute | solution.py:126
  116.8 44.5 %collective-permute-start.21 = (bf16[2,4,1,512,128]{3,4,2,0,1:T(8,128)(2,1)S(1)}, bf16[2,4,1,512,128]{3,4,2,0,1:T(8,128)(2,1)S(1)}, u32[]{:S(2)}, u32[]{:S(2)}) collective-permute-start(bf16[2,4,1,512,128]{3,4,2,0,1:T(8,128)(2,1)S(1)} %get-tuple-element.30), channel_id=1, source_target_pairs={{1,0},{2,1},{3,2},{4,3},{5,4},{6,5},{7,6},{9,8},{10,9},{11,10},{12... | collective-permute-start | bytes 3145736 | tf_op jit(solution)/shard_map/ppermute | solution.py:131
  118.1 38.6 %collective-permute-start.16 = (bf16[1,4,2,512,128]{3,4,2,0,1:T(8,128)(2,1)S(1)}, bf16[1,4,2,512,128]{3,4,2,0,1:T(8,128)(2,1)S(1)}, u32[]{:S(2)}, u32[]{:S(2)}) collective-permute-start(bf16[1,4,2,512,128]{3,4,2,0,1:T(8,128)(2,1)S(1)} %get-tuple-element.27), channel_id=1, source_target_pairs={{0,32},{32,64},{64,96},{1,33},{33,65},{65,97},{2,34},{34,66},{66,9... | collective-permute-start | bytes 3145736 | tf_op jit(solution)/shard_map/ppermute | solution.py:126
  158.0 3.3 %copy-start.3 = (bf16[2,4,1,512,128]{3,4,2,0,1:T(8,128)(2,1)S(1)}, bf16[2,4,1,512,128]{3,4,2,0,1:T(8,128)(2,1)}, u32[]{:S(2)}) copy-start(bf16[2,4,1,512,128]{3,4,2,0,1:T(8,128)(2,1)} %copy-done.2) | copy-start | bytes 3145732

commit v3 on v2

--- a/solution.py
+++ b/solution.py
@@ -77,9 +77,8 @@
         out_ref[i * ROWS:(i + 1) * ROWS, :] = values.astype(out_ref.dtype)
 
 
-def sample(grid, positions, block_leaf, block_count):
-    lx, ly, lz, cheb, cols = grid.shape
-    leaf_grid = jnp.transpose(grid, (1, 0, 2, 4, 3)).reshape(ly * lx * lz, cols, cheb)
+def sample(leaf_grid, positions, block_leaf, block_count):
+    leaves, cols, cheb = leaf_grid.shape
     blocks = block_leaf.shape[0]
     width = BLOCKS_PER_STEP * ROWS
     spec = pltpu.PrefetchScalarGridSpec(
@@ -87,7 +86,7 @@
         grid=(blocks // BLOCKS_PER_STEP,),
         in_specs=[
             pl.BlockSpec((3, width), lambda s, lf, ct: (0, s)),
-            pl.BlockSpec((lx * ly * lz, cols, cheb), lambda s, lf, ct: (0, 0, 0)),
+            pl.BlockSpec((leaves, cols, cheb), lambda s, lf, ct: (0, 0, 0)),
         ],
         out_specs=pl.BlockSpec((width, cols), lambda s, lf, ct: (s, 0)),
     )
@@ -103,7 +102,9 @@
 
 def pipelined(coefficients, level_weights, chunks):
     cells = [coefficients[:, k:k + 1] for k in range(chunks)]
+    partner_faces = [None] * chunks
     levels = len(LEVEL_PLAN)
+    side = lax.axis_index("gz") % 2
     for tick in range(chunks + levels - 1):
         active = [k for k in range(chunks) if 0 <= tick - k < levels]
         ready = {}
@@ -118,7 +119,12 @@
             block = ready[k]
             other = from_partner(block, axis, bit)
             cells[k] = mix(block, other, level_weights[level])
-    return cells
+            if level == levels - 1:
+                partner_faces[k] = (
+                    lax.dynamic_slice_in_dim(other, side, 1, axis=2),
+                    lax.dynamic_slice_in_dim(block, side, 1, axis=2),
+                )
+    return cells, partner_faces
 
 
 def from_below(slab, axis):
@@ -131,27 +137,84 @@
     return lax.ppermute(slab, axis, [(i + 1, i) for i in range(count - 1)])
 
 
-def faces(cells, axis, dim):
-    size = cells.shape[dim]
-    first = lax.slice_in_dim(cells, 0, 1, axis=dim)
-    last = lax.slice_in_dim(cells, size - 1, size, axis=dim)
-    below = jnp.concatenate([from_below(last, axis), lax.slice_in_dim(cells, 0, size - 1, axis=dim)], axis=dim)
-    above = jnp.concatenate([lax.slice_in_dim(cells, 1, size, axis=dim), from_above(first, axis)], axis=dim)
-    return below, above
+def z_faces(cells, partner_face):
+    count = lax.axis_size("gz")
+    side = lax.axis_index("gz") % 2
+    pairs = [(i, i - 1) for i in range(2, count, 2)] + [(i, i + 1) for i in range(1, count - 1, 2)]
+    sent = lax.ppermute(lax.dynamic_slice_in_dim(cells, side, 1, axis=2), "gz", pairs)
+    even = side == 0
+    return jnp.where(even, sent, partner_face), jnp.where(even, partner_face, sent)
+
+
+def coupling_kernel(weight_ref, prev_ref, cell_ref, next_ref, xb_ref, xa_ref, yb_ref, ya_ref, zb_ref, za_ref, out_ref):
+    y = pl.program_id(0)
+    last = pl.num_programs(0) - 1
+
+    def coupled(block, index):
+        return lax.dot_general(
+            block, weight_ref[index], (((1,), (1,)), ((), ())), preferred_element_type=jnp.float32
+        )
+
+    for x in range(2):
+        for z in range(2):
+            own = cell_ref[0, x, z]
+            total = own.astype(jnp.float32)
+            total = total + coupled(xb_ref[0, 0, z] if x == 0 else cell_ref[0, 0, z], 0)
+            total = total + coupled(cell_ref[0, 1, z] if x == 0 else xa_ref[0, 0, z], 1)
+            total = total + coupled(jnp.where(y == 0, yb_ref[0, x, z], prev_ref[0, x, z]), 2)
+            total = total + coupled(jnp.where(y == last, ya_ref[0, x, z], next_ref[0, x, z]), 3)
+            total = total + coupled(zb_ref[0, x, 0] if z == 0 else cell_ref[0, x, 0], 4)
+            total = total + coupled(cell_ref[0, x, 1] if z == 0 else za_ref[0, x, 0], 5)
+            out_ref[0, x, z] = total.astype(out_ref.dtype)
+
+
+def couple(coupling, cells, xb, xa, yb, ya, zb, za):
+    def turned(a):
+        return jnp.transpose(a, (1, 0, 2, 4, 3))
+
+    lx, ly, lz, cheb, cols = cells.shape
+    leaf = (1, lx, lz, cols, cheb)
+    weight_spec = pl.BlockSpec(coupling.shape, lambda y: (0, 0, 0))
+    specs = [
+        weight_spec,
+        pl.BlockSpec(leaf, lambda y: (jnp.maximum(y - 1, 0), 0, 0, 0, 0)),
+        pl.BlockSpec(leaf, lambda y: (y, 0, 0, 0, 0)),
+        pl.BlockSpec(leaf, lambda y: (jnp.minimum(y + 1, ly - 1), 0, 0, 0, 0)),
+        pl.BlockSpec((1, 1, lz, cols, cheb), lambda y: (y, 0, 0, 0, 0)),
+        pl.BlockSpec((1, 1, lz, cols, cheb), lambda y: (y, 0, 0, 0, 0)),
+        pl.BlockSpec(leaf, lambda y: (0, 0, 0, 0, 0)),
+        pl.BlockSpec(leaf, lambda y: (0, 0, 0, 0, 0)),
+        pl.BlockSpec((1, lx, 1, cols, cheb), lambda y: (y, 0, 0, 0, 0)),
+        pl.BlockSpec((1, lx, 1, cols, cheb), lambda y: (y, 0, 0, 0, 0)),
+    ]
+    cells_t = turned(cells)
+    out = pl.pallas_call(
+        coupling_kernel,
+        grid=(ly,),
+        in_specs=specs,
+        out_specs=pl.BlockSpec(leaf, lambda y: (y, 0, 0, 0, 0)),
+        out_shape=jax.ShapeDtypeStruct((ly, lx, lz, cols, cheb), jnp.bfloat16),
+    )(coupling, cells_t, cells_t, cells_t, turned(xb), turned(xa), turned(yb), turned(ya), turned(zb), turned(za))
+    return out.reshape(ly * lx * lz, cols, cheb)
 
 
 def local(coefficients, level_weights, coupling, positions, block_leaf, block_count):
     chunks = coefficients.shape[1]
-    cells = jnp.concatenate(pipelined(coefficients, level_weights, chunks), axis=1)
-    minus_x, plus_x = faces(cells, "gx", 0)
-    minus_y, plus_y = faces(cells, "gy", 1)
-    minus_z, plus_z = faces(cells, "gz", 2)
-    neighbours = (minus_x, plus_x, minus_y, plus_y, minus_z, plus_z)
-    total = cells.astype(jnp.float32)
-    for index in range(6):
-        total = total + apply_map(coupling[index], neighbours[index])
-    grid = total.astype(jnp.bfloat16)
-    return sample(grid, positions, block_leaf, block_count)
+    done, partner_slabs = pipelined(coefficients, level_weights, chunks)
+    done[-1], partner_slabs = lax.optimization_barrier((done[-1], partner_slabs))
+    cells = jnp.concatenate(done, axis=1)
+    partner_face = mix(
+        jnp.concatenate([theirs for theirs, _ in partner_slabs], axis=1),
+        jnp.concatenate([ours for _, ours in partner_slabs], axis=1),
+        level_weights[len(LEVEL_PLAN) - 1],
+    )
+    xb = from_below(cells[cells.shape[0] - 1:], "gx")
+    xa = from_above(cells[:1], "gx")
+    yb = from_below(cells[:, cells.shape[1] - 1:], "gy")
+    ya = from_above(cells[:, :1], "gy")
+    zb, za = z_faces(cells, partner_face)
+    leaf_grid = couple(coupling, cells, xb, xa, yb, ya, zb, za)
+    return sample(leaf_grid, positions, block_leaf, block_count)
 
 
 def solution(mesh):

time: 176 us -> 188 us (1.068)
  Pallas kernels: 8.26 us -> 29 us
  matrix products: 45.6 us -> 39.2 us
  starting transfers between devices: 29.6 us -> 26.9 us
  waiting for transfers between devices: 79.7 us -> 77.4 us
  local copies, waits for them, and re-layouts: 8.62 us -> 10.5 us
    pallas_call x0 -> x1, Pallas kernels: none -> 20.8 us  [couple(): pl.pallas_call(coupling_kernel, grid=(ly,), in_specs=specs, out_specs=pl....]
    dot_general x70 -> x68, matrix products: 45.6 us -> 39.2 us  [apply_map(): jnp.einsum('jk,...kc->...jc', weights, block, preferred_element_type=jnp....]
    ppermute x3 -> x2, waiting for transfers between devices: 6.49 us -> 3.93 us  [from_below(): return lax.ppermute(slab, axis, [(i, i + 1) for i in range(count - 1)])]
    ppermute x3 -> x2, starting transfers between devices: 9.89 us -> 7.52 us  [from_below(): return lax.ppermute(slab, axis, [(i, i + 1) for i in range(count - 1)])]
    ppermute x3 -> x2, starting transfers between devices: 5.92 us -> 4.36 us  [from_above(): return lax.ppermute(slab, axis, [(i + 1, i) for i in range(count - 1)])]
    ppermute x3 -> x2, waiting for transfers between devices: 25.7 us -> 26.6 us  [from_above(): return lax.ppermute(slab, axis, [(i + 1, i) for i in range(count - 1)])]
  transfers between devices with their start and end apart: 22 -> 21, of which waited for: 10 -> 9; matrix products, arithmetic and copies ran while one was open for 26% -> 25% of each run, Pallas kernels for 0% -> 0%
where the time goes in v3:
time: 188 us; the launch traced here: 187 us
  waiting for transfers between devices  77.4 us (41%)
  matrix products  39.2 us (21%)
  Pallas kernels  29 us (15%)
  starting transfers between devices  26.9 us (14%)
  local copies, waits for them, and re-layouts  10.5 us (6%)
  other arithmetic  3.57 us (2%)
    ppermute x16, waiting for transfers between devices, from_partner(): lax.ppermute(shard, axis, [(i, i ^ 1 << apart) for i in range(lax.axis_si...  46.8 us
    dot_general x68, matrix products, apply_map(): jnp.einsum('jk,...kc->...jc', weights, block, preferred_element_type=jnp....  39.2 us
    ppermute x2, waiting for transfers between devices, from_above(): return lax.ppermute(slab, axis, [(i + 1, i) for i in range(count - 1)])  26.6 us
    pallas_call x1, Pallas kernels, couple(): pl.pallas_call(coupling_kernel, grid=(ly,), in_specs=specs, out_specs=pl....  20.8 us
    ppermute x16, starting transfers between devices, from_partner(): lax.ppermute(shard, axis, [(i, i ^ 1 << apart) for i in range(lax.axis_si...  14.2 us
    pallas_call x1, Pallas kernels, sample(): pl.pallas_call(sample_kernel, grid_spec=spec, out_shape=jax.ShapeDtypeStr...  8.25 us
    ppermute x2, starting transfers between devices, from_below(): return lax.ppermute(slab, axis, [(i, i + 1) for i in range(count - 1)])  7.52 us
    squeeze x1, local copies, waits for them, and re-layouts, pipelined(): cells[k] = mix(block, other, level_weights[level])  5.74 us
  transfers between devices with their start and end apart: 21, of which 9 were waited for; matrix products, arithmetic and copies ran while one was open for 25% of the time, Pallas kernels for 0%

profile of v3, /device:TPU:34, one launch (start us, length us, event | category | flops | bytes accessed | tf_op | source)
XLA Modules:
  0.0 187.4 jit_solution(17504595683909773216)
XLA Ops:
  0.0 1.7 fusion.211
  1.7 1.0 copy.43
  3.0 1.0 copy.44
  4.2 5.7 %slice_bitcast_fusion = (bf16[2,2,512,512]{3,2,1,0:T(8,128)(2,1)}, bf16[2,2,512,512]{3,2,1,0:T(8,128)(2,1)}, bf16[2,2,512,512]{3,2,1,0:T(8,128)(2,1)}, bf16[2,2,512,512]{3,2,1,0:T(8,128)(2,1)S(1)}) fusion(bf16[4,2,2,512,512]{4,3,2,1,0:T(8,128)(2,1)} %param.7), kind=kLoop, calls=%fused_computation.4 | loop fusion | bytes 16777216 | tf_op jit(solution)/shard_map/squeeze | solution.py:121
  10.0 1.8 fusion.65
  11.9 1.5 fusion.67
  13.4 1.5 fusion.31
  15.1 1.6 fusion.64
  16.8 0.5 collective-permute-start.4
  20.3 0.5 collective-permute-start.8
  21.8 9.3 %collective-permute-done.1 = bf16[2,1,2,512,128]{3,4,2,0,1:T(8,128)(2,1)S(1)} collective-permute-done((bf16[2,1,2,512,128]{3,4,2,0,1:T(8,128)(2,1)S(1)}, bf16[2,1,2,512,128]{3,4,2,0,1:T(8,128)(2,1)S(1)}, u32[]{:S(2)}, u32[]{:S(2)}) %collective-permute-start.1) | collective-permute-done | bytes 524320 | tf_op jit(solution)/shard_map/ppermute | solution.py:24
  32.1 0.6 collective-permute-start.2
  35.5 0.5 fusion.56
  37.0 8.9 %collective-permute-done.5 = bf16[2,1,2,512,128]{3,4,2,0,1:T(8,128)(2,1)S(1)} collective-permute-done((bf16[2,1,2,512,128]{3,4,2,0,1:T(8,128)(2,1)S(1)}, bf16[2,1,2,512,128]{3,4,2,0,1:T(8,128)(2,1)S(1)}, u32[]{:S(2)}, u32[]{:S(2)}) %collective-permute-start.5) | collective-permute-done | bytes 524320 | tf_op jit(solution)/shard_map/ppermute | solution.py:24
  47.0 0.8 collective-permute-start.9
  49.8 1.6 collective-permute-start.3
  51.4 1.5 collective-permute-start.6
  55.4 4.2 %collective-permute-done.9 = bf16[2,1,2,512,128]{3,4,2,0,1:T(8,128)(2,1)S(1)} collective-permute-done((bf16[2,1,2,512,128]{3,4,2,0,1:T(8,128)(2,1)S(1)}, bf16[2,1,2,512,128]{3,4,2,0,1:T(8,128)(2,1)S(1)}, u32[]{:S(2)}, u32[]{:S(2)}) %collective-permute-start.9) | collective-permute-done | bytes 524320 | tf_op jit(solution)/shard_map/ppermute | solution.py:24
  60.2 0.5 fusion.52
  61.2 0.9 collective-permute-start.13
  64.0 0.5 fusion.58
  64.5 1.1 collective-permute-start.7
  65.6 1.5 collective-permute-start.10
  68.6 0.5 fusion.61
  69.1 2.4 %collective-permute-start.19 = (bf16[2,1,2,512,128]{3,4,2,0,1:T(8,128)(2,1)S(1)}, bf16[2,1,2,512,128]{3,4,2,0,1:T(8,128)(2,1)S(1)}, u32[]{:S(2)}, u32[]{:S(2)}) collective-permute-start(bf16[2,1,2,512,128]{3,4,2,0,1:T(8,128)(2,1)S(1)} %fusion.61), channel_id=1, source_target_pairs={{8,0},{16,8},{24,16},{9,1},{17,9},{25,17},{10,2},{18,10},{26,18},{... | collective-permute-start | bytes 1572872 | tf_op jit(solution)/shard_map/ppermute | solution.py:137
  72.6 6.9 %collective-permute-done.10 = bf16[2,1,2,512,128]{3,4,2,0,1:T(8,128)(2,1)S(1)} collective-permute-done((bf16[2,1,2,512,128]{3,4,2,0,1:T(8,128)(2,1)S(1)}, bf16[2,1,2,512,128]{3,4,2,0,1:T(8,128)(2,1)S(1)}, u32[]{:S(2)}, u32[]{:S(2)}) %collective-permute-start.10) | collective-permute-done | bytes 524320 | tf_op jit(solution)/shard_map/ppermute | solution.py:24
  80.0 0.5 fusion.54
  80.5 1.1 collective-permute-start.11
  82.7 2.8 %collective-permute-start.14 = (bf16[2,1,2,512,128]{3,4,2,0,1:T(8,128)(2,1)S(1)}, bf16[2,1,2,512,128]{3,4,2,0,1:T(8,128)(2,1)S(1)}, u32[]{:S(2)}, u32[]{:S(2)}) collective-permute-start(bf16[2,1,2,512,128]{3,4,2,0,1:T(8,128)(2,1)S(1)} %fusion.51), channel_id=1, source_target_pairs={{0,8},{8,0},{16,24},{24,16},{1,9},{9,1},{17,25},{25,17},{2,10},{10... | collective-permute-start | bytes 1572872 | tf_op jit(solution)/shard_map/ppermute | solution.py:24
  88.4 9.8 %collective-permute-done.14 = bf16[2,1,2,512,128]{3,4,2,0,1:T(8,128)(2,1)S(1)} collective-permute-done((bf16[2,1,2,512,128]{3,4,2,0,1:T(8,128)(2,1)S(1)}, bf16[2,1,2,512,128]{3,4,2,0,1:T(8,128)(2,1)S(1)}, u32[]{:S(2)}, u32[]{:S(2)}) %collective-permute-start.14) | collective-permute-done | bytes 524320 | tf_op jit(solution)/shard_map/ppermute | solution.py:24
  98.8 0.5 fusion.50
  99.3 0.8 collective-permute-start.15
  101.7 0.5 fusion.53
  102.1 7.5 %collective-permute-done.15 = bf16[2,1,2,512,128]{3,4,2,0,1:T(8,128)(2,1)S(1)} collective-permute-done((bf16[2,1,2,512,128]{3,4,2,0,1:T(8,128)(2,1)S(1)}, bf16[2,1,2,512,128]{3,4,2,0,1:T(8,128)(2,1)S(1)}, u32[]{:S(2)}, u32[]{:S(2)}) %collective-permute-start.15) | collective-permute-done | bytes 524320 | tf_op jit(solution)/shard_map/ppermute | solution.py:24
  110.2 0.5 fusion.49
  110.7 5.1 %collective-permute-start.18 = (bf16[2,1,2,512,128]{3,4,2,0,1:T(8,128)(2,1)S(1)}, bf16[2,1,2,512,128]{3,4,2,0,1:T(8,128)(2,1)S(1)}, u32[]{:S(2)}, u32[]{:S(2)}) collective-permute-start(bf16[2,1,2,512,128]{3,4,2,0,1:T(8,128)(2,1)S(1)} %fusion.49), channel_id=1, source_target_pairs={{0,8},{8,16},{16,24},{1,9},{9,17},{17,25},{2,10},{10,18},{18,26},{... | collective-permute-start | bytes 1572872 | tf_op jit(solution)/shard_map/ppermute | solution.py:132
  115.8 1.7 pad_maximum_fusion
  117.7 1.9 %collective-permute-start.17 = (bf16[1,4,2,512,128]{3,4,2,0,1:T(8,128)(2,1)S(1)}, bf16[1,4,2,512,128]{3,4,2,0,1:T(8,128)(2,1)S(1)}, u32[]{:S(2)}, u32[]{:S(2)}) collective-permute-start(bf16[1,4,2,512,128]{3,4,2,0,1:T(8,128)(2,1)S(1)} %get-tuple-element.49), channel_id=1, source_target_pairs={{32,0},{64,32},{96,64},{33,1},{65,33},{97,65},{34,2},{66,34},{98,6... | collective-permute-start | bytes 3145736 | tf_op jit(solution)/shard_map/ppermute | solution.py:137
  119.7 2.5 %collective-permute-start.16 = (bf16[1,4,2,512,128]{3,4,2,0,1:T(8,128)(2,1)S(1)}, bf16[1,4,2,512,128]{3,4,2,0,1:T(8,128)(2,1)}, u32[]{:S(2)}, u32[]{:S(2)}) collective-permute-start(bf16[1,4,2,512,128]{3,4,2,0,1:T(8,128)(2,1)S(1)} %get-tuple-element.50), channel_id=1, source_target_pairs={{0,32},{32,64},{64,96},{1,33},{33,65},{65,97},{2,34},{34,66},{66,9... | collective-permute-start | bytes 3145736 | tf_op jit(solution)/shard_map/ppermute | solution.py:132
  122.1 0.7 collective-permute-start.20
  122.9 0.7 fusion.128
  123.6 0.7 add_bitcast_fusion
  124.7 0.7 fusion.143
  125.4 2.4 %select_bitcast_fusion = (bf16[4,2,1,128,512]{4,3,2,1,0:T(8,128)(2,1)}, bf16[4,2,1,128,512]{4,3,2,1,0:T(8,128)(2,1)}) fusion(bf16[2,4,1,512,128]{3,4,2,0,1:T(8,128)(2,1)S(1)} %collective-permute-done.20, pred[]{:T(512)S(6)} %eq.6, f32[2,4,1,512,64]{3,4,2,0,1:T(8,128)S(1)} %get-tuple-element.48, f32[2,4,1,512,64]{3,4,2,0,1:T(8,128)S(1)} %get-tuple-element.47, ...), kind=kOutput, calls=%fused_computation.107 | convolution fusion | flops 541589504 | bytes 8912897 | tf_op jit(solution)/shard_map/jk,...kc->...jc/dot_general | solution.py:33
  127.8 26.6 %collective-permute-done.17 = bf16[1,4,2,512,128]{3,4,2,0,1:T(8,128)(2,1)S(1)} collective-permute-done((bf16[1,4,2,512,128]{3,4,2,0,1:T(8,128)(2,1)S(1)}, bf16[1,4,2,512,128]{3,4,2,0,1:T(8,128)(2,1)S(1)}, u32[]{:S(2)}, u32[]{:S(2)}) %collective-permute-start.17) | collective-permute-done | bytes 1048608 | tf_op jit(solution)/shard_map/ppermute | solution.py:137
  154.4 3.9 %collective-permute-done.16 = bf16[1,4,2,512,128]{3,4,2,0,1:T(8,128)(2,1)} collective-permute-done((bf16[1,4,2,512,128]{3,4,2,0,1:T(8,128)(2,1)S(1)}, bf16[1,4,2,512,128]{3,4,2,0,1:T(8,128)(2,1)}, u32[]{:S(2)}, u32[]{:S(2)}) %collective-permute-start.16) | collective-permute-done | bytes 1048608 | tf_op jit(solution)/shard_map/ppermute | solution.py:132
  158.4 20.8 %shard_map.64 = bf16[4,2,2,128,512]{4,3,2,1,0:T(8,128)(2,1)} custom-call(bf16[6,512,512]{2,1,0:T(8,128)(2,1)} %weight_ref.1, bf16[4,2,2,128,512]{4,3,2,1,0:T(8,128)(2,1)} %get-tuple-element.52.prev_ref.cell_ref.next_ref, bf16[4,2,2,128,512]{4,3,2,1,0:T(8,128)(2,1)} %get-tuple-element.52.prev_ref.cell_ref.next_ref, ...), custom_call_target="tpu_custom_call" | custom-call | tf_op jit(solution)/shard_map/pallas_call | solution.py:191
  179.2 8.2 %shard_map.65 = bf16[8192,128]{1,0:T(8,128)(2,1)} custom-call(s32[64]{0:T(128)} %leaf_ref.1, s32[64]{0:T(128)} %count_ref.1, f32[3,8192]{1,0:T(4,128)} %pos_ref.1, bf16[16,128,512]{2,1,0:T(8,128)(2,1)} %bitcast.575), custom_call_target="tpu_custom_call" | custom-call | tf_op jit(solution)/shard_map/pallas_call | solution.py:93
  (112 shorter events, 28.2 us)
Async XLA Ops:
  2.8 10.6 %collective-permute-start = (bf16[2,1,2,512,128]{3,4,2,0,1:T(8,128)(2,1)}, bf16[2,1,2,512,128]{3,4,2,0,1:T(8,128)(2,1)}, u32[]{:S(2)}, u32[]{:S(2)}) collective-permute-start(bf16[2,1,2,512,128]{3,4,2,0,1:T(8,128)(2,1)} %copy.43), channel_id=1, source_target_pairs={{0,32},{32,0},{64,96},{96,64},{1,33},{33,1},{65,97},{97,65},{2,34}... | collective-permute-start | bytes 1572872 | tf_op jit(solution)/shard_map/ppermute | solution.py:24
  10.0 1.9 %copy-start.1 = (bf16[2,2,512,512]{3,2,1,0:T(8,128)(2,1)S(1)}, bf16[2,2,512,512]{3,2,1,0:T(8,128)(2,1)}, u32[]{:S(2)}) copy-start(bf16[2,2,512,512]{3,2,1,0:T(8,128)(2,1)} %get-tuple-element.43) | copy-start | bytes 6291460
  15.0 1.8 copy-start.3
  16.6 1.6 copy-start
  16.6 14.4 %collective-permute-start.1 = (bf16[2,1,2,512,128]{3,4,2,0,1:T(8,128)(2,1)S(1)}, bf16[2,1,2,512,128]{3,4,2,0,1:T(8,128)(2,1)S(1)}, u32[]{:S(2)}, u32[]{:S(2)}) collective-permute-start(bf16[2,1,2,512,128]{3,4,2,0,1:T(8,128)(2,1)S(1)} %fusion.64), channel_id=1, source_target_pairs={{0,64},{32,96},{64,0},{96,32},{1,65},{33,97},{65,1},{97,33},{2,66}... | collective-permute-start | bytes 1572872 | tf_op jit(solution)/shard_map/ppermute | solution.py:24
  16.8 2.4 %collective-permute-start.4 = (bf16[2,1,2,512,128]{3,4,2,0,1:T(8,128)(2,1)S(1)}, bf16[2,1,2,512,128]{3,4,2,0,1:T(8,128)(2,1)S(1)}, u32[]{:S(2)}, u32[]{:S(2)}) collective-permute-start(bf16[2,1,2,512,128]{3,4,2,0,1:T(8,128)(2,1)S(1)} %copy-done.3), channel_id=1, source_target_pairs={{0,32},{32,0},{64,96},{96,64},{1,33},{33,1},{65,97},{97,65},{2,34}... | collective-permute-start | bytes 1572872 | tf_op jit(solution)/shard_map/ppermute | solution.py:24
  20.3 14.6 %collective-permute-start.8 = (bf16[2,1,2,512,128]{3,4,2,0,1:T(8,128)(2,1)S(1)}, bf16[2,1,2,512,128]{3,4,2,0,1:T(8,128)(2,1)S(1)}, u32[]{:S(2)}, u32[]{:S(2)}) collective-permute-start(bf16[2,1,2,512,128]{3,4,2,0,1:T(8,128)(2,1)S(1)} %copy.45), channel_id=1, source_target_pairs={{0,32},{32,0},{64,96},{96,64},{1,33},{33,1},{65,97},{97,65},{2,34}... | collective-permute-start | bytes 1572872 | tf_op jit(solution)/shard_map/ppermute | solution.py:24
  32.1 16.6 %collective-permute-start.2 = (bf16[2,1,2,512,128]{3,4,2,0,1:T(8,128)(2,1)S(1)}, bf16[2,1,2,512,128]{3,4,2,0,1:T(8,128)(2,1)S(1)}, u32[]{:S(2)}, u32[]{:S(2)}) collective-permute-start(bf16[2,1,2,512,128]{3,4,2,0,1:T(8,128)(2,1)S(1)} %fusion.63), channel_id=1, source_target_pairs={{0,8},{8,0},{16,24},{24,16},{1,9},{9,1},{17,25},{25,17},{2,10},{10... | collective-permute-start | bytes 1572872 | tf_op jit(solution)/shard_map/ppermute | solution.py:24
  32.7 13.2 %collective-permute-start.5 = (bf16[2,1,2,512,128]{3,4,2,0,1:T(8,128)(2,1)S(1)}, bf16[2,1,2,512,128]{3,4,2,0,1:T(8,128)(2,1)S(1)}, u32[]{:S(2)}, u32[]{:S(2)}) collective-permute-start(bf16[2,1,2,512,128]{3,4,2,0,1:T(8,128)(2,1)S(1)} %fusion.60), channel_id=1, source_target_pairs={{0,64},{32,96},{64,0},{96,32},{1,65},{33,97},{65,1},{97,33},{2,66}... | collective-permute-start | bytes 1572872 | tf_op jit(solution)/shard_map/ppermute | solution.py:24
  36.0 18.8 %collective-permute-start.12 = (bf16[2,1,2,512,128]{3,4,2,0,1:T(8,128)(2,1)S(1)}, bf16[2,1,2,512,128]{3,4,2,0,1:T(8,128)(2,1)S(1)}, u32[]{:S(2)}, u32[]{:S(2)}) collective-permute-start(bf16[2,1,2,512,128]{3,4,2,0,1:T(8,128)(2,1)S(1)} %copy.46), channel_id=1, source_target_pairs={{0,32},{32,0},{64,96},{96,64},{1,33},{33,1},{65,97},{97,65},{2,34}... | collective-permute-start | bytes 1572872 | tf_op jit(solution)/shard_map/ppermute | solution.py:24
  47.0 12.6 %collective-permute-start.9 = (bf16[2,1,2,512,128]{3,4,2,0,1:T(8,128)(2,1)S(1)}, bf16[2,1,2,512,128]{3,4,2,0,1:T(8,128)(2,1)S(1)}, u32[]{:S(2)}, u32[]{:S(2)}) collective-permute-start(bf16[2,1,2,512,128]{3,4,2,0,1:T(8,128)(2,1)S(1)} %fusion.56), channel_id=1, source_target_pairs={{0,64},{32,96},{64,0},{96,32},{1,65},{33,97},{65,1},{97,33},{2,66}... | collective-permute-start | bytes 1572872 | tf_op jit(solution)/shard_map/ppermute | solution.py:24
  49.8 4.0 %copy-start.2 = (bf16[2,2,512,512]{3,2,1,0:T(8,128)(2,1)S(1)}, bf16[2,2,512,512]{3,2,1,0:T(8,128)(2,1)}, u32[]{:S(2)}) copy-start(bf16[2,2,512,512]{3,2,1,0:T(8,128)(2,1)} %get-tuple-element.41) | copy-start | bytes 6291460
  49.8 18.2 %collective-permute-start.3 = (bf16[2,1,2,512,128]{3,4,2,0,1:T(8,128)(2,1)S(1)}, bf16[2,1,2,512,128]{3,4,2,0,1:T(8,128)(2,1)S(1)}, u32[]{:S(2)}, u32[]{:S(2)}) collective-permute-start(bf16[2,1,2,512,128]{3,4,2,0,1:T(8,128)(2,1)S(1)} %fusion.62), channel_id=1, source_target_pairs={{0,1},{1,0},{2,3},{3,2},{4,5},{5,4},{6,7},{7,6},{8,9},{9,8},{10,11... | collective-permute-start | bytes 1572872 | tf_op jit(solution)/shard_map/ppermute | solution.py:24
  51.4 12.0 %collective-permute-start.6 = (bf16[2,1,2,512,128]{3,4,2,0,1:T(8,128)(2,1)S(1)}, bf16[2,1,2,512,128]{3,4,2,0,1:T(8,128)(2,1)S(1)}, u32[]{:S(2)}, u32[]{:S(2)}) collective-permute-start(bf16[2,1,2,512,128]{3,4,2,0,1:T(8,128)(2,1)S(1)} %fusion.59), channel_id=1, source_target_pairs={{0,8},{8,0},{16,24},{24,16},{1,9},{9,1},{17,25},{25,17},{2,10},{10... | collective-permute-start | bytes 1572872 | tf_op jit(solution)/shard_map/ppermute | solution.py:24
  61.2 20.4 %collective-permute-start.13 = (bf16[2,1,2,512,128]{3,4,2,0,1:T(8,128)(2,1)S(1)}, bf16[2,1,2,512,128]{3,4,2,0,1:T(8,128)(2,1)S(1)}, u32[]{:S(2)}, u32[]{:S(2)}) collective-permute-start(bf16[2,1,2,512,128]{3,4,2,0,1:T(8,128)(2,1)S(1)} %fusion.52), channel_id=1, source_target_pairs={{0,64},{32,96},{64,0},{96,32},{1,65},{33,97},{65,1},{97,33},{2,66}... | collective-permute-start | bytes 1572872 | tf_op jit(solution)/shard_map/ppermute | solution.py:24
  64.5 22.9 %collective-permute-start.7 = (bf16[2,1,2,512,128]{3,4,2,0,1:T(8,128)(2,1)S(1)}, bf16[2,1,2,512,128]{3,4,2,0,1:T(8,128)(2,1)S(1)}, u32[]{:S(2)}, u32[]{:S(2)}) collective-permute-start(bf16[2,1,2,512,128]{3,4,2,0,1:T(8,128)(2,1)S(1)} %fusion.58), channel_id=1, source_target_pairs={{0,1},{1,0},{2,3},{3,2},{4,5},{5,4},{6,7},{7,6},{8,9},{9,8},{10,11... | collective-permute-start | bytes 1572872 | tf_op jit(solution)/shard_map/ppermute | solution.py:24
  65.6 13.8 %collective-permute-start.10 = (bf16[2,1,2,512,128]{3,4,2,0,1:T(8,128)(2,1)S(1)}, bf16[2,1,2,512,128]{3,4,2,0,1:T(8,128)(2,1)S(1)}, u32[]{:S(2)}, u32[]{:S(2)}) collective-permute-start(bf16[2,1,2,512,128]{3,4,2,0,1:T(8,128)(2,1)S(1)} %fusion.55), channel_id=1, source_target_pairs={{0,8},{8,0},{16,24},{24,16},{1,9},{9,1},{17,25},{25,17},{2,10},{10... | collective-permute-start | bytes 1572872 | tf_op jit(solution)/shard_map/ppermute | solution.py:24
  69.1 58.7 %collective-permute-start.19 = (bf16[2,1,2,512,128]{3,4,2,0,1:T(8,128)(2,1)S(1)}, bf16[2,1,2,512,128]{3,4,2,0,1:T(8,128)(2,1)S(1)}, u32[]{:S(2)}, u32[]{:S(2)}) collective-permute-start(bf16[2,1,2,512,128]{3,4,2,0,1:T(8,128)(2,1)S(1)} %fusion.61), channel_id=1, source_target_pairs={{8,0},{16,8},{24,16},{9,1},{17,9},{25,17},{10,2},{18,10},{26,18},{... | collective-permute-start | bytes 1572872 | tf_op jit(solution)/shard_map/ppermute | solution.py:137
  80.5 20.5 %collective-permute-start.11 = (bf16[2,1,2,512,128]{3,4,2,0,1:T(8,128)(2,1)S(1)}, bf16[2,1,2,512,128]{3,4,2,0,1:T(8,128)(2,1)S(1)}, u32[]{:S(2)}, u32[]{:S(2)}) collective-permute-start(bf16[2,1,2,512,128]{3,4,2,0,1:T(8,128)(2,1)S(1)} %fusion.54), channel_id=1, source_target_pairs={{0,1},{1,0},{2,3},{3,2},{4,5},{5,4},{6,7},{7,6},{8,9},{9,8},{10,11... | collective-permute-start | bytes 1572872 | tf_op jit(solution)/shard_map/ppermute | solution.py:24
  82.7 15.5 %collective-permute-start.14 = (bf16[2,1,2,512,128]{3,4,2,0,1:T(8,128)(2,1)S(1)}, bf16[2,1,2,512,128]{3,4,2,0,1:T(8,128)(2,1)S(1)}, u32[]{:S(2)}, u32[]{:S(2)}) collective-permute-start(bf16[2,1,2,512,128]{3,4,2,0,1:T(8,128)(2,1)S(1)} %fusion.51), channel_id=1, source_target_pairs={{0,8},{8,0},{16,24},{24,16},{1,9},{9,1},{17,25},{25,17},{2,10},{10... | collective-permute-start | bytes 1572872 | tf_op jit(solution)/shard_map/ppermute | solution.py:24
  99.3 10.3 %collective-permute-start.15 = (bf16[2,1,2,512,128]{3,4,2,0,1:T(8,128)(2,1)S(1)}, bf16[2,1,2,512,128]{3,4,2,0,1:T(8,128)(2,1)S(1)}, u32[]{:S(2)}, u32[]{:S(2)}) collective-permute-start(bf16[2,1,2,512,128]{3,4,2,0,1:T(8,128)(2,1)S(1)} %fusion.50), channel_id=1, source_target_pairs={{0,1},{1,0},{2,3},{3,2},{4,5},{5,4},{6,7},{7,6},{8,9},{9,8},{10,11... | collective-permute-start | bytes 1572872 | tf_op jit(solution)/shard_map/ppermute | solution.py:24
  110.7 17.1 %collective-permute-start.18 = (bf16[2,1,2,512,128]{3,4,2,0,1:T(8,128)(2,1)S(1)}, bf16[2,1,2,512,128]{3,4,2,0,1:T(8,128)(2,1)S(1)}, u32[]{:S(2)}, u32[]{:S(2)}) collective-permute-start(bf16[2,1,2,512,128]{3,4,2,0,1:T(8,128)(2,1)S(1)} %fusion.49), channel_id=1, source_target_pairs={{0,8},{8,16},{16,24},{1,9},{9,17},{17,25},{2,10},{10,18},{18,26},{... | collective-permute-start | bytes 1572872 | tf_op jit(solution)/shard_map/ppermute | solution.py:132
  117.7 36.7 %collective-permute-start.17 = (bf16[1,4,2,512,128]{3,4,2,0,1:T(8,128)(2,1)S(1)}, bf16[1,4,2,512,128]{3,4,2,0,1:T(8,128)(2,1)S(1)}, u32[]{:S(2)}, u32[]{:S(2)}) collective-permute-start(bf16[1,4,2,512,128]{3,4,2,0,1:T(8,128)(2,1)S(1)} %get-tuple-element.49), channel_id=1, source_target_pairs={{32,0},{64,32},{96,64},{33,1},{65,33},{97,65},{34,2},{66,34},{98,6... | collective-permute-start | bytes 3145736 | tf_op jit(solution)/shard_map/ppermute | solution.py:137
  119.7 38.7 %collective-permute-start.16 = (bf16[1,4,2,512,128]{3,4,2,0,1:T(8,128)(2,1)S(1)}, bf16[1,4,2,512,128]{3,4,2,0,1:T(8,128)(2,1)}, u32[]{:S(2)}, u32[]{:S(2)}) collective-permute-start(bf16[1,4,2,512,128]{3,4,2,0,1:T(8,128)(2,1)S(1)} %get-tuple-element.50), channel_id=1, source_target_pairs={{0,32},{32,64},{64,96},{1,33},{33,65},{65,97},{2,34},{34,66},{66,9... | collective-permute-start | bytes 3145736 | tf_op jit(solution)/shard_map/ppermute | solution.py:132
  122.1 3.3 %collective-permute-start.20 = (bf16[2,4,1,512,128]{3,4,2,0,1:T(8,128)(2,1)S(1)}, bf16[2,4,1,512,128]{3,4,2,0,1:T(8,128)(2,1)S(1)}, u32[]{:S(2)}, u32[]{:S(2)}) collective-permute-start(bf16[2,4,1,512,128]{3,4,2,0,1:T(8,128)(2,1)S(1)} %constant_dynamic-slice_fusion), channel_id=1, source_target_pairs={{2,1},{4,3},{6,5},{1,2},{3,4},{5,6},{10,9},{12,11},{14,13},{9,10},... | collective-permute-start | bytes 3145736 | tf_op jit(solution)/shard_map/ppermute | solution.py:144
  127.8 30.6 %copy-start.5 = (bf16[2,1,2,512,128]{3,4,2,0,1:T(8,128)(2,1)}, bf16[2,1,2,512,128]{3,4,2,0,1:T(8,128)(2,1)S(1)}, u32[]{:S(2)}) copy-start(bf16[2,1,2,512,128]{3,4,2,0,1:T(8,128)(2,1)S(1)} %collective-permute-done.19) | copy-start | bytes 1572868
  127.8 30.6 %copy-start.6 = (bf16[2,1,2,512,128]{3,4,2,0,1:T(8,128)(2,1)}, bf16[2,1,2,512,128]{3,4,2,0,1:T(8,128)(2,1)S(1)}, u32[]{:S(2)}) copy-start(bf16[2,1,2,512,128]{3,4,2,0,1:T(8,128)(2,1)S(1)} %collective-permute-done.18) | copy-start | bytes 1572868
  154.4 3.9 %copy-start.4 = (bf16[1,4,2,512,128]{3,4,2,0,1:T(8,128)(2,1)}, bf16[1,4,2,512,128]{3,4,2,0,1:T(8,128)(2,1)S(1)}, u32[]{:S(2)}) copy-start(bf16[1,4,2,512,128]{3,4,2,0,1:T(8,128)(2,1)S(1)} %collective-permute-done.17) | copy-start | bytes 3145732

commit v4 on v3

--- a/solution.py
+++ b/solution.py
@@ -151,9 +151,7 @@
     last = pl.num_programs(0) - 1
 
     def coupled(block, index):
-        return lax.dot_general(
-            block, weight_ref[index], (((1,), (1,)), ((), ())), preferred_element_type=jnp.float32
-        )
+        return jnp.dot(block, weight_ref[index], preferred_element_type=jnp.float32)
 
     for x in range(2):
         for z in range(2):
@@ -194,7 +192,7 @@
         in_specs=specs,
         out_specs=pl.BlockSpec(leaf, lambda y: (y, 0, 0, 0, 0)),
         out_shape=jax.ShapeDtypeStruct((ly, lx, lz, cols, cheb), jnp.bfloat16),
-    )(coupling, cells_t, cells_t, cells_t, turned(xb), turned(xa), turned(yb), turned(ya), turned(zb), turned(za))
+    )(jnp.swapaxes(coupling, 1, 2), cells_t, cells_t, cells_t, turned(xb), turned(xa), turned(yb), turned(ya), turned(zb), turned(za))
     return out.reshape(ly * lx * lz, cols, cheb)
 
 

time: 188 us -> 189 us (level)
  Pallas kernels: 29 us -> 19.8 us
  local copies, waits for them, and re-layouts: 10.5 us -> 18 us
  waiting for transfers between devices: 77.4 us -> 79.9 us
    ppermute x2, waiting for transfers between devices: 26.6 us -> 0.01 us  [from_above(): return lax.ppermute(slab, axis, [(i + 1, i) for i in range(count - 1)])]
    ppermute x2, waiting for transfers between devices: 3.93 us -> 28.1 us  [from_below(): return lax.ppermute(slab, axis, [(i, i + 1) for i in range(count - 1)])]
    pallas_call x1, Pallas kernels: 20.8 us -> 11.6 us  [couple(): pl.pallas_call(coupling_kernel, grid=(ly,), in_specs=specs, out_specs=pl....]
    unnamed x15 -> x16, local copies, waits for them, and re-layouts: 1.14 us -> 6.87 us
    ppermute x16, waiting for transfers between devices: 46.8 us -> 51.9 us  [from_partner(): lax.ppermute(shard, axis, [(i, i ^ 1 << apart) for i in range(lax.axis_si...]
    ppermute x2, starting transfers between devices: 4.36 us -> 7.04 us  [from_above(): return lax.ppermute(slab, axis, [(i + 1, i) for i in range(count - 1)])]
    ppermute x16, starting transfers between devices: 14.2 us -> 11.8 us  [from_partner(): lax.ppermute(shard, axis, [(i, i ^ 1 << apart) for i in range(lax.axis_si...]
  transfers between devices with their start and end apart: 21 -> 21, of which waited for: 9 -> 10; matrix products, arithmetic and copies ran while one was open for 25% -> 28% of each run, Pallas kernels for 0% -> 0%
where the time goes in v4:
time: 189 us; the launch traced here: 188 us
  waiting for transfers between devices  79.9 us (42%)
  matrix products  39.3 us (21%)
  starting transfers between devices  26.5 us (14%)
  Pallas kernels  19.8 us (10%)
  local copies, waits for them, and re-layouts  18 us (10%)
  other arithmetic  3.67 us (2%)
    ppermute x16, waiting for transfers between devices, from_partner(): lax.ppermute(shard, axis, [(i, i ^ 1 << apart) for i in range(lax.axis_si...  51.9 us
    dot_general x68, matrix products, apply_map(): jnp.einsum('jk,...kc->...jc', weights, block, preferred_element_type=jnp....  39.3 us
    ppermute x2, waiting for transfers between devices, from_below(): return lax.ppermute(slab, axis, [(i, i + 1) for i in range(count - 1)])  28.1 us
    ppermute x16, starting transfers between devices, from_partner(): lax.ppermute(shard, axis, [(i, i ^ 1 << apart) for i in range(lax.axis_si...  11.8 us
    pallas_call x1, Pallas kernels, couple(): pl.pallas_call(coupling_kernel, grid=(ly,), in_specs=specs, out_specs=pl....  11.6 us
    pallas_call x1, Pallas kernels, sample(): pl.pallas_call(sample_kernel, grid_spec=spec, out_shape=jax.ShapeDtypeStr...  8.26 us
    ppermute x2, starting transfers between devices, from_above(): return lax.ppermute(slab, axis, [(i + 1, i) for i in range(count - 1)])  7.04 us
    ppermute x2, starting transfers between devices, from_below(): return lax.ppermute(slab, axis, [(i, i + 1) for i in range(count - 1)])  6.95 us
  transfers between devices with their start and end apart: 21, of which 10 were waited for; matrix products, arithmetic and copies ran while one was open for 28% of the time, Pallas kernels for 0%

profile of v4, /device:TPU:34, one launch (start us, length us, event | category | flops | bytes accessed | tf_op | source)
XLA Modules:
  0.0 188.1 jit_solution(14937517440863414621)
XLA Ops:
  0.0 2.5 %fusion.211 = (bf16[2,1,2,512,128]{4,3,2,1,0:T(8,128)(2,1)S(1)}, bf16[2,1,2,512,128]{4,3,2,1,0:T(8,128)(2,1)S(1)}, bf16[2,1,2,512,128]{4,3,2,1,0:T(8,128)(2,1)S(1)}, bf16[2,1,2,512,128]{4,3,2,1,0:T(8,128)(2,1)}) fusion(bf16[2,4,2,512,128]{4,3,2,1,0:T(8,128)(2,1)} %param.6), kind=kLoop, calls=%fused_computation.292 | loop fusion | bytes 4194304 | tf_op jit(solution)/shard_map/slice | solution.py:104
  2.5 1.1 copy.44
  3.6 5.7 %slice_bitcast_fusion = (bf16[2,2,512,512]{3,2,1,0:T(8,128)(2,1)}, bf16[2,2,512,512]{3,2,1,0:T(8,128)(2,1)}, bf16[2,2,512,512]{3,2,1,0:T(8,128)(2,1)}, bf16[2,2,512,512]{3,2,1,0:T(8,128)(2,1)S(1)}) fusion(bf16[4,2,2,512,512]{4,3,2,1,0:T(8,128)(2,1)} %param.7), kind=kLoop, calls=%fused_computation.4 | loop fusion | bytes 16777216 | tf_op jit(solution)/shard_map/squeeze | solution.py:121
  9.3 1.0 copy.45
  10.5 1.2 copy.47
  11.8 4.7 %copy.7 = bf16[6,512,512]{1,2,0:T(8,128)(2,1)} copy(bf16[6,512,512]{2,1,0:T(8,128)(2,1)} %param.8) | data formatting | bytes 6291456 | tf_op args[2]
  16.5 1.8 fusion.65
  18.4 1.5 fusion.67
  19.9 1.5 fusion.31
  21.6 1.7 fusion.64
  25.8 11.8 %collective-permute-done.1 = bf16[2,1,2,512,128]{3,4,2,0,1:T(8,128)(2,1)S(1)} collective-permute-done((bf16[2,1,2,512,128]{3,4,2,0,1:T(8,128)(2,1)S(1)}, bf16[2,1,2,512,128]{3,4,2,0,1:T(8,128)(2,1)S(1)}, u32[]{:S(2)}, u32[]{:S(2)}) %collective-permute-start.1) | collective-permute-done | bytes 524320 | tf_op jit(solution)/shard_map/ppermute | solution.py:24
  38.7 0.6 collective-permute-start.2
  43.7 8.6 %collective-permute-done.2 = bf16[2,1,2,512,128]{3,4,2,0,1:T(8,128)(2,1)S(1)} collective-permute-done((bf16[2,1,2,512,128]{3,4,2,0,1:T(8,128)(2,1)S(1)}, bf16[2,1,2,512,128]{3,4,2,0,1:T(8,128)(2,1)S(1)}, u32[]{:S(2)}, u32[]{:S(2)}) %collective-permute-start.2) | collective-permute-done | bytes 524320 | tf_op jit(solution)/shard_map/ppermute | solution.py:24
  52.8 2.2 %collective-permute-done.5 = bf16[2,1,2,512,128]{3,4,2,0,1:T(8,128)(2,1)S(1)} collective-permute-done((bf16[2,1,2,512,128]{3,4,2,0,1:T(8,128)(2,1)S(1)}, bf16[2,1,2,512,128]{3,4,2,0,1:T(8,128)(2,1)S(1)}, u32[]{:S(2)}, u32[]{:S(2)}) %collective-permute-start.5) | collective-permute-done | bytes 524320 | tf_op jit(solution)/shard_map/ppermute | solution.py:24
  56.6 1.7 collective-permute-start.6
  59.9 0.5 fusion.56
  60.9 0.5 collective-permute-start.9
  62.9 1.7 collective-permute-start.3
  65.6 3.7 %collective-permute-done.6 = bf16[2,1,2,512,128]{3,4,2,0,1:T(8,128)(2,1)S(1)} collective-permute-done((bf16[2,1,2,512,128]{3,4,2,0,1:T(8,128)(2,1)S(1)}, bf16[2,1,2,512,128]{3,4,2,0,1:T(8,128)(2,1)S(1)}, u32[]{:S(2)}, u32[]{:S(2)}) %collective-permute-start.6) | collective-permute-done | bytes 524320 | tf_op jit(solution)/shard_map/ppermute | solution.py:24
  69.8 3.2 %collective-permute-done.9 = bf16[2,1,2,512,128]{3,4,2,0,1:T(8,128)(2,1)S(1)} collective-permute-done((bf16[2,1,2,512,128]{3,4,2,0,1:T(8,128)(2,1)S(1)}, bf16[2,1,2,512,128]{3,4,2,0,1:T(8,128)(2,1)S(1)}, u32[]{:S(2)}, u32[]{:S(2)}) %collective-permute-start.9) | collective-permute-done | bytes 524320 | tf_op jit(solution)/shard_map/ppermute | solution.py:24
  73.6 0.5 fusion.58
  74.1 1.7 collective-permute-start.7
  76.2 0.6 collective-permute-start.10
  78.9 0.7 collective-permute-start.13
  82.1 3.4 %collective-permute-start.19 = (bf16[2,1,2,512,128]{3,4,2,0,1:T(8,128)(2,1)S(1)}, bf16[2,1,2,512,128]{3,4,2,0,1:T(8,128)(2,1)S(1)}, u32[]{:S(2)}, u32[]{:S(2)}) collective-permute-start(bf16[2,1,2,512,128]{3,4,2,0,1:T(8,128)(2,1)S(1)} %fusion.61), channel_id=1, source_target_pairs={{8,0},{16,8},{24,16},{9,1},{17,9},{25,17},{10,2},{18,10},{26,18},{... | collective-permute-start | bytes 1572872 | tf_op jit(solution)/shard_map/ppermute | solution.py:137
  86.0 2.3 %collective-permute-done.10 = bf16[2,1,2,512,128]{3,4,2,0,1:T(8,128)(2,1)S(1)} collective-permute-done((bf16[2,1,2,512,128]{3,4,2,0,1:T(8,128)(2,1)S(1)}, bf16[2,1,2,512,128]{3,4,2,0,1:T(8,128)(2,1)S(1)}, u32[]{:S(2)}, u32[]{:S(2)}) %collective-permute-start.10) | collective-permute-done | bytes 524320 | tf_op jit(solution)/shard_map/ppermute | solution.py:24
  88.9 0.7 collective-permute-done.13
  90.7 0.5 fusion.51
  91.7 1.8 collective-permute-start.14
  94.0 0.8 collective-permute-start.11
  96.8 11.0 %collective-permute-done.14 = bf16[2,1,2,512,128]{3,4,2,0,1:T(8,128)(2,1)S(1)} collective-permute-done((bf16[2,1,2,512,128]{3,4,2,0,1:T(8,128)(2,1)S(1)}, bf16[2,1,2,512,128]{3,4,2,0,1:T(8,128)(2,1)S(1)}, u32[]{:S(2)}, u32[]{:S(2)}) %collective-permute-start.14) | collective-permute-done | bytes 524320 | tf_op jit(solution)/shard_map/ppermute | solution.py:24
  108.8 0.5 collective-permute-start.15
  111.0 0.5 fusion.53
  111.5 8.4 %collective-permute-done.15 = bf16[2,1,2,512,128]{3,4,2,0,1:T(8,128)(2,1)S(1)} collective-permute-done((bf16[2,1,2,512,128]{3,4,2,0,1:T(8,128)(2,1)S(1)}, bf16[2,1,2,512,128]{3,4,2,0,1:T(8,128)(2,1)S(1)}, u32[]{:S(2)}, u32[]{:S(2)}) %collective-permute-start.15) | collective-permute-done | bytes 524320 | tf_op jit(solution)/shard_map/ppermute | solution.py:24
  120.5 0.5 fusion.49
  121.0 1.7 pad_maximum_fusion
  122.9 5.0 %collective-permute-start.18 = (bf16[2,1,2,512,128]{3,4,2,0,1:T(8,128)(2,1)S(1)}, bf16[2,1,2,512,128]{3,4,2,0,1:T(8,128)(2,1)S(1)}, u32[]{:S(2)}, u32[]{:S(2)}) collective-permute-start(bf16[2,1,2,512,128]{3,4,2,0,1:T(8,128)(2,1)S(1)} %fusion.49), channel_id=1, source_target_pairs={{0,8},{8,16},{16,24},{1,9},{9,17},{17,25},{2,10},{10,18},{18,26},{... | collective-permute-start | bytes 1572872 | tf_op jit(solution)/shard_map/ppermute | solution.py:132
  127.9 0.7 collective-permute-start.20
  128.7 1.9 %collective-permute-start.16 = (bf16[1,4,2,512,128]{3,4,2,0,1:T(8,128)(2,1)S(1)}, bf16[1,4,2,512,128]{3,4,2,0,1:T(8,128)(2,1)S(1)}, u32[]{:S(2)}, u32[]{:S(2)}) collective-permute-start(bf16[1,4,2,512,128]{3,4,2,0,1:T(8,128)(2,1)S(1)} %get-tuple-element.50), channel_id=1, source_target_pairs={{0,32},{32,64},{64,96},{1,33},{33,65},{65,97},{2,34},{34,66},{66,9... | collective-permute-start | bytes 3145736 | tf_op jit(solution)/shard_map/ppermute | solution.py:132
  130.6 3.6 %collective-permute-start.17 = (bf16[1,4,2,512,128]{3,4,2,0,1:T(8,128)(2,1)S(1)}, bf16[1,4,2,512,128]{3,4,2,0,1:T(8,128)(2,1)}, u32[]{:S(2)}, u32[]{:S(2)}) collective-permute-start(bf16[1,4,2,512,128]{3,4,2,0,1:T(8,128)(2,1)S(1)} %get-tuple-element.49), channel_id=1, source_target_pairs={{32,0},{64,32},{96,64},{33,1},{65,33},{97,65},{34,2},{66,34},{98,6... | collective-permute-start | bytes 3145736 | tf_op jit(solution)/shard_map/ppermute | solution.py:137
  134.3 0.7 fusion.128
  135.0 0.8 add_bitcast_fusion
  136.1 0.7 fusion.143
  136.8 2.4 %select_bitcast_fusion = (bf16[4,2,1,128,512]{4,3,2,1,0:T(8,128)(2,1)}, bf16[4,2,1,128,512]{4,3,2,1,0:T(8,128)(2,1)}) fusion(bf16[2,4,1,512,128]{3,4,2,0,1:T(8,128)(2,1)S(1)} %collective-permute-done.20, pred[]{:T(512)S(6)} %eq.6, f32[2,4,1,512,64]{3,4,2,0,1:T(8,128)S(1)} %get-tuple-element.48, f32[2,4,1,512,64]{3,4,2,0,1:T(8,128)S(1)} %get-tuple-element.47, ...), kind=kOutput, calls=%fused_computation.107 | convolution fusion | flops 541589504 | bytes 8912897 | tf_op jit(solution)/shard_map/jk,...kc->...jc/dot_general | solution.py:33
  139.2 28.1 %collective-permute-done.16 = bf16[1,4,2,512,128]{3,4,2,0,1:T(8,128)(2,1)S(1)} collective-permute-done((bf16[1,4,2,512,128]{3,4,2,0,1:T(8,128)(2,1)S(1)}, bf16[1,4,2,512,128]{3,4,2,0,1:T(8,128)(2,1)S(1)}, u32[]{:S(2)}, u32[]{:S(2)}) %collective-permute-start.16) | collective-permute-done | bytes 1048608 | tf_op jit(solution)/shard_map/ppermute | solution.py:132
  167.3 1.0 copy-done.4
  168.2 11.6 %shard_map.64 = bf16[4,2,2,128,512]{4,3,2,1,0:T(8,128)(2,1)} custom-call(bf16[6,512,512]{2,1,0:T(8,128)(2,1)} %bitcast.576, bf16[4,2,2,128,512]{4,3,2,1,0:T(8,128)(2,1)} %get-tuple-element.52.prev_ref.cell_ref.next_ref, bf16[4,2,2,128,512]{4,3,2,1,0:T(8,128)(2,1)} %get-tuple-element.52.prev_ref.cell_ref.next_ref, ...), custom_call_target="tpu_custom_call" | custom-call | tf_op jit(solution)/shard_map/pallas_call | solution.py:189
  179.8 8.3 %shard_map.65 = bf16[8192,128]{1,0:T(8,128)(2,1)} custom-call(s32[64]{0:T(128)} %leaf_ref.1, s32[64]{0:T(128)} %count_ref.1, f32[3,8192]{1,0:T(4,128)} %pos_ref.1, bf16[16,128,512]{2,1,0:T(8,128)(2,1)} %bitcast.577), custom_call_target="tpu_custom_call" | custom-call | tf_op jit(solution)/shard_map/pallas_call | solution.py:93
  (113 shorter events, 29.7 us)
Async XLA Ops:
  3.6 16.3 %collective-permute-start = (bf16[2,1,2,512,128]{3,4,2,0,1:T(8,128)(2,1)}, bf16[2,1,2,512,128]{3,4,2,0,1:T(8,128)(2,1)}, u32[]{:S(2)}, u32[]{:S(2)}) collective-permute-start(bf16[2,1,2,512,128]{3,4,2,0,1:T(8,128)(2,1)} %copy.44), channel_id=1, source_target_pairs={{0,32},{32,0},{64,96},{96,64},{1,33},{33,1},{65,97},{97,65},{2,34}... | collective-permute-start | bytes 1572872 | tf_op jit(solution)/shard_map/ppermute | solution.py:24
  16.5 1.9 %copy-start.1 = (bf16[2,2,512,512]{3,2,1,0:T(8,128)(2,1)S(1)}, bf16[2,2,512,512]{3,2,1,0:T(8,128)(2,1)}, u32[]{:S(2)}) copy-start(bf16[2,2,512,512]{3,2,1,0:T(8,128)(2,1)} %get-tuple-element.43) | copy-start | bytes 6291460
  21.5 1.9 copy-start
  23.2 14.4 %collective-permute-start.1 = (bf16[2,1,2,512,128]{3,4,2,0,1:T(8,128)(2,1)S(1)}, bf16[2,1,2,512,128]{3,4,2,0,1:T(8,128)(2,1)S(1)}, u32[]{:S(2)}, u32[]{:S(2)}) collective-permute-start(bf16[2,1,2,512,128]{3,4,2,0,1:T(8,128)(2,1)S(1)} %fusion.64), channel_id=1, source_target_pairs={{0,64},{32,96},{64,0},{96,32},{1,65},{33,97},{65,1},{97,33},{2,66}... | collective-permute-start | bytes 1572872 | tf_op jit(solution)/shard_map/ppermute | solution.py:24
  23.4 1.0 copy-start.3
  24.5 15.8 %collective-permute-start.4 = (bf16[2,1,2,512,128]{3,4,2,0,1:T(8,128)(2,1)S(1)}, bf16[2,1,2,512,128]{3,4,2,0,1:T(8,128)(2,1)S(1)}, u32[]{:S(2)}, u32[]{:S(2)}) collective-permute-start(bf16[2,1,2,512,128]{3,4,2,0,1:T(8,128)(2,1)S(1)} %copy-done.3), channel_id=1, source_target_pairs={{0,32},{32,0},{64,96},{96,64},{1,33},{33,1},{65,97},{97,65},{2,34}... | collective-permute-start | bytes 1572872 | tf_op jit(solution)/shard_map/ppermute | solution.py:24
  38.7 13.5 %collective-permute-start.2 = (bf16[2,1,2,512,128]{3,4,2,0,1:T(8,128)(2,1)S(1)}, bf16[2,1,2,512,128]{3,4,2,0,1:T(8,128)(2,1)S(1)}, u32[]{:S(2)}, u32[]{:S(2)}) collective-permute-start(bf16[2,1,2,512,128]{3,4,2,0,1:T(8,128)(2,1)S(1)} %fusion.63), channel_id=1, source_target_pairs={{0,8},{8,0},{16,24},{24,16},{1,9},{9,1},{17,25},{25,17},{2,10},{10... | collective-permute-start | bytes 1572872 | tf_op jit(solution)/shard_map/ppermute | solution.py:24
  41.8 13.3 %collective-permute-start.5 = (bf16[2,1,2,512,128]{3,4,2,0,1:T(8,128)(2,1)S(1)}, bf16[2,1,2,512,128]{3,4,2,0,1:T(8,128)(2,1)S(1)}, u32[]{:S(2)}, u32[]{:S(2)}) collective-permute-start(bf16[2,1,2,512,128]{3,4,2,0,1:T(8,128)(2,1)S(1)} %fusion.60), channel_id=1, source_target_pairs={{0,64},{32,96},{64,0},{96,32},{1,65},{33,97},{65,1},{97,33},{2,66}... | collective-permute-start | bytes 1572872 | tf_op jit(solution)/shard_map/ppermute | solution.py:24
  42.6 16.7 %collective-permute-start.8 = (bf16[2,1,2,512,128]{3,4,2,0,1:T(8,128)(2,1)S(1)}, bf16[2,1,2,512,128]{3,4,2,0,1:T(8,128)(2,1)S(1)}, u32[]{:S(2)}, u32[]{:S(2)}) collective-permute-start(bf16[2,1,2,512,128]{3,4,2,0,1:T(8,128)(2,1)S(1)} %copy.46), channel_id=1, source_target_pairs={{0,32},{32,0},{64,96},{96,64},{1,33},{33,1},{65,97},{97,65},{2,34}... | collective-permute-start | bytes 1572872 | tf_op jit(solution)/shard_map/ppermute | solution.py:24
  56.6 12.6 %collective-permute-start.6 = (bf16[2,1,2,512,128]{3,4,2,0,1:T(8,128)(2,1)S(1)}, bf16[2,1,2,512,128]{3,4,2,0,1:T(8,128)(2,1)S(1)}, u32[]{:S(2)}, u32[]{:S(2)}) collective-permute-start(bf16[2,1,2,512,128]{3,4,2,0,1:T(8,128)(2,1)S(1)} %fusion.59), channel_id=1, source_target_pairs={{0,8},{8,0},{16,24},{24,16},{1,9},{9,1},{17,25},{25,17},{2,10},{10... | collective-permute-start | bytes 1572872 | tf_op jit(solution)/shard_map/ppermute | solution.py:24
  60.9 12.1 %collective-permute-start.9 = (bf16[2,1,2,512,128]{3,4,2,0,1:T(8,128)(2,1)S(1)}, bf16[2,1,2,512,128]{3,4,2,0,1:T(8,128)(2,1)S(1)}, u32[]{:S(2)}, u32[]{:S(2)}) collective-permute-start(bf16[2,1,2,512,128]{3,4,2,0,1:T(8,128)(2,1)S(1)} %fusion.56), channel_id=1, source_target_pairs={{0,64},{32,96},{64,0},{96,32},{1,65},{33,97},{65,1},{97,33},{2,66}... | collective-permute-start | bytes 1572872 | tf_op jit(solution)/shard_map/ppermute | solution.py:24
  61.9 2.7 %copy-start.2 = (bf16[2,2,512,512]{3,2,1,0:T(8,128)(2,1)S(1)}, bf16[2,2,512,512]{3,2,1,0:T(8,128)(2,1)}, u32[]{:S(2)}) copy-start(bf16[2,2,512,512]{3,2,1,0:T(8,128)(2,1)} %get-tuple-element.41) | copy-start | bytes 6291460
  62.4 15.4 %collective-permute-start.12 = (bf16[2,1,2,512,128]{3,4,2,0,1:T(8,128)(2,1)S(1)}, bf16[2,1,2,512,128]{3,4,2,0,1:T(8,128)(2,1)S(1)}, u32[]{:S(2)}, u32[]{:S(2)}) collective-permute-start(bf16[2,1,2,512,128]{3,4,2,0,1:T(8,128)(2,1)S(1)} %copy.47), channel_id=1, source_target_pairs={{0,32},{32,0},{64,96},{96,64},{1,33},{33,1},{65,97},{97,65},{2,34}... | collective-permute-start | bytes 1572872 | tf_op jit(solution)/shard_map/ppermute | solution.py:24
  62.9 17.6 %collective-permute-start.3 = (bf16[2,1,2,512,128]{3,4,2,0,1:T(8,128)(2,1)S(1)}, bf16[2,1,2,512,128]{3,4,2,0,1:T(8,128)(2,1)S(1)}, u32[]{:S(2)}, u32[]{:S(2)}) collective-permute-start(bf16[2,1,2,512,128]{3,4,2,0,1:T(8,128)(2,1)S(1)} %fusion.62), channel_id=1, source_target_pairs={{0,1},{1,0},{2,3},{3,2},{4,5},{5,4},{6,7},{7,6},{8,9},{9,8},{10,11... | collective-permute-start | bytes 1572872 | tf_op jit(solution)/shard_map/ppermute | solution.py:24
  74.1 21.6 %collective-permute-start.7 = (bf16[2,1,2,512,128]{3,4,2,0,1:T(8,128)(2,1)S(1)}, bf16[2,1,2,512,128]{3,4,2,0,1:T(8,128)(2,1)S(1)}, u32[]{:S(2)}, u32[]{:S(2)}) collective-permute-start(bf16[2,1,2,512,128]{3,4,2,0,1:T(8,128)(2,1)S(1)} %fusion.58), channel_id=1, source_target_pairs={{0,1},{1,0},{2,3},{3,2},{4,5},{5,4},{6,7},{7,6},{8,9},{9,8},{10,11... | collective-permute-start | bytes 1572872 | tf_op jit(solution)/shard_map/ppermute | solution.py:24
  76.2 12.1 %collective-permute-start.10 = (bf16[2,1,2,512,128]{3,4,2,0,1:T(8,128)(2,1)S(1)}, bf16[2,1,2,512,128]{3,4,2,0,1:T(8,128)(2,1)S(1)}, u32[]{:S(2)}, u32[]{:S(2)}) collective-permute-start(bf16[2,1,2,512,128]{3,4,2,0,1:T(8,128)(2,1)S(1)} %fusion.55), channel_id=1, source_target_pairs={{0,8},{8,0},{16,24},{24,16},{1,9},{9,1},{17,25},{25,17},{2,10},{10... | collective-permute-start | bytes 1572872 | tf_op jit(solution)/shard_map/ppermute | solution.py:24
  78.9 10.7 %collective-permute-start.13 = (bf16[2,1,2,512,128]{3,4,2,0,1:T(8,128)(2,1)S(1)}, bf16[2,1,2,512,128]{3,4,2,0,1:T(8,128)(2,1)S(1)}, u32[]{:S(2)}, u32[]{:S(2)}) collective-permute-start(bf16[2,1,2,512,128]{3,4,2,0,1:T(8,128)(2,1)S(1)} %fusion.52), channel_id=1, source_target_pairs={{0,64},{32,96},{64,0},{96,32},{1,65},{33,97},{65,1},{97,33},{2,66}... | collective-permute-start | bytes 1572872 | tf_op jit(solution)/shard_map/ppermute | solution.py:24
  82.1 57.1 %collective-permute-start.19 = (bf16[2,1,2,512,128]{3,4,2,0,1:T(8,128)(2,1)S(1)}, bf16[2,1,2,512,128]{3,4,2,0,1:T(8,128)(2,1)S(1)}, u32[]{:S(2)}, u32[]{:S(2)}) collective-permute-start(bf16[2,1,2,512,128]{3,4,2,0,1:T(8,128)(2,1)S(1)} %fusion.61), channel_id=1, source_target_pairs={{8,0},{16,8},{24,16},{9,1},{17,9},{25,17},{10,2},{18,10},{26,18},{... | collective-permute-start | bytes 1572872 | tf_op jit(solution)/shard_map/ppermute | solution.py:137
  91.7 16.1 %collective-permute-start.14 = (bf16[2,1,2,512,128]{3,4,2,0,1:T(8,128)(2,1)S(1)}, bf16[2,1,2,512,128]{3,4,2,0,1:T(8,128)(2,1)S(1)}, u32[]{:S(2)}, u32[]{:S(2)}) collective-permute-start(bf16[2,1,2,512,128]{3,4,2,0,1:T(8,128)(2,1)S(1)} %fusion.51), channel_id=1, source_target_pairs={{0,8},{8,0},{16,24},{24,16},{1,9},{9,1},{17,25},{25,17},{2,10},{10... | collective-permute-start | bytes 1572872 | tf_op jit(solution)/shard_map/ppermute | solution.py:24
  94.0 16.4 %collective-permute-start.11 = (bf16[2,1,2,512,128]{3,4,2,0,1:T(8,128)(2,1)S(1)}, bf16[2,1,2,512,128]{3,4,2,0,1:T(8,128)(2,1)S(1)}, u32[]{:S(2)}, u32[]{:S(2)}) collective-permute-start(bf16[2,1,2,512,128]{3,4,2,0,1:T(8,128)(2,1)S(1)} %fusion.54), channel_id=1, source_target_pairs={{0,1},{1,0},{2,3},{3,2},{4,5},{5,4},{6,7},{7,6},{8,9},{9,8},{10,11... | collective-permute-start | bytes 1572872 | tf_op jit(solution)/shard_map/ppermute | solution.py:24
  108.8 11.0 %collective-permute-start.15 = (bf16[2,1,2,512,128]{3,4,2,0,1:T(8,128)(2,1)S(1)}, bf16[2,1,2,512,128]{3,4,2,0,1:T(8,128)(2,1)S(1)}, u32[]{:S(2)}, u32[]{:S(2)}) collective-permute-start(bf16[2,1,2,512,128]{3,4,2,0,1:T(8,128)(2,1)S(1)} %fusion.50), channel_id=1, source_target_pairs={{0,1},{1,0},{2,3},{3,2},{4,5},{5,4},{6,7},{7,6},{8,9},{9,8},{10,11... | collective-permute-start | bytes 1572872 | tf_op jit(solution)/shard_map/ppermute | solution.py:24
  122.9 16.3 %collective-permute-start.18 = (bf16[2,1,2,512,128]{3,4,2,0,1:T(8,128)(2,1)S(1)}, bf16[2,1,2,512,128]{3,4,2,0,1:T(8,128)(2,1)S(1)}, u32[]{:S(2)}, u32[]{:S(2)}) collective-permute-start(bf16[2,1,2,512,128]{3,4,2,0,1:T(8,128)(2,1)S(1)} %fusion.49), channel_id=1, source_target_pairs={{0,8},{8,16},{16,24},{1,9},{9,17},{17,25},{2,10},{10,18},{18,26},{... | collective-permute-start | bytes 1572872 | tf_op jit(solution)/shard_map/ppermute | solution.py:132
  127.9 8.9 %collective-permute-start.20 = (bf16[2,4,1,512,128]{3,4,2,0,1:T(8,128)(2,1)S(1)}, bf16[2,4,1,512,128]{3,4,2,0,1:T(8,128)(2,1)S(1)}, u32[]{:S(2)}, u32[]{:S(2)}) collective-permute-start(bf16[2,4,1,512,128]{3,4,2,0,1:T(8,128)(2,1)S(1)} %constant_dynamic-slice_fusion), channel_id=1, source_target_pairs={{2,1},{4,3},{6,5},{1,2},{3,4},{5,6},{10,9},{12,11},{14,13},{9,10},... | collective-permute-start | bytes 3145736 | tf_op jit(solution)/shard_map/ppermute | solution.py:144
  128.7 38.6 %collective-permute-start.16 = (bf16[1,4,2,512,128]{3,4,2,0,1:T(8,128)(2,1)S(1)}, bf16[1,4,2,512,128]{3,4,2,0,1:T(8,128)(2,1)S(1)}, u32[]{:S(2)}, u32[]{:S(2)}) collective-permute-start(bf16[1,4,2,512,128]{3,4,2,0,1:T(8,128)(2,1)S(1)} %get-tuple-element.50), channel_id=1, source_target_pairs={{0,32},{32,64},{64,96},{1,33},{33,65},{65,97},{2,34},{34,66},{66,9... | collective-permute-start | bytes 3145736 | tf_op jit(solution)/shard_map/ppermute | solution.py:132
  130.6 36.7 %collective-permute-start.17 = (bf16[1,4,2,512,128]{3,4,2,0,1:T(8,128)(2,1)S(1)}, bf16[1,4,2,512,128]{3,4,2,0,1:T(8,128)(2,1)}, u32[]{:S(2)}, u32[]{:S(2)}) collective-permute-start(bf16[1,4,2,512,128]{3,4,2,0,1:T(8,128)(2,1)S(1)} %get-tuple-element.49), channel_id=1, source_target_pairs={{32,0},{64,32},{96,64},{33,1},{65,33},{97,65},{34,2},{66,34},{98,6... | collective-permute-start | bytes 3145736 | tf_op jit(solution)/shard_map/ppermute | solution.py:137
  139.2 28.1 %copy-start.5 = (bf16[2,1,2,512,128]{3,4,2,0,1:T(8,128)(2,1)}, bf16[2,1,2,512,128]{3,4,2,0,1:T(8,128)(2,1)S(1)}, u32[]{:S(2)}) copy-start(bf16[2,1,2,512,128]{3,4,2,0,1:T(8,128)(2,1)S(1)} %collective-permute-done.19) | copy-start | bytes 1572868
  139.2 28.1 %copy-start.6 = (bf16[2,1,2,512,128]{3,4,2,0,1:T(8,128)(2,1)}, bf16[2,1,2,512,128]{3,4,2,0,1:T(8,128)(2,1)S(1)}, u32[]{:S(2)}) copy-start(bf16[2,1,2,512,128]{3,4,2,0,1:T(8,128)(2,1)S(1)} %collective-permute-done.18) | copy-start | bytes 1572868
  167.3 1.0 copy-start.4

commit v5 on v4

--- a/solution.py
+++ b/solution.py
@@ -100,7 +100,7 @@
 LEVEL_PLAN = (("gx", 0), ("gx", 1), ("gy", 0), ("gz", 0))
 
 
-def pipelined(coefficients, level_weights, chunks):
+def pipelined(coefficients, level_weights, chunks, late):
     cells = [coefficients[:, k:k + 1] for k in range(chunks)]
     partner_faces = [None] * chunks
     levels = len(LEVEL_PLAN)
@@ -113,6 +113,8 @@
                 ready[k], _ = lax.optimization_barrier((cells[k], cells[k - 1]))
             else:
                 ready[k] = cells[k]
+        if tick == chunks + levels - 2:
+            late, _ = lax.optimization_barrier((late, ready[active[-1]]))
         for k in active:
             level = tick - k
             axis, bit = LEVEL_PLAN[level]
@@ -124,7 +126,7 @@
                     lax.dynamic_slice_in_dim(other, side, 1, axis=2),
                     lax.dynamic_slice_in_dim(block, side, 1, axis=2),
                 )
-    return cells, partner_faces
+    return cells, partner_faces, late
 
 
 def from_below(slab, axis):
@@ -192,13 +194,14 @@
         in_specs=specs,
         out_specs=pl.BlockSpec(leaf, lambda y: (y, 0, 0, 0, 0)),
         out_shape=jax.ShapeDtypeStruct((ly, lx, lz, cols, cheb), jnp.bfloat16),
-    )(jnp.swapaxes(coupling, 1, 2), cells_t, cells_t, cells_t, turned(xb), turned(xa), turned(yb), turned(ya), turned(zb), turned(za))
+    )(coupling, cells_t, cells_t, cells_t, turned(xb), turned(xa), turned(yb), turned(ya), turned(zb), turned(za))
     return out.reshape(ly * lx * lz, cols, cheb)
 
 
 def local(coefficients, level_weights, coupling, positions, block_leaf, block_count):
     chunks = coefficients.shape[1]
-    done, partner_slabs = pipelined(coefficients, level_weights, chunks)
+    done, partner_slabs, coupling = pipelined(coefficients, level_weights, chunks, coupling)
+    coupling_t = jnp.swapaxes(coupling, 1, 2)
     done[-1], partner_slabs = lax.optimization_barrier((done[-1], partner_slabs))
     cells = jnp.concatenate(done, axis=1)
     partner_face = mix(
@@ -211,7 +214,7 @@
     yb = from_below(cells[:, cells.shape[1] - 1:], "gy")
     ya = from_above(cells[:, :1], "gy")
     zb, za = z_faces(cells, partner_face)
-    leaf_grid = couple(coupling, cells, xb, xa, yb, ya, zb, za)
+    leaf_grid = couple(coupling_t, cells, xb, xa, yb, ya, zb, za)
     return sample(leaf_grid, positions, block_leaf, block_count)
 
 

time: 189 us -> 185 us (0.979)
  waiting for transfers between devices: 79.9 us -> 64.3 us
  matrix products: 39.3 us -> 46.9 us
  local copies, waits for them, and re-layouts: 18 us -> 20.6 us
    ppermute x2, waiting for transfers between devices: 0.01 us -> 26.5 us  [from_above(): return lax.ppermute(slab, axis, [(i + 1, i) for i in range(count - 1)])]
    ppermute x2, waiting for transfers between devices: 28.1 us -> 4.09 us  [from_below(): return lax.ppermute(slab, axis, [(i, i + 1) for i in range(count - 1)])]
    ppermute x16, waiting for transfers between devices: 51.9 us -> 33.7 us  [from_partner(): lax.ppermute(shard, axis, [(i, i ^ 1 << apart) for i in range(lax.axis_si...]
    dot_general x68, matrix products: 39.3 us -> 46.9 us  [apply_map(): jnp.einsum('jk,...kc->...jc', weights, block, preferred_element_type=jnp....]
    unnamed x16 -> x31, local copies, waits for them, and re-layouts: 6.87 us -> 1.14 us
    optimization_barrier x0 -> x1, local copies, waits for them, and re-layouts: none -> 4.66 us  [pipelined(): late, _ = lax.optimization_barrier((late, ready[active[-1]]))]
    dynamic_slice x4, local copies, waits for them, and re-layouts: 0.11 us -> 3.49 us  [pipelined(): lax.dynamic_slice_in_dim(other, side, 1, axis=2)]
    ppermute x2, starting transfers between devices: 7.04 us -> 4.34 us  [from_above(): return lax.ppermute(slab, axis, [(i + 1, i) for i in range(count - 1)])]
  transfers between devices with their start and end apart: 21 -> 21, of which waited for: 10 -> 8; matrix products, arithmetic and copies ran while one was open for 28% -> 36% of each run, Pallas kernels for 0% -> 0%
where the time goes in v5:
time: 185 us; the launch traced here: 184 us
  waiting for transfers between devices  64.3 us (35%)
  matrix products  46.9 us (25%)
  starting transfers between devices  26.8 us (14%)
  local copies, waits for them, and re-layouts  20.6 us (11%)
  Pallas kernels  19.7 us (11%)
  other arithmetic  4.6 us (2%)
    dot_general x68, matrix products, apply_map(): jnp.einsum('jk,...kc->...jc', weights, block, preferred_element_type=jnp....  46.9 us
    ppermute x16, waiting for transfers between devices, from_partner(): lax.ppermute(shard, axis, [(i, i ^ 1 << apart) for i in range(lax.axis_si...  33.7 us
    ppermute x2, waiting for transfers between devices, from_above(): return lax.ppermute(slab, axis, [(i + 1, i) for i in range(count - 1)])  26.5 us
    ppermute x16, starting transfers between devices, from_partner(): lax.ppermute(shard, axis, [(i, i ^ 1 << apart) for i in range(lax.axis_si...  14.1 us
    pallas_call x1, Pallas kernels, couple(): pl.pallas_call(coupling_kernel, grid=(ly,), in_specs=specs, out_specs=pl....  11.4 us
    pallas_call x1, Pallas kernels, sample(): pl.pallas_call(sample_kernel, grid_spec=spec, out_shape=jax.ShapeDtypeStr...  8.25 us
    ppermute x2, starting transfers between devices, from_below(): return lax.ppermute(slab, axis, [(i, i + 1) for i in range(count - 1)])  7.66 us
    squeeze x1, local copies, waits for them, and re-layouts, pipelined(): cells[k] = mix(block, other, level_weights[level])  5.73 us
  transfers between devices with their start and end apart: 21, of which 8 were waited for; matrix products, arithmetic and copies ran while one was open for 36% of the time, Pallas kernels for 0%

profile of v5, /device:TPU:34, one launch (start us, length us, event | category | flops | bytes accessed | tf_op | source)
XLA Modules:
  0.0 183.8 jit_solution(11290642537323491964)
XLA Ops:
  0.0 1.7 fusion.211
  1.7 1.0 copy.47
  2.7 1.0 copy.46
  4.2 5.7 %slice_bitcast_fusion = (bf16[2,2,512,512]{3,2,1,0:T(8,128)(2,1)}, bf16[2,2,512,512]{3,2,1,0:T(8,128)(2,1)}, bf16[2,2,512,512]{3,2,1,0:T(8,128)(2,1)}, bf16[2,2,512,512]{3,2,1,0:T(8,128)(2,1)S(1)}) fusion(bf16[4,2,2,512,512]{4,3,2,1,0:T(8,128)(2,1)} %param.7), kind=kLoop, calls=%fused_computation.4 | loop fusion | bytes 16777216 | tf_op jit(solution)/shard_map/squeeze | solution.py:123
  9.9 1.8 fusion.65
  11.8 1.5 fusion.67
  13.4 1.5 fusion.31
  15.0 1.6 fusion.64
  21.7 9.3 %collective-permute-done.4 = bf16[2,1,2,512,128]{3,4,2,0,1:T(8,128)(2,1)S(1)} collective-permute-done((bf16[2,1,2,512,128]{3,4,2,0,1:T(8,128)(2,1)S(1)}, bf16[2,1,2,512,128]{3,4,2,0,1:T(8,128)(2,1)S(1)}, u32[]{:S(2)}, u32[]{:S(2)}) %collective-permute-start.4) | collective-permute-done | bytes 524320 | tf_op jit(solution)/shard_map/ppermute | solution.py:24
  37.0 8.9 %collective-permute-done.5 = bf16[2,1,2,512,128]{3,4,2,0,1:T(8,128)(2,1)S(1)} collective-permute-done((bf16[2,1,2,512,128]{3,4,2,0,1:T(8,128)(2,1)S(1)}, bf16[2,1,2,512,128]{3,4,2,0,1:T(8,128)(2,1)S(1)}, u32[]{:S(2)}, u32[]{:S(2)}) %collective-permute-start.5) | collective-permute-done | bytes 524320 | tf_op jit(solution)/shard_map/ppermute | solution.py:24
  46.9 0.8 collective-permute-start.6
  49.8 1.6 collective-permute-start.12
  51.4 1.5 collective-permute-start.9
  55.4 4.2 %collective-permute-done.6 = bf16[2,1,2,512,128]{3,4,2,0,1:T(8,128)(2,1)S(1)} collective-permute-done((bf16[2,1,2,512,128]{3,4,2,0,1:T(8,128)(2,1)S(1)}, bf16[2,1,2,512,128]{3,4,2,0,1:T(8,128)(2,1)S(1)}, u32[]{:S(2)}, u32[]{:S(2)}) %collective-permute-start.6) | collective-permute-done | bytes 524320 | tf_op jit(solution)/shard_map/ppermute | solution.py:24
  61.1 0.9 collective-permute-start.7
  64.4 0.7 constant_dynamic-slice_fusion.5
  65.1 1.0 collective-permute-start.13
  66.1 1.5 collective-permute-start.10
  69.2 1.3 fusion.52
  70.5 2.4 %collective-permute-start.19 = (bf16[2,1,2,512,128]{3,4,2,0,1:T(8,128)(2,1)}, bf16[2,1,2,512,128]{3,4,2,0,1:T(8,128)(2,1)}, u32[]{:S(2)}, u32[]{:S(2)}) collective-permute-start(bf16[2,1,2,512,128]{3,4,2,0,1:T(8,128)(2,1)} %fusion.52), channel_id=1, source_target_pairs={{8,0},{16,8},{24,16},{9,1},{17,9},{25,17},{10,2},{18,10},{26,18},{... | collective-permute-start | bytes 1572872 | tf_op jit(solution)/shard_map/ppermute | solution.py:139
  74.5 5.4 %collective-permute-done.10 = bf16[2,1,2,512,128]{3,4,2,0,1:T(8,128)(2,1)S(1)} collective-permute-done((bf16[2,1,2,512,128]{3,4,2,0,1:T(8,128)(2,1)S(1)}, bf16[2,1,2,512,128]{3,4,2,0,1:T(8,128)(2,1)S(1)}, u32[]{:S(2)}, u32[]{:S(2)}) %collective-permute-start.10) | collective-permute-done | bytes 524320 | tf_op jit(solution)/shard_map/ppermute | solution.py:24
  81.0 1.1 collective-permute-start.14
  83.9 2.8 %collective-permute-start.11 = (bf16[2,1,2,512,128]{3,4,2,0,1:T(8,128)(2,1)S(1)}, bf16[2,1,2,512,128]{3,4,2,0,1:T(8,128)(2,1)S(1)}, u32[]{:S(2)}, u32[]{:S(2)}) collective-permute-start(bf16[2,1,2,512,128]{3,4,2,0,1:T(8,128)(2,1)S(1)} %fusion.57), channel_id=1, source_target_pairs={{0,8},{8,0},{16,24},{24,16},{1,9},{9,1},{17,25},{25,17},{2,10},{10... | collective-permute-start | bytes 1572872 | tf_op jit(solution)/shard_map/ppermute | solution.py:24
  87.6 1.5 fusion.77
  89.1 1.4 fusion.79
  90.5 0.8 constant_dynamic-slice_fusion.6
  91.8 1.3 fusion.51
  93.1 5.6 %collective-permute-done.11 = bf16[2,1,2,512,128]{3,4,2,0,1:T(8,128)(2,1)S(1)} collective-permute-done((bf16[2,1,2,512,128]{3,4,2,0,1:T(8,128)(2,1)S(1)}, bf16[2,1,2,512,128]{3,4,2,0,1:T(8,128)(2,1)S(1)}, u32[]{:S(2)}, u32[]{:S(2)}) %collective-permute-start.11) | collective-permute-done | bytes 524320 | tf_op jit(solution)/shard_map/ppermute | solution.py:24
  101.2 4.7 %copy.11 = bf16[6,512,512]{1,2,0:T(8,128)(2,1)} copy(bf16[6,512,512]{2,1,0:T(8,128)(2,1)} %param.8) | data formatting | bytes 6291456 | tf_op jit(solution)/shard_map/optimization_barrier | solution.py:117
  106.8 1.0 constant_dynamic-slice_fusion.4
  107.8 1.6 fusion.3
  109.6 1.5 fusion.50
  111.1 1.5 fusion.1
  112.7 1.0 constant_dynamic-slice_fusion.2
  113.8 1.5 fusion.49
  115.3 5.1 %collective-permute-start.18 = (bf16[2,1,2,512,128]{3,4,2,0,1:T(8,128)(2,1)S(1)}, bf16[2,1,2,512,128]{3,4,2,0,1:T(8,128)(2,1)S(1)}, u32[]{:S(2)}, u32[]{:S(2)}) collective-permute-start(bf16[2,1,2,512,128]{3,4,2,0,1:T(8,128)(2,1)S(1)} %fusion.49), channel_id=1, source_target_pairs={{0,8},{8,16},{16,24},{1,9},{9,17},{17,25},{2,10},{10,18},{18,26},{... | collective-permute-start | bytes 1572872 | tf_op jit(solution)/shard_map/ppermute | solution.py:134
  120.4 2.7 %pad_maximum_fusion = (bf16[2,4,2,512,128]{3,4,2,0,1:T(8,128)(2,1)S(1)}, bf16[4,2,2,128,512]{4,3,2,1,0:T(8,128)(2,1)}) fusion(bf16[2,1,2,512,128]{3,4,2,0,1:T(8,128)(2,1)S(1)} %fusion.49, bf16[2,1,2,512,128]{3,4,2,0,1:T(8,128)(2,1)S(1)} %fusion.50, bf16[2,1,2,512,128]{3,4,2,0,1:T(8,128)(2,1)S(1)} %copy-done.7, bf16[2,1,2,512,128]{3,4,2,0,1:T(8,128)(2,1)} %fusion.52), kind=kLoop, calls=%fused_computation | loop fusion | flops 3145728 | bytes 6291456 | tf_op jit(solution)/shard_map/concatenate | solution.py:206
  123.3 1.9 %collective-permute-start.17 = (bf16[1,4,2,512,128]{3,4,2,0,1:T(8,128)(2,1)S(1)}, bf16[1,4,2,512,128]{3,4,2,0,1:T(8,128)(2,1)S(1)}, u32[]{:S(2)}, u32[]{:S(2)}) collective-permute-start(bf16[1,4,2,512,128]{3,4,2,0,1:T(8,128)(2,1)S(1)} %get-tuple-element.51), channel_id=1, source_target_pairs={{32,0},{64,32},{96,64},{33,1},{65,33},{97,65},{34,2},{66,34},{98,6... | collective-permute-start | bytes 3145736 | tf_op jit(solution)/shard_map/ppermute | solution.py:139
  125.3 2.6 %collective-permute-start.16 = (bf16[1,4,2,512,128]{3,4,2,0,1:T(8,128)(2,1)S(1)}, bf16[1,4,2,512,128]{3,4,2,0,1:T(8,128)(2,1)}, u32[]{:S(2)}, u32[]{:S(2)}) collective-permute-start(bf16[1,4,2,512,128]{3,4,2,0,1:T(8,128)(2,1)S(1)} %get-tuple-element.52), channel_id=1, source_target_pairs={{0,32},{32,64},{64,96},{1,33},{33,65},{65,97},{2,34},{34,66},{66,9... | collective-permute-start | bytes 3145736 | tf_op jit(solution)/shard_map/ppermute | solution.py:134
  127.9 0.7 collective-permute-start.20
  128.6 0.7 fusion.92
  129.4 0.7 add_bitcast_fusion
  130.4 0.7 fusion.107
  131.1 2.4 %select_bitcast_fusion = (bf16[4,2,1,128,512]{4,3,2,1,0:T(8,128)(2,1)}, bf16[4,2,1,128,512]{4,3,2,1,0:T(8,128)(2,1)}) fusion(bf16[2,4,1,512,128]{3,4,2,0,1:T(8,128)(2,1)S(1)} %collective-permute-done.20, pred[]{:T(512)S(6)} %eq.6, f32[2,4,1,512,64]{3,4,2,0,1:T(8,128)S(1)} %get-tuple-element.50, f32[2,4,1,512,64]{3,4,2,0,1:T(8,128)S(1)} %get-tuple-element.49, ...), kind=kOutput, calls=%fused_computation.107 | convolution fusion | flops 541589504 | bytes 8912897 | tf_op jit(solution)/shard_map/jk,...kc->...jc/dot_general | solution.py:33
  133.5 26.5 %collective-permute-done.17 = bf16[1,4,2,512,128]{3,4,2,0,1:T(8,128)(2,1)S(1)} collective-permute-done((bf16[1,4,2,512,128]{3,4,2,0,1:T(8,128)(2,1)S(1)}, bf16[1,4,2,512,128]{3,4,2,0,1:T(8,128)(2,1)S(1)}, u32[]{:S(2)}, u32[]{:S(2)}) %collective-permute-start.17) | collective-permute-done | bytes 1048608 | tf_op jit(solution)/shard_map/ppermute | solution.py:139
  160.0 4.1 %collective-permute-done.16 = bf16[1,4,2,512,128]{3,4,2,0,1:T(8,128)(2,1)} collective-permute-done((bf16[1,4,2,512,128]{3,4,2,0,1:T(8,128)(2,1)S(1)}, bf16[1,4,2,512,128]{3,4,2,0,1:T(8,128)(2,1)}, u32[]{:S(2)}, u32[]{:S(2)}) %collective-permute-start.16) | collective-permute-done | bytes 1048608 | tf_op jit(solution)/shard_map/ppermute | solution.py:134
  164.1 11.4 %shard_map.64 = bf16[4,2,2,128,512]{4,3,2,1,0:T(8,128)(2,1)} custom-call(bf16[6,512,512]{2,1,0:T(8,128)(2,1)} %bitcast.576, bf16[4,2,2,128,512]{4,3,2,1,0:T(8,128)(2,1)} %get-tuple-element.54.prev_ref.cell_ref.next_ref, bf16[4,2,2,128,512]{4,3,2,1,0:T(8,128)(2,1)} %get-tuple-element.54.prev_ref.cell_ref.next_ref, ...), custom_call_target="tpu_custom_call" | custom-call | tf_op jit(solution)/shard_map/pallas_call | solution.py:191
  175.5 8.2 %shard_map.65 = bf16[8192,128]{1,0:T(8,128)(2,1)} custom-call(s32[64]{0:T(128)} %leaf_ref.1, s32[64]{0:T(128)} %count_ref.1, f32[3,8192]{1,0:T(4,128)} %pos_ref.1, bf16[16,128,512]{2,1,0:T(8,128)(2,1)} %bitcast.577), custom_call_target="tpu_custom_call" | custom-call | tf_op jit(solution)/shard_map/pallas_call | solution.py:93
  (129 shorter events, 32.4 us)
Async XLA Ops:
  2.7 10.6 %collective-permute-start = (bf16[2,1,2,512,128]{3,4,2,0,1:T(8,128)(2,1)}, bf16[2,1,2,512,128]{3,4,2,0,1:T(8,128)(2,1)}, u32[]{:S(2)}, u32[]{:S(2)}) collective-permute-start(bf16[2,1,2,512,128]{3,4,2,0,1:T(8,128)(2,1)} %copy.47), channel_id=1, source_target_pairs={{0,32},{32,0},{64,96},{96,64},{1,33},{33,1},{65,97},{97,65},{2,34}... | collective-permute-start | bytes 1572872 | tf_op jit(solution)/shard_map/ppermute | solution.py:24
  9.9 1.9 %copy-start.1 = (bf16[2,2,512,512]{3,2,1,0:T(8,128)(2,1)S(1)}, bf16[2,2,512,512]{3,2,1,0:T(8,128)(2,1)}, u32[]{:S(2)}) copy-start(bf16[2,2,512,512]{3,2,1,0:T(8,128)(2,1)} %get-tuple-element.45) | copy-start | bytes 6291460
  15.0 1.8 copy-start.4
  16.6 1.6 copy-start
  16.6 14.4 %collective-permute-start.4 = (bf16[2,1,2,512,128]{3,4,2,0,1:T(8,128)(2,1)S(1)}, bf16[2,1,2,512,128]{3,4,2,0,1:T(8,128)(2,1)S(1)}, u32[]{:S(2)}, u32[]{:S(2)}) collective-permute-start(bf16[2,1,2,512,128]{3,4,2,0,1:T(8,128)(2,1)S(1)} %fusion.64), channel_id=1, source_target_pairs={{0,64},{32,96},{64,0},{96,32},{1,65},{33,97},{65,1},{97,33},{2,66}... | collective-permute-start | bytes 1572872 | tf_op jit(solution)/shard_map/ppermute | solution.py:24
  16.8 2.4 %collective-permute-start.1 = (bf16[2,1,2,512,128]{3,4,2,0,1:T(8,128)(2,1)S(1)}, bf16[2,1,2,512,128]{3,4,2,0,1:T(8,128)(2,1)S(1)}, u32[]{:S(2)}, u32[]{:S(2)}) collective-permute-start(bf16[2,1,2,512,128]{3,4,2,0,1:T(8,128)(2,1)S(1)} %copy-done.4), channel_id=1, source_target_pairs={{0,32},{32,0},{64,96},{96,64},{1,33},{33,1},{65,97},{97,65},{2,34}... | collective-permute-start | bytes 1572872 | tf_op jit(solution)/shard_map/ppermute | solution.py:24
  20.2 14.6 %collective-permute-start.2 = (bf16[2,1,2,512,128]{3,4,2,0,1:T(8,128)(2,1)S(1)}, bf16[2,1,2,512,128]{3,4,2,0,1:T(8,128)(2,1)S(1)}, u32[]{:S(2)}, u32[]{:S(2)}) collective-permute-start(bf16[2,1,2,512,128]{3,4,2,0,1:T(8,128)(2,1)S(1)} %copy.45), channel_id=1, source_target_pairs={{0,32},{32,0},{64,96},{96,64},{1,33},{33,1},{65,97},{97,65},{2,34}... | collective-permute-start | bytes 1572872 | tf_op jit(solution)/shard_map/ppermute | solution.py:24
  32.1 16.6 %collective-permute-start.8 = (bf16[2,1,2,512,128]{3,4,2,0,1:T(8,128)(2,1)S(1)}, bf16[2,1,2,512,128]{3,4,2,0,1:T(8,128)(2,1)S(1)}, u32[]{:S(2)}, u32[]{:S(2)}) collective-permute-start(bf16[2,1,2,512,128]{3,4,2,0,1:T(8,128)(2,1)S(1)} %fusion.60), channel_id=1, source_target_pairs={{0,8},{8,0},{16,24},{24,16},{1,9},{9,1},{17,25},{25,17},{2,10},{10... | collective-permute-start | bytes 1572872 | tf_op jit(solution)/shard_map/ppermute | solution.py:24
  32.7 13.2 %collective-permute-start.5 = (bf16[2,1,2,512,128]{3,4,2,0,1:T(8,128)(2,1)S(1)}, bf16[2,1,2,512,128]{3,4,2,0,1:T(8,128)(2,1)S(1)}, u32[]{:S(2)}, u32[]{:S(2)}) collective-permute-start(bf16[2,1,2,512,128]{3,4,2,0,1:T(8,128)(2,1)S(1)} %fusion.63), channel_id=1, source_target_pairs={{0,64},{32,96},{64,0},{96,32},{1,65},{33,97},{65,1},{97,33},{2,66}... | collective-permute-start | bytes 1572872 | tf_op jit(solution)/shard_map/ppermute | solution.py:24
  35.9 18.9 %collective-permute-start.3 = (bf16[2,1,2,512,128]{3,4,2,0,1:T(8,128)(2,1)S(1)}, bf16[2,1,2,512,128]{3,4,2,0,1:T(8,128)(2,1)S(1)}, u32[]{:S(2)}, u32[]{:S(2)}) collective-permute-start(bf16[2,1,2,512,128]{3,4,2,0,1:T(8,128)(2,1)S(1)} %copy.44), channel_id=1, source_target_pairs={{0,32},{32,0},{64,96},{96,64},{1,33},{33,1},{65,97},{97,65},{2,34}... | collective-permute-start | bytes 1572872 | tf_op jit(solution)/shard_map/ppermute | solution.py:24
  46.9 12.6 %collective-permute-start.6 = (bf16[2,1,2,512,128]{3,4,2,0,1:T(8,128)(2,1)S(1)}, bf16[2,1,2,512,128]{3,4,2,0,1:T(8,128)(2,1)S(1)}, u32[]{:S(2)}, u32[]{:S(2)}) collective-permute-start(bf16[2,1,2,512,128]{3,4,2,0,1:T(8,128)(2,1)S(1)} %fusion.62), channel_id=1, source_target_pairs={{0,64},{32,96},{64,0},{96,32},{1,65},{33,97},{65,1},{97,33},{2,66}... | collective-permute-start | bytes 1572872 | tf_op jit(solution)/shard_map/ppermute | solution.py:24
  49.8 4.0 %copy-start.2 = (bf16[2,2,512,512]{3,2,1,0:T(8,128)(2,1)S(1)}, bf16[2,2,512,512]{3,2,1,0:T(8,128)(2,1)}, u32[]{:S(2)}) copy-start(bf16[2,2,512,512]{3,2,1,0:T(8,128)(2,1)} %get-tuple-element.43) | copy-start | bytes 6291460
  49.8 18.8 %collective-permute-start.12 = (bf16[2,1,2,512,128]{3,4,2,0,1:T(8,128)(2,1)S(1)}, bf16[2,1,2,512,128]{3,4,2,0,1:T(8,128)(2,1)S(1)}, u32[]{:S(2)}, u32[]{:S(2)}) collective-permute-start(bf16[2,1,2,512,128]{3,4,2,0,1:T(8,128)(2,1)S(1)} %fusion.56), channel_id=1, source_target_pairs={{0,1},{1,0},{2,3},{3,2},{4,5},{5,4},{6,7},{7,6},{8,9},{9,8},{10,11... | collective-permute-start | bytes 1572872 | tf_op jit(solution)/shard_map/ppermute | solution.py:24
  51.4 11.9 %collective-permute-start.9 = (bf16[2,1,2,512,128]{3,4,2,0,1:T(8,128)(2,1)S(1)}, bf16[2,1,2,512,128]{3,4,2,0,1:T(8,128)(2,1)S(1)}, u32[]{:S(2)}, u32[]{:S(2)}) collective-permute-start(bf16[2,1,2,512,128]{3,4,2,0,1:T(8,128)(2,1)S(1)} %fusion.59), channel_id=1, source_target_pairs={{0,8},{8,0},{16,24},{24,16},{1,9},{9,1},{17,25},{25,17},{2,10},{10... | collective-permute-start | bytes 1572872 | tf_op jit(solution)/shard_map/ppermute | solution.py:24
  61.1 21.7 %collective-permute-start.7 = (bf16[2,1,2,512,128]{3,4,2,0,1:T(8,128)(2,1)S(1)}, bf16[2,1,2,512,128]{3,4,2,0,1:T(8,128)(2,1)S(1)}, u32[]{:S(2)}, u32[]{:S(2)}) collective-permute-start(bf16[2,1,2,512,128]{3,4,2,0,1:T(8,128)(2,1)S(1)} %fusion.61), channel_id=1, source_target_pairs={{0,64},{32,96},{64,0},{96,32},{1,65},{33,97},{65,1},{97,33},{2,66}... | collective-permute-start | bytes 1572872 | tf_op jit(solution)/shard_map/ppermute | solution.py:24
  65.1 25.4 %collective-permute-start.13 = (bf16[2,1,2,512,128]{3,4,2,0,1:T(8,128)(2,1)S(1)}, bf16[2,1,2,512,128]{3,4,2,0,1:T(8,128)(2,1)S(1)}, u32[]{:S(2)}, u32[]{:S(2)}) collective-permute-start(bf16[2,1,2,512,128]{3,4,2,0,1:T(8,128)(2,1)S(1)} %fusion.55), channel_id=1, source_target_pairs={{0,1},{1,0},{2,3},{3,2},{4,5},{5,4},{6,7},{7,6},{8,9},{9,8},{10,11... | collective-permute-start | bytes 1572872 | tf_op jit(solution)/shard_map/ppermute | solution.py:24
  66.1 13.8 %collective-permute-start.10 = (bf16[2,1,2,512,128]{3,4,2,0,1:T(8,128)(2,1)S(1)}, bf16[2,1,2,512,128]{3,4,2,0,1:T(8,128)(2,1)S(1)}, u32[]{:S(2)}, u32[]{:S(2)}) collective-permute-start(bf16[2,1,2,512,128]{3,4,2,0,1:T(8,128)(2,1)S(1)} %fusion.58), channel_id=1, source_target_pairs={{0,8},{8,0},{16,24},{24,16},{1,9},{9,1},{17,25},{25,17},{2,10},{10... | collective-permute-start | bytes 1572872 | tf_op jit(solution)/shard_map/ppermute | solution.py:24
  70.5 63.1 %collective-permute-start.19 = (bf16[2,1,2,512,128]{3,4,2,0,1:T(8,128)(2,1)}, bf16[2,1,2,512,128]{3,4,2,0,1:T(8,128)(2,1)}, u32[]{:S(2)}, u32[]{:S(2)}) collective-permute-start(bf16[2,1,2,512,128]{3,4,2,0,1:T(8,128)(2,1)} %fusion.52), channel_id=1, source_target_pairs={{8,0},{16,8},{24,16},{9,1},{17,9},{25,17},{10,2},{18,10},{26,18},{... | collective-permute-start | bytes 1572872 | tf_op jit(solution)/shard_map/ppermute | solution.py:139
  81.0 25.8 %collective-permute-start.14 = (bf16[2,1,2,512,128]{3,4,2,0,1:T(8,128)(2,1)S(1)}, bf16[2,1,2,512,128]{3,4,2,0,1:T(8,128)(2,1)}, u32[]{:S(2)}, u32[]{:S(2)}) collective-permute-start(bf16[2,1,2,512,128]{3,4,2,0,1:T(8,128)(2,1)S(1)} %fusion.54), channel_id=1, source_target_pairs={{0,1},{1,0},{2,3},{3,2},{4,5},{5,4},{6,7},{7,6},{8,9},{9,8},{10,11... | collective-permute-start | bytes 1572872 | tf_op jit(solution)/shard_map/ppermute | solution.py:24
  83.9 14.9 %collective-permute-start.11 = (bf16[2,1,2,512,128]{3,4,2,0,1:T(8,128)(2,1)S(1)}, bf16[2,1,2,512,128]{3,4,2,0,1:T(8,128)(2,1)S(1)}, u32[]{:S(2)}, u32[]{:S(2)}) collective-permute-start(bf16[2,1,2,512,128]{3,4,2,0,1:T(8,128)(2,1)S(1)} %fusion.57), channel_id=1, source_target_pairs={{0,8},{8,0},{16,24},{24,16},{1,9},{9,1},{17,25},{25,17},{2,10},{10... | collective-permute-start | bytes 1572872 | tf_op jit(solution)/shard_map/ppermute | solution.py:24
  100.5 5.4 %copy-start.3 = (bf16[2,2,512,512]{3,2,1,0:T(8,128)(2,1)S(1)}, bf16[2,2,512,512]{3,2,1,0:T(8,128)(2,1)}, u32[]{:S(2)}) copy-start(bf16[2,2,512,512]{3,2,1,0:T(8,128)(2,1)} %get-tuple-element.43) | copy-start | bytes 6291460
  100.5 10.6 %collective-permute-start.15 = (bf16[2,1,2,512,128]{3,4,2,0,1:T(8,128)(2,1)S(1)}, bf16[2,1,2,512,128]{3,4,2,0,1:T(8,128)(2,1)}, u32[]{:S(2)}, u32[]{:S(2)}) collective-permute-start(bf16[2,1,2,512,128]{3,4,2,0,1:T(8,128)(2,1)S(1)} %fusion.53), channel_id=1, source_target_pairs={{0,1},{1,0},{2,3},{3,2},{4,5},{5,4},{6,7},{7,6},{8,9},{9,8},{10,11... | collective-permute-start | bytes 1572872 | tf_op jit(solution)/shard_map/ppermute | solution.py:24
  105.9 1.9 %copy-start.6 = (f32[2,2,128,512]{3,2,1,0:T(8,128)S(1)}, f32[2,2,128,512]{3,2,1,0:T(8,128)}, u32[]{:S(2)}) copy-start(f32[2,2,128,512]{3,2,1,0:T(8,128)} %fusion.77) | copy-start | bytes 3145732
  107.8 1.7 copy-start.5
  112.7 7.6 %copy-start.7 = (bf16[2,1,2,512,128]{3,4,2,0,1:T(8,128)(2,1)S(1)}, bf16[2,1,2,512,128]{3,4,2,0,1:T(8,128)(2,1)}, u32[]{:S(2)}) copy-start(bf16[2,1,2,512,128]{3,4,2,0,1:T(8,128)(2,1)} %fusion.51) | copy-start | bytes 1572868
  115.3 18.2 %collective-permute-start.18 = (bf16[2,1,2,512,128]{3,4,2,0,1:T(8,128)(2,1)S(1)}, bf16[2,1,2,512,128]{3,4,2,0,1:T(8,128)(2,1)S(1)}, u32[]{:S(2)}, u32[]{:S(2)}) collective-permute-start(bf16[2,1,2,512,128]{3,4,2,0,1:T(8,128)(2,1)S(1)} %fusion.49), channel_id=1, source_target_pairs={{0,8},{8,16},{16,24},{1,9},{9,17},{17,25},{2,10},{10,18},{18,26},{... | collective-permute-start | bytes 1572872 | tf_op jit(solution)/shard_map/ppermute | solution.py:134
  123.1 5.5 %copy-start.11 = (bf16[2,1,1,512,128]{3,4,2,0,1:T(8,128)(2,1)S(1)}, bf16[2,1,1,512,128]{3,4,2,0,1:T(8,128)(2,1)}, u32[]{:S(2)}) copy-start(bf16[2,1,1,512,128]{3,4,2,0,1:T(8,128)(2,1)} %constant_dynamic-slice_fusion.8) | copy-start | bytes 786436
  123.2 5.5 %copy-start.13 = (bf16[2,1,1,512,128]{3,4,2,0,1:T(8,128)(2,1)S(1)}, bf16[2,1,1,512,128]{3,4,2,0,1:T(8,128)(2,1)}, u32[]{:S(2)}) copy-start(bf16[2,1,1,512,128]{3,4,2,0,1:T(8,128)(2,1)} %constant_dynamic-slice_fusion.6) | copy-start | bytes 786436
  123.3 36.7 %collective-permute-start.17 = (bf16[1,4,2,512,128]{3,4,2,0,1:T(8,128)(2,1)S(1)}, bf16[1,4,2,512,128]{3,4,2,0,1:T(8,128)(2,1)S(1)}, u32[]{:S(2)}, u32[]{:S(2)}) collective-permute-start(bf16[1,4,2,512,128]{3,4,2,0,1:T(8,128)(2,1)S(1)} %get-tuple-element.51), channel_id=1, source_target_pairs={{32,0},{64,32},{96,64},{33,1},{65,33},{97,65},{34,2},{66,34},{98,6... | collective-permute-start | bytes 3145736 | tf_op jit(solution)/shard_map/ppermute | solution.py:139
  125.2 4.1 %copy-start.10 = (bf16[2,1,1,512,128]{3,4,2,0,1:T(8,128)(2,1)S(1)}, bf16[2,1,1,512,128]{3,4,2,0,1:T(8,128)(2,1)}, u32[]{:S(2)}) copy-start(bf16[2,1,1,512,128]{3,4,2,0,1:T(8,128)(2,1)} %constant_dynamic-slice_fusion.5) | copy-start | bytes 786436
  125.2 4.1 %copy-start.12 = (bf16[2,1,1,512,128]{3,4,2,0,1:T(8,128)(2,1)S(1)}, bf16[2,1,1,512,128]{3,4,2,0,1:T(8,128)(2,1)}, u32[]{:S(2)}) copy-start(bf16[2,1,1,512,128]{3,4,2,0,1:T(8,128)(2,1)} %constant_dynamic-slice_fusion.3) | copy-start | bytes 786436
  125.3 4.1 %copy-start.14 = (bf16[2,1,1,512,128]{3,4,2,0,1:T(8,128)(2,1)S(1)}, bf16[2,1,1,512,128]{3,4,2,0,1:T(8,128)(2,1)}, u32[]{:S(2)}) copy-start(bf16[2,1,1,512,128]{3,4,2,0,1:T(8,128)(2,1)} %constant_dynamic-slice_fusion.1) | copy-start | bytes 786436
  125.3 38.8 %collective-permute-start.16 = (bf16[1,4,2,512,128]{3,4,2,0,1:T(8,128)(2,1)S(1)}, bf16[1,4,2,512,128]{3,4,2,0,1:T(8,128)(2,1)}, u32[]{:S(2)}, u32[]{:S(2)}) collective-permute-start(bf16[1,4,2,512,128]{3,4,2,0,1:T(8,128)(2,1)S(1)} %get-tuple-element.52), channel_id=1, source_target_pairs={{0,32},{32,64},{64,96},{1,33},{33,65},{65,97},{2,34},{34,66},{66,9... | collective-permute-start | bytes 3145736 | tf_op jit(solution)/shard_map/ppermute | solution.py:134
  127.9 3.3 %collective-permute-start.20 = (bf16[2,4,1,512,128]{3,4,2,0,1:T(8,128)(2,1)S(1)}, bf16[2,4,1,512,128]{3,4,2,0,1:T(8,128)(2,1)S(1)}, u32[]{:S(2)}, u32[]{:S(2)}) collective-permute-start(bf16[2,4,1,512,128]{3,4,2,0,1:T(8,128)(2,1)S(1)} %constant_dynamic-slice_fusion), channel_id=1, source_target_pairs={{2,1},{4,3},{6,5},{1,2},{3,4},{5,6},{10,9},{12,11},{14,13},{9,10},... | collective-permute-start | bytes 3145736 | tf_op jit(solution)/shard_map/ppermute | solution.py:146
  133.5 30.6 %copy-start.9 = (bf16[2,1,2,512,128]{3,4,2,0,1:T(8,128)(2,1)}, bf16[2,1,2,512,128]{3,4,2,0,1:T(8,128)(2,1)S(1)}, u32[]{:S(2)}) copy-start(bf16[2,1,2,512,128]{3,4,2,0,1:T(8,128)(2,1)S(1)} %collective-permute-done.18) | copy-start | bytes 1572868
  160.0 4.1 %copy-start.8 = (bf16[1,4,2,512,128]{3,4,2,0,1:T(8,128)(2,1)}, bf16[1,4,2,512,128]{3,4,2,0,1:T(8,128)(2,1)S(1)}, u32[]{:S(2)}) copy-start(bf16[1,4,2,512,128]{3,4,2,0,1:T(8,128)(2,1)S(1)} %collective-permute-done.17) | copy-start | bytes 3145732

commit v6 on v2

--- a/solution.py
+++ b/solution.py
@@ -143,9 +143,12 @@
 def local(coefficients, level_weights, coupling, positions, block_leaf, block_count):
     chunks = coefficients.shape[1]
     cells = jnp.concatenate(pipelined(coefficients, level_weights, chunks), axis=1)
+    minus_z, plus_z = faces(cells, "gz", 2)
     minus_x, plus_x = faces(cells, "gx", 0)
-    minus_y, plus_y = faces(cells, "gy", 1)
-    minus_z, plus_z = faces(cells, "gz", 2)
+    size = cells.shape[1]
+    below_y = from_below(cells[:, size - 1:], "gy")
+    minus_y = jnp.concatenate([below_y, cells[:, :size - 1]], axis=1)
+    plus_y = jnp.concatenate([cells[:, 1:], from_above(cells[:, :1], "gy")], axis=1)
     neighbours = (minus_x, plus_x, minus_y, plus_y, minus_z, plus_z)
     total = cells.astype(jnp.float32)
     for index in range(6):
@@ -163,6 +166,5 @@
         P(("gx", "gy", "gz")),
         P(("gx", "gy", "gz")),
     )
-    return jax.shard_map(
-        local, mesh=mesh, in_specs=placed, out_specs=P(("gx", "gy", "gz"), None), check_vma=False
-    )
+
+    return jax.shard_map(local, mesh=mesh, in_specs=placed, out_specs=P(("gx", "gy", "gz"), None), check_vma=False)

time: 176 us -> 176 us (level)
  no operation moved by 1% of the time
where the time goes in v6:
time: 176 us; the launch traced here: 175 us
  waiting for transfers between devices  79.7 us (45%)
  matrix products  45.6 us (26%)
  starting transfers between devices  29.6 us (17%)
  local copies, waits for them, and re-layouts  8.62 us (5%)
  Pallas kernels  8.26 us (5%)
  other arithmetic  1.96 us (1%)
    ppermute x16, waiting for transfers between devices, from_partner(): lax.ppermute(shard, axis, [(i, i ^ 1 << apart) for i in range(lax.axis_si...  47.5 us
    dot_general x70, matrix products, apply_map(): jnp.einsum('jk,...kc->...jc', weights, block, preferred_element_type=jnp....  45.6 us
    ppermute x3, waiting for transfers between devices, from_above(): return lax.ppermute(slab, axis, [(i + 1, i) for i in range(count - 1)])  25.7 us
    ppermute x16, starting transfers between devices, from_partner(): lax.ppermute(shard, axis, [(i, i ^ 1 << apart) for i in range(lax.axis_si...  13.8 us
    ppermute x3, starting transfers between devices, from_below(): return lax.ppermute(slab, axis, [(i, i + 1) for i in range(count - 1)])  9.89 us
    pallas_call x1, Pallas kernels, sample(): pl.pallas_call(sample_kernel, grid_spec=spec, out_shape=jax.ShapeDtypeStr...  8.26 us
    ppermute x3, waiting for transfers between devices, from_below(): return lax.ppermute(slab, axis, [(i, i + 1) for i in range(count - 1)])  6.49 us
    ppermute x3, starting transfers between devices, from_above(): return lax.ppermute(slab, axis, [(i + 1, i) for i in range(count - 1)])  5.92 us
  transfers between devices with their start and end apart: 22, of which 10 were waited for; matrix products, arithmetic and copies ran while one was open for 26% of the time, Pallas kernels for 0%

profile of v6, /device:TPU:34, one launch (start us, length us, event | category | flops | bytes accessed | tf_op | source)
XLA Modules:
  0.0 174.6 jit_solution(10686473763726255930)
XLA Ops:
  0.0 1.7 fusion.214
  1.7 1.0 copy.57
  2.9 1.0 copy.58
  4.2 4.0 %slice_bitcast_fusion = (bf16[2,2,512,512]{3,2,1,0:T(8,128)(2,1)S(1)}, bf16[2,2,512,512]{3,2,1,0:T(8,128)(2,1)S(1)}, bf16[2,2,512,512]{3,2,1,0:T(8,128)(2,1)S(1)}, bf16[2,2,512,512]{3,2,1,0:T(8,128)(2,1)S(1)}) fusion(bf16[4,2,2,512,512]{4,3,2,1,0:T(8,128)(2,1)} %param.7), kind=kLoop, calls=%fused_computation.39 | loop fusion | bytes 16777216 | tf_op jit(solution)/shard_map/squeeze | solution.py:120
  8.2 0.5 fusion.96
  8.7 0.5 fusion.98
  9.2 1.5 fusion.62
  10.9 1.6 fusion.95
  12.6 0.5 collective-permute-start.4
  15.6 0.5 fusion.91
  17.1 9.7 %collective-permute-done.1 = bf16[2,1,2,512,128]{3,4,2,0,1:T(8,128)(2,1)S(1)} collective-permute-done((bf16[2,1,2,512,128]{3,4,2,0,1:T(8,128)(2,1)S(1)}, bf16[2,1,2,512,128]{3,4,2,0,1:T(8,128)(2,1)S(1)}, u32[]{:S(2)}, u32[]{:S(2)}) %collective-permute-start.1) | collective-permute-done | bytes 524320 | tf_op jit(solution)/shard_map/ppermute | solution.py:24
  27.9 0.6 collective-permute-start.2
  32.8 8.9 %collective-permute-done.5 = bf16[2,1,2,512,128]{3,4,2,0,1:T(8,128)(2,1)S(1)} collective-permute-done((bf16[2,1,2,512,128]{3,4,2,0,1:T(8,128)(2,1)S(1)}, bf16[2,1,2,512,128]{3,4,2,0,1:T(8,128)(2,1)S(1)}, u32[]{:S(2)}, u32[]{:S(2)}) %collective-permute-start.5) | collective-permute-done | bytes 524320 | tf_op jit(solution)/shard_map/ppermute | solution.py:24
  42.3 0.5 fusion.90
  42.8 0.8 collective-permute-start.9
  45.7 1.5 collective-permute-start.3
  47.2 1.5 collective-permute-start.6
  51.2 4.2 %collective-permute-done.9 = bf16[2,1,2,512,128]{3,4,2,0,1:T(8,128)(2,1)S(1)} collective-permute-done((bf16[2,1,2,512,128]{3,4,2,0,1:T(8,128)(2,1)S(1)}, bf16[2,1,2,512,128]{3,4,2,0,1:T(8,128)(2,1)S(1)}, u32[]{:S(2)}, u32[]{:S(2)}) %collective-permute-start.9) | collective-permute-done | bytes 524320 | tf_op jit(solution)/shard_map/ppermute | solution.py:24
  56.0 0.5 fusion.83
  56.5 0.5 fusion.86
  57.0 0.9 collective-permute-start.13
  59.7 0.5 fusion.89
  60.2 1.1 collective-permute-start.7
  61.4 1.5 collective-permute-start.10
  65.8 2.4 %collective-permute-start.19 = (bf16[2,1,2,512,128]{3,4,2,0,1:T(8,128)(2,1)S(1)}, bf16[2,1,2,512,128]{3,4,2,0,1:T(8,128)(2,1)S(1)}, u32[]{:S(2)}, u32[]{:S(2)}) collective-permute-start(bf16[2,1,2,512,128]{3,4,2,0,1:T(8,128)(2,1)S(1)} %fusion.92), channel_id=1, source_target_pairs={{8,0},{16,8},{24,16},{9,1},{17,9},{25,17},{10,2},{18,10},{26,18},{... | collective-permute-start | bytes 1572872 | tf_op jit(solution)/shard_map/ppermute | solution.py:131
  69.1 6.0 %collective-permute-done.10 = bf16[2,1,2,512,128]{3,4,2,0,1:T(8,128)(2,1)S(1)} collective-permute-done((bf16[2,1,2,512,128]{3,4,2,0,1:T(8,128)(2,1)S(1)}, bf16[2,1,2,512,128]{3,4,2,0,1:T(8,128)(2,1)S(1)}, u32[]{:S(2)}, u32[]{:S(2)}) %collective-permute-start.10) | collective-permute-done | bytes 524320 | tf_op jit(solution)/shard_map/ppermute | solution.py:24
  75.8 0.5 fusion.85
  76.2 1.1 collective-permute-start.11
  77.3 0.5 fusion.82
  77.8 2.8 %collective-permute-start.14 = (bf16[2,1,2,512,128]{3,4,2,0,1:T(8,128)(2,1)S(1)}, bf16[2,1,2,512,128]{3,4,2,0,1:T(8,128)(2,1)S(1)}, u32[]{:S(2)}, u32[]{:S(2)}) collective-permute-start(bf16[2,1,2,512,128]{3,4,2,0,1:T(8,128)(2,1)S(1)} %fusion.82), channel_id=1, source_target_pairs={{0,8},{8,0},{16,24},{24,16},{1,9},{9,1},{17,25},{25,17},{2,10},{10... | collective-permute-start | bytes 1572872 | tf_op jit(solution)/shard_map/ppermute | solution.py:24
  83.0 0.5 fusion.88
  83.5 10.4 %collective-permute-done.14 = bf16[2,1,2,512,128]{3,4,2,0,1:T(8,128)(2,1)S(1)} collective-permute-done((bf16[2,1,2,512,128]{3,4,2,0,1:T(8,128)(2,1)S(1)}, bf16[2,1,2,512,128]{3,4,2,0,1:T(8,128)(2,1)S(1)}, u32[]{:S(2)}, u32[]{:S(2)}) %collective-permute-start.14) | collective-permute-done | bytes 524320 | tf_op jit(solution)/shard_map/ppermute | solution.py:24
  95.0 0.8 collective-permute-start.15
  97.8 7.5 %collective-permute-done.15 = bf16[2,1,2,512,128]{3,4,2,0,1:T(8,128)(2,1)S(1)} collective-permute-done((bf16[2,1,2,512,128]{3,4,2,0,1:T(8,128)(2,1)S(1)}, bf16[2,1,2,512,128]{3,4,2,0,1:T(8,128)(2,1)S(1)}, u32[]{:S(2)}, u32[]{:S(2)}) %collective-permute-start.15) | collective-permute-done | bytes 524320 | tf_op jit(solution)/shard_map/ppermute | solution.py:24
  106.4 5.0 %collective-permute-start.18 = (bf16[2,1,2,512,128]{3,4,2,0,1:T(8,128)(2,1)S(1)}, bf16[2,1,2,512,128]{3,4,2,0,1:T(8,128)(2,1)S(1)}, u32[]{:S(2)}, u32[]{:S(2)}) collective-permute-start(bf16[2,1,2,512,128]{3,4,2,0,1:T(8,128)(2,1)S(1)} %fusion.80), channel_id=1, source_target_pairs={{0,8},{8,16},{16,24},{1,9},{9,17},{17,25},{2,10},{10,18},{18,26},{... | collective-permute-start | bytes 1572872 | tf_op jit(solution)/shard_map/ppermute | solution.py:126
  111.9 2.2 %collective-permute-start.17 = (bf16[1,4,2,512,128]{3,4,2,0,1:T(8,128)(2,1)S(1)}, bf16[1,4,2,512,128]{3,4,2,0,1:T(8,128)(2,1)S(1)}, u32[]{:S(2)}, u32[]{:S(2)}) collective-permute-start(bf16[1,4,2,512,128]{3,4,2,0,1:T(8,128)(2,1)S(1)} %get-tuple-element.28), channel_id=1, source_target_pairs={{32,0},{64,32},{96,64},{33,1},{65,33},{97,65},{34,2},{66,34},{98,6... | collective-permute-start | bytes 3145736 | tf_op jit(solution)/shard_map/ppermute | solution.py:131
  114.4 2.4 %collective-permute-start.20 = (bf16[2,4,1,512,128]{3,4,2,0,1:T(8,128)(2,1)S(1)}, bf16[2,4,1,512,128]{3,4,2,0,1:T(8,128)(2,1)S(1)}, u32[]{:S(2)}, u32[]{:S(2)}) collective-permute-start(bf16[2,4,1,512,128]{3,4,2,0,1:T(8,128)(2,1)S(1)} %get-tuple-element.29), channel_id=1, source_target_pairs={{0,1},{1,2},{2,3},{3,4},{4,5},{5,6},{6,7},{8,9},{9,10},{10,11},{11... | collective-permute-start | bytes 3145736 | tf_op jit(solution)/shard_map/ppermute | solution.py:126
  116.8 1.3 collective-permute-start.21
  118.1 2.4 %collective-permute-start.16 = (bf16[1,4,2,512,128]{3,4,2,0,1:T(8,128)(2,1)S(1)}, bf16[1,4,2,512,128]{3,4,2,0,1:T(8,128)(2,1)S(1)}, u32[]{:S(2)}, u32[]{:S(2)}) collective-permute-start(bf16[1,4,2,512,128]{3,4,2,0,1:T(8,128)(2,1)S(1)} %get-tuple-element.27), channel_id=1, source_target_pairs={{0,32},{32,64},{64,96},{1,33},{33,65},{65,97},{2,34},{34,66},{66,9... | collective-permute-start | bytes 3145736 | tf_op jit(solution)/shard_map/ppermute | solution.py:126
  120.5 1.3 fusion.17
  121.9 1.3 fusion.9
  123.2 25.7 %collective-permute-done.17 = bf16[1,4,2,512,128]{3,4,2,0,1:T(8,128)(2,1)S(1)} collective-permute-done((bf16[1,4,2,512,128]{3,4,2,0,1:T(8,128)(2,1)S(1)}, bf16[1,4,2,512,128]{3,4,2,0,1:T(8,128)(2,1)S(1)}, u32[]{:S(2)}, u32[]{:S(2)}) %collective-permute-start.17) | collective-permute-done | bytes 1048608 | tf_op jit(solution)/shard_map/ppermute | solution.py:131
  148.9 1.3 fusion.5
  150.2 6.5 %collective-permute-done.16 = bf16[1,4,2,512,128]{3,4,2,0,1:T(8,128)(2,1)S(1)} collective-permute-done((bf16[1,4,2,512,128]{3,4,2,0,1:T(8,128)(2,1)S(1)}, bf16[1,4,2,512,128]{3,4,2,0,1:T(8,128)(2,1)S(1)}, u32[]{:S(2)}, u32[]{:S(2)}) %collective-permute-start.16) | collective-permute-done | bytes 1048608 | tf_op jit(solution)/shard_map/ppermute | solution.py:126
  156.7 1.3 fusion.1
  158.0 3.3 %fusion.25 = f32[2,4,2,128,512]{4,3,2,0,1:T(8,128)} fusion(bf16[2,4,1,512,128]{3,4,2,0,1:T(8,128)(2,1)S(1)} %get-tuple-element.30, bf16[2,4,1,512,128]{3,4,2,0,1:T(8,128)(2,1)S(1)} %collective-permute-done.20, bf16[6,512,512]{2,1,0:T(8,128)(2,1)S(1)} %copy-done.4), kind=kOutput, calls=%fused_computation.32 | convolution fusion | flops 1074790400 | bytes 6815744 | tf_op jit(solution)/shard_map/jk,...kc->...jc/dot_general | solution.py:33
  161.3 5.1 %fusion = bf16[2,4,2,512,128]{3,4,2,0,1:T(8,128)(2,1)} fusion(f32[2,4,2,128,512]{4,3,2,0,1:T(8,128)} %fusion.25, f32[2,4,2,128,512]{4,3,2,0,1:T(8,128)S(1)} %fusion.17, f32[2,4,2,128,512]{4,3,2,0,1:T(8,128)S(1)} %fusion.9, f32[2,4,2,128,512]{4,3,2,0,1:T(8,128)S(1)} %fusion.5, f32[2,4,2,128,512]{4,3,2,0,1:T(8,128)S(1)} %fusion.1, ...), kind=kOutput, calls=%fused_computation.1 | convolution fusion | flops 1086324736 | bytes 27787264 | tf_op jit(solution)/shard_map/jk,...kc->...jc/dot_general | solution.py:33
  166.3 8.3 %shard_map.64 = bf16[8192,128]{1,0:T(8,128)(2,1)} custom-call(s32[64]{0:T(128)} %leaf_ref.1, s32[64]{0:T(128)} %count_ref.1, f32[3,8192]{1,0:T(4,128)} %pos_ref.1, bf16[16,128,512]{2,1,0:T(8,128)(2,1)} %bitcast.591), custom_call_target="tpu_custom_call" | custom-call | tf_op jit(solution)/shard_map/pallas_call | solution.py:94
  (102 shorter events, 28.4 us)
Async XLA Ops:
  2.7 6.5 %collective-permute-start = (bf16[2,1,2,512,128]{3,4,2,0,1:T(8,128)(2,1)}, bf16[2,1,2,512,128]{3,4,2,0,1:T(8,128)(2,1)}, u32[]{:S(2)}, u32[]{:S(2)}) collective-permute-start(bf16[2,1,2,512,128]{3,4,2,0,1:T(8,128)(2,1)} %copy.57), channel_id=1, source_target_pairs={{0,32},{32,0},{64,96},{96,64},{1,33},{33,1},{65,97},{97,65},{2,34}... | collective-permute-start | bytes 1572872 | tf_op jit(solution)/shard_map/ppermute | solution.py:24
  4.2 4.1 %copy-start = (bf16[2,4,2,512,128]{4,3,2,1,0:T(8,128)(2,1)S(1)}, bf16[2,4,2,512,128]{4,3,2,1,0:T(8,128)(2,1)}, u32[]{:S(2)}) copy-start(bf16[2,4,2,512,128]{4,3,2,1,0:T(8,128)(2,1)} %param.6) | copy-start | bytes 6291460
  10.9 1.8 %copy-start.1 = (bf16[2,1,2,512,128]{3,4,2,0,1:T(8,128)(2,1)S(1)}, bf16[2,1,2,512,128]{3,4,2,0,1:T(8,128)(2,1)}, u32[]{:S(2)}) copy-start(bf16[2,1,2,512,128]{3,4,2,0,1:T(8,128)(2,1)} %copy.58) | copy-start | bytes 1572868
  12.4 14.4 %collective-permute-start.1 = (bf16[2,1,2,512,128]{3,4,2,0,1:T(8,128)(2,1)S(1)}, bf16[2,1,2,512,128]{3,4,2,0,1:T(8,128)(2,1)S(1)}, u32[]{:S(2)}, u32[]{:S(2)}) collective-permute-start(bf16[2,1,2,512,128]{3,4,2,0,1:T(8,128)(2,1)S(1)} %fusion.95), channel_id=1, source_target_pairs={{0,64},{32,96},{64,0},{96,32},{1,65},{33,97},{65,1},{97,33},{2,66}... | collective-permute-start | bytes 1572872 | tf_op jit(solution)/shard_map/ppermute | solution.py:24
  12.6 2.4 %collective-permute-start.4 = (bf16[2,1,2,512,128]{3,4,2,0,1:T(8,128)(2,1)S(1)}, bf16[2,1,2,512,128]{3,4,2,0,1:T(8,128)(2,1)S(1)}, u32[]{:S(2)}, u32[]{:S(2)}) collective-permute-start(bf16[2,1,2,512,128]{3,4,2,0,1:T(8,128)(2,1)S(1)} %copy-done.1), channel_id=1, source_target_pairs={{0,32},{32,0},{64,96},{96,64},{1,33},{33,1},{65,97},{97,65},{2,34}... | collective-permute-start | bytes 1572872 | tf_op jit(solution)/shard_map/ppermute | solution.py:24
  16.1 14.6 %collective-permute-start.8 = (bf16[2,1,2,512,128]{3,4,2,0,1:T(8,128)(2,1)S(1)}, bf16[2,1,2,512,128]{3,4,2,0,1:T(8,128)(2,1)S(1)}, u32[]{:S(2)}, u32[]{:S(2)}) collective-permute-start(bf16[2,1,2,512,128]{3,4,2,0,1:T(8,128)(2,1)S(1)} %copy.59), channel_id=1, source_target_pairs={{0,32},{32,0},{64,96},{96,64},{1,33},{33,1},{65,97},{97,65},{2,34}... | collective-permute-start | bytes 1572872 | tf_op jit(solution)/shard_map/ppermute | solution.py:24
  27.9 16.7 %collective-permute-start.2 = (bf16[2,1,2,512,128]{3,4,2,0,1:T(8,128)(2,1)S(1)}, bf16[2,1,2,512,128]{3,4,2,0,1:T(8,128)(2,1)S(1)}, u32[]{:S(2)}, u32[]{:S(2)}) collective-permute-start(bf16[2,1,2,512,128]{3,4,2,0,1:T(8,128)(2,1)S(1)} %fusion.94), channel_id=1, source_target_pairs={{0,8},{8,0},{16,24},{24,16},{1,9},{9,1},{17,25},{25,17},{2,10},{10... | collective-permute-start | bytes 1572872 | tf_op jit(solution)/shard_map/ppermute | solution.py:24
  28.5 13.2 %collective-permute-start.5 = (bf16[2,1,2,512,128]{3,4,2,0,1:T(8,128)(2,1)S(1)}, bf16[2,1,2,512,128]{3,4,2,0,1:T(8,128)(2,1)S(1)}, u32[]{:S(2)}, u32[]{:S(2)}) collective-permute-start(bf16[2,1,2,512,128]{3,4,2,0,1:T(8,128)(2,1)S(1)} %fusion.91), channel_id=1, source_target_pairs={{0,64},{32,96},{64,0},{96,32},{1,65},{33,97},{65,1},{97,33},{2,66}... | collective-permute-start | bytes 1572872 | tf_op jit(solution)/shard_map/ppermute | solution.py:24
  31.8 18.8 %collective-permute-start.12 = (bf16[2,1,2,512,128]{3,4,2,0,1:T(8,128)(2,1)S(1)}, bf16[2,1,2,512,128]{3,4,2,0,1:T(8,128)(2,1)S(1)}, u32[]{:S(2)}, u32[]{:S(2)}) collective-permute-start(bf16[2,1,2,512,128]{3,4,2,0,1:T(8,128)(2,1)S(1)} %copy.60), channel_id=1, source_target_pairs={{0,32},{32,0},{64,96},{96,64},{1,33},{33,1},{65,97},{97,65},{2,34}... | collective-permute-start | bytes 1572872 | tf_op jit(solution)/shard_map/ppermute | solution.py:24
  42.8 12.6 %collective-permute-start.9 = (bf16[2,1,2,512,128]{3,4,2,0,1:T(8,128)(2,1)S(1)}, bf16[2,1,2,512,128]{3,4,2,0,1:T(8,128)(2,1)S(1)}, u32[]{:S(2)}, u32[]{:S(2)}) collective-permute-start(bf16[2,1,2,512,128]{3,4,2,0,1:T(8,128)(2,1)S(1)} %fusion.87), channel_id=1, source_target_pairs={{0,64},{32,96},{64,0},{96,32},{1,65},{33,97},{65,1},{97,33},{2,66}... | collective-permute-start | bytes 1572872 | tf_op jit(solution)/shard_map/ppermute | solution.py:24
  45.7 18.1 %collective-permute-start.3 = (bf16[2,1,2,512,128]{3,4,2,0,1:T(8,128)(2,1)S(1)}, bf16[2,1,2,512,128]{3,4,2,0,1:T(8,128)(2,1)S(1)}, u32[]{:S(2)}, u32[]{:S(2)}) collective-permute-start(bf16[2,1,2,512,128]{3,4,2,0,1:T(8,128)(2,1)S(1)} %fusion.93), channel_id=1, source_target_pairs={{0,1},{1,0},{2,3},{3,2},{4,5},{5,4},{6,7},{7,6},{8,9},{9,8},{10,11... | collective-permute-start | bytes 1572872 | tf_op jit(solution)/shard_map/ppermute | solution.py:24
  47.2 12.0 %collective-permute-start.6 = (bf16[2,1,2,512,128]{3,4,2,0,1:T(8,128)(2,1)S(1)}, bf16[2,1,2,512,128]{3,4,2,0,1:T(8,128)(2,1)S(1)}, u32[]{:S(2)}, u32[]{:S(2)}) collective-permute-start(bf16[2,1,2,512,128]{3,4,2,0,1:T(8,128)(2,1)S(1)} %fusion.90), channel_id=1, source_target_pairs={{0,8},{8,0},{16,24},{24,16},{1,9},{9,1},{17,25},{25,17},{2,10},{10... | collective-permute-start | bytes 1572872 | tf_op jit(solution)/shard_map/ppermute | solution.py:24
  57.0 11.6 %collective-permute-start.13 = (bf16[2,1,2,512,128]{3,4,2,0,1:T(8,128)(2,1)S(1)}, bf16[2,1,2,512,128]{3,4,2,0,1:T(8,128)(2,1)S(1)}, u32[]{:S(2)}, u32[]{:S(2)}) collective-permute-start(bf16[2,1,2,512,128]{3,4,2,0,1:T(8,128)(2,1)S(1)} %fusion.83), channel_id=1, source_target_pairs={{0,64},{32,96},{64,0},{96,32},{1,65},{33,97},{65,1},{97,33},{2,66}... | collective-permute-start | bytes 1572872 | tf_op jit(solution)/shard_map/ppermute | solution.py:24
  60.2 22.2 %collective-permute-start.7 = (bf16[2,1,2,512,128]{3,4,2,0,1:T(8,128)(2,1)S(1)}, bf16[2,1,2,512,128]{3,4,2,0,1:T(8,128)(2,1)S(1)}, u32[]{:S(2)}, u32[]{:S(2)}) collective-permute-start(bf16[2,1,2,512,128]{3,4,2,0,1:T(8,128)(2,1)S(1)} %fusion.89), channel_id=1, source_target_pairs={{0,1},{1,0},{2,3},{3,2},{4,5},{5,4},{6,7},{7,6},{8,9},{9,8},{10,11... | collective-permute-start | bytes 1572872 | tf_op jit(solution)/shard_map/ppermute | solution.py:24
  61.4 13.8 %collective-permute-start.10 = (bf16[2,1,2,512,128]{3,4,2,0,1:T(8,128)(2,1)S(1)}, bf16[2,1,2,512,128]{3,4,2,0,1:T(8,128)(2,1)S(1)}, u32[]{:S(2)}, u32[]{:S(2)}) collective-permute-start(bf16[2,1,2,512,128]{3,4,2,0,1:T(8,128)(2,1)S(1)} %fusion.86), channel_id=1, source_target_pairs={{0,8},{8,0},{16,24},{24,16},{1,9},{9,1},{17,25},{25,17},{2,10},{10... | collective-permute-start | bytes 1572872 | tf_op jit(solution)/shard_map/ppermute | solution.py:24
  65.8 52.2 %collective-permute-start.19 = (bf16[2,1,2,512,128]{3,4,2,0,1:T(8,128)(2,1)S(1)}, bf16[2,1,2,512,128]{3,4,2,0,1:T(8,128)(2,1)S(1)}, u32[]{:S(2)}, u32[]{:S(2)}) collective-permute-start(bf16[2,1,2,512,128]{3,4,2,0,1:T(8,128)(2,1)S(1)} %fusion.92), channel_id=1, source_target_pairs={{8,0},{16,8},{24,16},{9,1},{17,9},{25,17},{10,2},{18,10},{26,18},{... | collective-permute-start | bytes 1572872 | tf_op jit(solution)/shard_map/ppermute | solution.py:131
  76.2 20.5 %collective-permute-start.11 = (bf16[2,1,2,512,128]{3,4,2,0,1:T(8,128)(2,1)S(1)}, bf16[2,1,2,512,128]{3,4,2,0,1:T(8,128)(2,1)S(1)}, u32[]{:S(2)}, u32[]{:S(2)}) collective-permute-start(bf16[2,1,2,512,128]{3,4,2,0,1:T(8,128)(2,1)S(1)} %fusion.85), channel_id=1, source_target_pairs={{0,1},{1,0},{2,3},{3,2},{4,5},{5,4},{6,7},{7,6},{8,9},{9,8},{10,11... | collective-permute-start | bytes 1572872 | tf_op jit(solution)/shard_map/ppermute | solution.py:24
  77.8 16.2 %collective-permute-start.14 = (bf16[2,1,2,512,128]{3,4,2,0,1:T(8,128)(2,1)S(1)}, bf16[2,1,2,512,128]{3,4,2,0,1:T(8,128)(2,1)S(1)}, u32[]{:S(2)}, u32[]{:S(2)}) collective-permute-start(bf16[2,1,2,512,128]{3,4,2,0,1:T(8,128)(2,1)S(1)} %fusion.82), channel_id=1, source_target_pairs={{0,8},{8,0},{16,24},{24,16},{1,9},{9,1},{17,25},{25,17},{2,10},{10... | collective-permute-start | bytes 1572872 | tf_op jit(solution)/shard_map/ppermute | solution.py:24
  95.0 10.3 %collective-permute-start.15 = (bf16[2,1,2,512,128]{3,4,2,0,1:T(8,128)(2,1)S(1)}, bf16[2,1,2,512,128]{3,4,2,0,1:T(8,128)(2,1)S(1)}, u32[]{:S(2)}, u32[]{:S(2)}) collective-permute-start(bf16[2,1,2,512,128]{3,4,2,0,1:T(8,128)(2,1)S(1)} %fusion.81), channel_id=1, source_target_pairs={{0,1},{1,0},{2,3},{3,2},{4,5},{5,4},{6,7},{7,6},{8,9},{9,8},{10,11... | collective-permute-start | bytes 1572872 | tf_op jit(solution)/shard_map/ppermute | solution.py:24
  106.4 15.5 %collective-permute-start.18 = (bf16[2,1,2,512,128]{3,4,2,0,1:T(8,128)(2,1)S(1)}, bf16[2,1,2,512,128]{3,4,2,0,1:T(8,128)(2,1)S(1)}, u32[]{:S(2)}, u32[]{:S(2)}) collective-permute-start(bf16[2,1,2,512,128]{3,4,2,0,1:T(8,128)(2,1)S(1)} %fusion.80), channel_id=1, source_target_pairs={{0,8},{8,16},{16,24},{1,9},{9,17},{17,25},{2,10},{10,18},{18,26},{... | collective-permute-start | bytes 1572872 | tf_op jit(solution)/shard_map/ppermute | solution.py:126
  111.9 8.6 %copy-start.4 = (bf16[6,512,512]{2,1,0:T(8,128)(2,1)S(1)}, bf16[6,512,512]{2,1,0:T(8,128)(2,1)}, u32[]{:S(2)}) copy-start(bf16[6,512,512]{2,1,0:T(8,128)(2,1)} %param.8) | copy-start | bytes 9437188
  111.9 37.0 %collective-permute-start.17 = (bf16[1,4,2,512,128]{3,4,2,0,1:T(8,128)(2,1)S(1)}, bf16[1,4,2,512,128]{3,4,2,0,1:T(8,128)(2,1)S(1)}, u32[]{:S(2)}, u32[]{:S(2)}) collective-permute-start(bf16[1,4,2,512,128]{3,4,2,0,1:T(8,128)(2,1)S(1)} %get-tuple-element.28), channel_id=1, source_target_pairs={{32,0},{64,32},{96,64},{33,1},{65,33},{97,65},{34,2},{66,34},{98,6... | collective-permute-start | bytes 3145736 | tf_op jit(solution)/shard_map/ppermute | solution.py:131
  114.3 7.5 %copy-start.2 = (bf16[2,4,1,512,128]{3,4,2,0,1:T(8,128)(2,1)}, bf16[2,4,1,512,128]{3,4,2,0,1:T(8,128)(2,1)S(1)}, u32[]{:S(2)}) copy-start(bf16[2,4,1,512,128]{3,4,2,0,1:T(8,128)(2,1)S(1)} %get-tuple-element.29) | copy-start | bytes 3145732
  114.4 43.6 %collective-permute-start.20 = (bf16[2,4,1,512,128]{3,4,2,0,1:T(8,128)(2,1)S(1)}, bf16[2,4,1,512,128]{3,4,2,0,1:T(8,128)(2,1)S(1)}, u32[]{:S(2)}, u32[]{:S(2)}) collective-permute-start(bf16[2,4,1,512,128]{3,4,2,0,1:T(8,128)(2,1)S(1)} %get-tuple-element.29), channel_id=1, source_target_pairs={{0,1},{1,2},{2,3},{3,4},{4,5},{5,6},{6,7},{8,9},{9,10},{10,11},{11... | collective-permute-start | bytes 3145736 | tf_op jit(solution)/shard_map/ppermute | solution.py:126
  116.8 44.5 %collective-permute-start.21 = (bf16[2,4,1,512,128]{3,4,2,0,1:T(8,128)(2,1)S(1)}, bf16[2,4,1,512,128]{3,4,2,0,1:T(8,128)(2,1)S(1)}, u32[]{:S(2)}, u32[]{:S(2)}) collective-permute-start(bf16[2,4,1,512,128]{3,4,2,0,1:T(8,128)(2,1)S(1)} %get-tuple-element.30), channel_id=1, source_target_pairs={{1,0},{2,1},{3,2},{4,3},{5,4},{6,5},{7,6},{9,8},{10,9},{11,10},{12... | collective-permute-start | bytes 3145736 | tf_op jit(solution)/shard_map/ppermute | solution.py:131
  118.1 38.6 %collective-permute-start.16 = (bf16[1,4,2,512,128]{3,4,2,0,1:T(8,128)(2,1)S(1)}, bf16[1,4,2,512,128]{3,4,2,0,1:T(8,128)(2,1)S(1)}, u32[]{:S(2)}, u32[]{:S(2)}) collective-permute-start(bf16[1,4,2,512,128]{3,4,2,0,1:T(8,128)(2,1)S(1)} %get-tuple-element.27), channel_id=1, source_target_pairs={{0,32},{32,64},{64,96},{1,33},{33,65},{65,97},{2,34},{34,66},{66,9... | collective-permute-start | bytes 3145736 | tf_op jit(solution)/shard_map/ppermute | solution.py:126
  158.0 3.3 %copy-start.3 = (bf16[2,4,1,512,128]{3,4,2,0,1:T(8,128)(2,1)S(1)}, bf16[2,4,1,512,128]{3,4,2,0,1:T(8,128)(2,1)}, u32[]{:S(2)}) copy-start(bf16[2,4,1,512,128]{3,4,2,0,1:T(8,128)(2,1)} %copy-done.2) | copy-start | bytes 3145732
